TPU v7x, 32 devices: a whole 2x2x4 slice. The times are simulated.
32 devices in a mesh: tile: 4 (over z), seq: 8 (over y, x, core).
Axes of the slice: x: 2, y: 2, z: 4, core: 2. Of those that a mesh axis runs over, the one named last changes fastest.
Arguments:
- embeddings: bfloat16 [32768, 1536], P(('tile', 'seq')), may hold values from -6 to 6
- slot: int32 [32768], P(('tile', 'seq')), may hold values from 0 to 32767, as said below
- lengths: int32 [4], P('tile'), may hold values from 1 to 8192, 20480 in all
- in_weight: bfloat16 [1536, 768], replicated, may hold values from -0.15625 to 0.15625
- norm_gain: float32 [768], replicated, may hold values from 0.1 to 1.9
- qkv_weight: bfloat16 [768, 2304], replicated, may hold values from -1 to 1
- out_weight: bfloat16 [768, 768], replicated, may hold values from -0.21875 to 0.21875
Outputs:
- encoded: bfloat16 [4, 8192, 768], P('tile', 'seq')
Inputs may be any that keep to these rules, and one draw needn't show every extreme that they name: `slot`: every value appears exactly once. With P = 32 and B = 1024 // P, the rows q * 1024 + k * B to q * 1024 + (k + 1) * B - 1 have slots between k * 1024 and (k + 1) * 1024 - 1, for every q and k.
All inputs are finite; a program needn't handle non-finite values. No bound on the sum of `lengths` on one device may be relied on, other than what follows from the above.
Results may differ from a plain program's by a relative error of at most 0.017.
The roundings to bfloat16 on the way count: a program that leaves them out, or rounds other values in their place, can miss the bound.
Values may be sent and summed in bfloat16 or wider, within the bound.
No kernel may reach another device: no remote copies, remote signals or barrier semaphores. Data moves between devices by JAX's collectives and lax.ppermute only.
A program may use at most 256 MiB of HBM per device.

v0:
```python
import jax
import jax.numpy as jnp
from jax import lax
from jax.sharding import PartitionSpec as P

HEAD_COUNT = 16
DILATION_RATE = 8


big_negative = -1e30
norm_epsilon = 1e-05


def normalize(features, gain):
    wide = features.astype(jnp.float32)
    average = jnp.mean(wide, axis=-1, keepdims=True)
    centered = wide - average
    spread = jnp.mean(centered * centered, axis=-1, keepdims=True)
    return (centered * lax.rsqrt(spread + norm_epsilon) * gain).astype(jnp.bfloat16)


def body(embeddings, slot, lengths, in_weight, norm_gain, qkv_weight, out_weight):
    seq_count = lax.axis_size("seq")
    device_count = lax.axis_size("tile") * seq_count
    sequence_rows = embeddings.shape[0]
    block_rows = sequence_rows // device_count
    model_width = in_weight.shape[1]
    my_index = lax.axis_index("tile") * seq_count + lax.axis_index("seq")
    parted_slot = slot.reshape(device_count, block_rows)
    arrived_raw, arrived_slot = (
        lax.all_to_all(
            embeddings.reshape(device_count, block_rows, embeddings.shape[1]),
            ("tile", "seq"),
            split_axis=0,
            concat_axis=0,
            tiled=True,
        ),
        lax.all_to_all(parted_slot, ("tile", "seq"), split_axis=0, concat_axis=0, tiled=True),
    )
    arrived = jnp.dot(
        arrived_raw.reshape(sequence_rows, embeddings.shape[1]),
        in_weight,
        preferred_element_type=jnp.float32,
    ).astype(jnp.bfloat16)
    local_slot = arrived_slot.reshape(sequence_rows) - my_index * sequence_rows
    features = jnp.zeros((sequence_rows, model_width), jnp.bfloat16).at[local_slot].set(arrived)
    slide_length = lengths[0]
    first_pos = lax.axis_index("seq") * sequence_rows
    positions = first_pos + jnp.arange(sequence_rows, dtype=jnp.int32)
    key_ok = positions < slide_length
    head_feature_size = model_width // HEAD_COUNT
    logit_scale = head_feature_size ** (-0.5)
    start_offsets = jnp.arange(HEAD_COUNT, dtype=jnp.int32) % DILATION_RATE
    head_index_list = jnp.arange(HEAD_COUNT, dtype=jnp.int32)
    dilated_mask = jnp.arange(DILATION_RATE, dtype=jnp.int32)[None, :] == start_offsets[:, None]
    dilated_row_index = sequence_rows // DILATION_RATE
    normed = normalize(features, norm_gain)
    projections = jnp.dot(normed, qkv_weight, preferred_element_type=jnp.float32).astype(
        jnp.bfloat16
    )
    query_matrix = projections[:, :model_width].reshape(
        sequence_rows, HEAD_COUNT, head_feature_size
    )
    key_matrix = projections[:, model_width : 2 * model_width].reshape(
        sequence_rows, HEAD_COUNT, head_feature_size
    )
    value_matrix = projections[:, 2 * model_width :].reshape(
        sequence_rows, HEAD_COUNT, head_feature_size
    )
    dilated_query_rows = query_matrix.reshape(
        dilated_row_index, DILATION_RATE, HEAD_COUNT, head_feature_size
    )[:, start_offsets, head_index_list, :]
    dilated_key_rows = key_matrix.reshape(
        dilated_row_index, DILATION_RATE, HEAD_COUNT, head_feature_size
    )[:, start_offsets, head_index_list, :]
    dilated_value_rows = value_matrix.reshape(
        dilated_row_index, DILATION_RATE, HEAD_COUNT, head_feature_size
    )[:, start_offsets, head_index_list, :]
    packed = jnp.stack(
        [
            dilated_key_rows.reshape(dilated_row_index, model_width),
            dilated_value_rows.reshape(dilated_row_index, model_width),
        ]
    )
    gathered = lax.all_gather(packed, "seq", axis=1, tiled=True)
    distant_count = gathered.shape[1]
    far_keys = gathered[0].reshape(distant_count, HEAD_COUNT, head_feature_size)
    far_values = gathered[1].reshape(distant_count, HEAD_COUNT, head_feature_size)
    distant_valid_mask = (
        jnp.arange(distant_count, dtype=jnp.int32)[:, None] * DILATION_RATE + start_offsets[None, :]
        < slide_length
    )
    grouped_heads = 4
    pieces = []
    for first_head in range(0, HEAD_COUNT, grouped_heads):
        chosen = slice(first_head, first_head + grouped_heads)
        group_mask = dilated_mask[chosen]
        nearby_scores = (
            jnp.einsum(
                "qhd,khd->hqk",
                query_matrix[:, chosen],
                key_matrix[:, chosen],
                preferred_element_type=jnp.float32,
            )
            * logit_scale
        )
        nearby_scores = jnp.where(key_ok[None, None, :], nearby_scores, big_negative)
        nearby_maximum = jnp.max(nearby_scores, axis=-1).reshape(
            grouped_heads, dilated_row_index, DILATION_RATE
        )
        local_sparse_max = jnp.max(
            jnp.where(group_mask[:, None, :], nearby_maximum, big_negative), axis=-1
        )
        distant_scores = (
            jnp.einsum(
                "sbz,ebz->bse",
                dilated_query_rows[:, chosen],
                far_keys[:, chosen],
                preferred_element_type=jnp.float32,
            )
            * logit_scale
        )
        distant_scores = jnp.where(
            distant_valid_mask[:, chosen].T[:, None, :], distant_scores, big_negative
        )
        joint = jnp.maximum(local_sparse_max, jnp.max(distant_scores, axis=-1))
        distant_weights = jnp.exp(distant_scores - joint[:, :, None])
        distant_total = jnp.sum(distant_weights, axis=-1)
        distant_accumulator = jnp.einsum(
            "aup,pae->uae",
            distant_weights.astype(jnp.bfloat16),
            far_values[:, chosen],
            preferred_element_type=jnp.float32,
        )
        row_max = jnp.where(group_mask[:, None, :], joint[:, :, None], nearby_maximum).reshape(
            grouped_heads, sequence_rows
        )
        local_weights = jnp.exp(nearby_scores - row_max[:, :, None])
        nearby_total = jnp.sum(local_weights, axis=-1)
        nearby_accumulator = jnp.einsum(
            "hqk,khd->qhd",
            local_weights.astype(jnp.bfloat16),
            value_matrix[:, chosen],
            preferred_element_type=jnp.float32,
        )
        softmax_totals = nearby_total.reshape(
            grouped_heads, dilated_row_index, DILATION_RATE
        ) + jnp.where(group_mask[:, None, :], distant_total[:, :, None], 0.0)
        softmax_totals = softmax_totals.transpose(1, 2, 0).reshape(sequence_rows, grouped_heads)
        summed_output = nearby_accumulator.reshape(
            dilated_row_index, DILATION_RATE, grouped_heads, head_feature_size
        ) + jnp.where(group_mask.T[None, :, :, None], distant_accumulator[:, None, :, :], 0.0)
        pieces.append(
            summed_output.reshape(sequence_rows, grouped_heads, head_feature_size)
            / softmax_totals[:, :, None]
        )
    attended = (
        jnp.concatenate(pieces, axis=1).reshape(sequence_rows, model_width).astype(jnp.bfloat16)
    )
    output = jnp.dot(attended, out_weight, preferred_element_type=jnp.float32) + features.astype(
        jnp.float32
    )
    output = jnp.where(key_ok[:, None], output, 0.0).astype(jnp.bfloat16)
    return output.reshape(1, sequence_rows, model_width)


def solution(mesh):
    return jax.shard_map(
        body,
        mesh=mesh,
        in_specs=(P(("tile", "seq"), None), P(("tile", "seq")), P("tile"), P(), P(), P(), P()),
        out_specs=P("tile", "seq", None),
        check_vma=False,
    )
```

profile of v0, /device:TPU:0, one launch (start us, length us, event | category | flops | bytes accessed | tf_op | source)
XLA Modules:
  0.0 323.5 jit_solution(13487590693442350272)
XLA Ops:
  7.5 14.4 %all_to_all.14 = s32[32,1,32]{2,1,0:T(1,128)} all-to-all(s32[32,1,32]{2,1,0:T(1,128)S(1)} %all_to_all.9), channel_id=1, replica_groups=mesh['tile'=4,'seq'=8] {'tile','seq'}, dimensions={0} | all-to-all | bytes 8192 | tf_op jit(solution)/shard_map/all_to_all | solution.py:38
  21.8 3.5 %all-to-all-start.1 = ((bf16[32,32,1536]{2,1,0:T(8,128)(2,1)}), bf16[32,32,1536]{2,1,0:T(8,128)(2,1)}, u32[]{:S(2)}, u32[]{:S(2)}) async-start(bf16[32,32,1536]{2,1,0:T(8,128)(2,1)} %bitcast.152), calls=%async_computation.1 | async-start | bytes 6291456 | tf_op jit(solution)/shard_map/all_to_all | solution.py:31
  27.6 69.2 %all-to-all-done.1 = bf16[32,32,1536]{2,1,0:T(8,128)(2,1)} async-done(((bf16[32,32,1536]{2,1,0:T(8,128)(2,1)}), bf16[32,32,1536]{2,1,0:T(8,128)(2,1)}, u32[]{:S(2)}, u32[]{:S(2)}) %all-to-all-start.1) | async-done | bytes 3145760 | tf_op jit(solution)/shard_map/all_to_all | solution.py:31
  96.8 6.4 %convolution_convert_fusion.1 = bf16[1024,768]{1,0:T(8,128)(2,1)} fusion(bf16[1024,1536]{1,0:T(8,128)(2,1)} %bitcast.3, bf16[1536,768]{1,0:T(8,128)(2,1)} %param.10), kind=kOutput, calls=%fused_computation.55 | convolution fusion | flops 2416705536 | bytes 7077888 | tf_op jit(solution)/shard_map/dot_general | solution.py:40
  103.2 7.1 %scatter_custom_fusion = bf16[1024,768]{1,0:T(8,128)(2,1)} fusion(s32[1024]{0:T(1024)S(1)} %bitcast.168, bf16[1024,768]{1,0:T(8,128)(2,1)} %convolution_convert_fusion.1, bf16[]{:T(256)} %constant.20.clone.1), kind=kCustom, calls=%fused_computation.109 | custom fusion | bytes 1573376 | tf_op jit(solution)/shard_map/scatter | solution.py:46
  110.3 1.8 convert_reduce_fusion
  112.8 4.9 %convolution_convert_fusion = bf16[1024,2304]{1,0:T(8,128)(2,1)S(1)} fusion(bf16[768,2304]{1,0:T(8,128)(2,1)S(1)} %copy-done, bf16[1024,768]{1,0:T(8,128)(2,1)S(1)} %copy-done.2, f32[768]{0:T(1024)S(1)} %copy-done.54, f32[1024]{0:T(1024)S(1)} %add_rsqrt_fusion, f32[1024]{0:T(1024)S(1)} %broadcast_multiply_fusion), kind=kOutput, calls=%fused_computation.32 | convolution fusion | flops 3630170112 | bytes 9841664 | tf_op jit(solution)/shard_map/dot_general | solution.py:58
  119.2 6.0 %reshape_reshape.10 = bf16[128,8,16,48]{3,2,1,0:T(8,128)(2,1)} reshape(bf16[1024,768]{1,0:T(8,128)(2,1)S(1)} %get-tuple-element.12) | data formatting | bytes 3145728 | tf_op jit(solution)/shard_map/reshape;reshape | solution.py:73
  125.2 6.4 %copy.30 = bf16[128,8,16,48]{0,3,2,1:T(8,128)(2,1)} copy(bf16[128,8,16,48]{3,2,1,0:T(8,128)(2,1)} %reshape_reshape.10) | data formatting | bytes 3145728 | tf_op jit(solution)/shard_map/reshape;reshape | solution.py:73
  131.6 6.0 %reshape_reshape.11 = bf16[128,8,16,48]{3,2,1,0:T(8,128)(2,1)} reshape(bf16[1024,768]{1,0:T(8,128)(2,1)S(1)} %get-tuple-element.14) | data formatting | bytes 3145728 | tf_op jit(solution)/shard_map/reshape;reshape | solution.py:76
  137.6 6.4 %copy.31 = bf16[128,8,16,48]{0,3,2,1:T(8,128)(2,1)} copy(bf16[128,8,16,48]{3,2,1,0:T(8,128)(2,1)} %reshape_reshape.11) | data formatting | bytes 3145728 | tf_op jit(solution)/shard_map/reshape;reshape | solution.py:76
  144.0 2.1 gather_fusion.1
  146.1 2.0 gather_fusion.2
  155.7 6.0 %reshape_reshape.9 = bf16[128,8,16,48]{3,2,1,0:T(8,128)(2,1)} reshape(bf16[1024,768]{1,0:T(8,128)(2,1)S(1)} %copy-done.5) | data formatting | bytes 3145728 | tf_op jit(solution)/shard_map/reshape;reshape | solution.py:70
  161.7 1.7 copy.27
  163.4 2.6 copy.28
  167.6 6.8 %copy.29 = bf16[128,8,16,48]{0,3,2,1:T(8,128)(2,1)} copy(bf16[128,8,16,48]{3,2,1,0:T(8,128)(2,1)} %reshape_reshape.9) | data formatting | bytes 3145728 | tf_op jit(solution)/shard_map/reshape;reshape | solution.py:70
  174.4 2.0 gather_fusion
  176.4 7.8 %fusion = (f32[4,1024]{1,0:T(4,128)S(1)}, f32[4,1024,1024]{1,2,0:T(8,128)}) fusion(pred[1024]{0:T(1024)(128)(4,1)S(1)} %add_compare_fusion.1, bf16[1024,16,48]{0,2,1:T(8,128)(2,1)S(1)} %bitcast.144, bf16[1024,16,48]{0,2,1:T(8,128)(2,1)S(1)} %bitcast.148), kind=kOutput, calls=%fused_computation.12 | convolution fusion | flops 415232000 | bytes 18760704 | tf_op jit(solution)/shard_map/qhd,khd->hqk/dot_general | solution.py:99
  186.2 8.1 %fusion.124 = f32[4,1024,1024]{1,2,0:T(8,128)} fusion(bf16[1024,16,48]{0,2,1:T(8,128)(2,1)S(1)} %bitcast.145, bf16[1024,16,48]{0,2,1:T(8,128)(2,1)S(1)} %bitcast.149), kind=kOutput, calls=%fused_computation.117 | convolution fusion | flops 402653184 | bytes 18743296 | tf_op jit(solution)/shard_map/qhd,khd->hqk/dot_general | solution.py:99
  194.3 8.1 %fusion.120 = f32[4,1024,1024]{1,2,0:T(8,128)} fusion(bf16[1024,16,48]{0,2,1:T(8,128)(2,1)S(1)} %bitcast.146, bf16[1024,16,48]{0,2,1:T(8,128)(2,1)S(1)} %bitcast.150), kind=kOutput, calls=%fused_computation.113 | convolution fusion | flops 402653184 | bytes 18743296 | tf_op jit(solution)/shard_map/qhd,khd->hqk/dot_general | solution.py:99
  202.4 2.2 fusion.159
  209.7 24.1 %fusion.4 = (f32[4,1024]{1,0:T(4,128)}, f32[4,1024]{1,0:T(4,128)S(1)}, f32[4,1024]{1,0:T(4,128)S(1)}, f32[4,1024]{1,0:T(4,128)S(1)}, f32[4,1024,1024]{1,2,0:T(8,128)}) fusion(f32[4,1024,1024]{1,2,0:T(8,128)} %get-tuple-element.30, f32[4,1024]{1,0:T(4,128)S(1)} %select_n.189, pred[1024]{0:T(1024)(128)(4,1)S(1)} %add_compare_fusion.1, ...), kind=kOutput, calls=%fused_computation.16 | convolution fusion | flops 457162752 | bytes 69157888 | tf_op jit(solution)/shard_map/qhd,khd->hqk/dot_general | solution.py:99
  234.2 1.8 fusion.32
  239.7 2.2 convolution_bitcast_fusion.1
  243.5 1.8 fusion.34
  249.3 18.9 %fusion.6 = (f32[4,1024]{1,0:T(4,128)S(1)}, f32[4,1024]{1,0:T(4,128)S(1)}, f32[4,1024]{1,0:T(4,128)S(1)}) fusion(f32[4,1024,1024]{1,2,0:T(8,128)} %get-tuple-element.33, f32[4,1024]{1,0:T(4,128)S(1)} %select_n.195, pred[1024]{0:T(1024)(128)(4,1)S(1)} %copy-done.48, f32[4,1024]{1,0:T(4,128)S(1)} %select_n.201, f32[4,1024,1024]{1,2,0:T(8,128)} %fusion.124, ...), kind=kLoop, calls=%fused_computation.18 | loop fusion | flops 50319360 | bytes 50430976 | tf_op jit(solution)/shard_map/reduce_sum | solution.py:139
  277.8 9.7 %fusion.95 = bf16[1024,4,48]{0,2,1:T(8,128)(2,1)S(1)} fusion(bf16[1024,16,48]{0,2,1:T(8,128)(2,1)} %bitcast.155, f32[4,1024,1024]{1,2,0:T(8,128)} %get-tuple-element.30, f32[4,1024]{1,0:T(4,128)} %copy-done.31, pred[1024]{0:T(1024)(128)(4,1)} %copy-done.47, f32[1024,4,48]{0,2,1:T(8,128)S(1)} %copy.34, f32[1024,4]{0,1:T(4,128)} %div.48, ...), kind=kOutput, calls=%fused_computation.102 | convolution fusion | flops 420216832 | bytes 19567616 | tf_op jit(solution)/shard_map/hqk,khd->qhd/dot_general | solution.py:140
  287.6 8.1 %fusion.101 = bf16[1024,4,48]{0,2,1:T(8,128)(2,1)S(1)} fusion(bf16[1024,16,48]{0,2,1:T(8,128)(2,1)S(1)} %bitcast.156, f32[4,1024,1024]{1,2,0:T(8,128)} %get-tuple-element.33, f32[4,1024]{1,0:T(4,128)S(1)} %copy-done.20, pred[1024]{0:T(1024)(128)(4,1)S(1)} %copy-done.49, f32[1024,4,48]{0,2,1:T(8,128)S(1)} %copy-done.12, f32[1024,4]{0,1:T(4,128)S(1)} %copy-done.28, ...), kind=kOutput, calls=%fused_computation.104 | convolution fusion | flops 420216832 | bytes 19567616 | tf_op jit(solution)/shard_map/hqk,khd->qhd/dot_general | solution.py:140
  295.7 8.1 %fusion.107 = bf16[1024,4,48]{0,2,1:T(8,128)(2,1)S(1)} fusion(bf16[1024,16,48]{0,2,1:T(8,128)(2,1)S(1)} %bitcast.157, f32[4,1024,1024]{1,2,0:T(8,128)} %fusion.124, f32[4,1024]{1,0:T(4,128)S(1)} %select_n.201, pred[1024]{0:T(1024)(128)(4,1)S(1)} %copy-done.49, f32[1024,4,48]{0,2,1:T(8,128)S(1)} %copy-done.13, f32[1024,4]{0,1:T(4,128)S(1)} %copy-done.30, ...), kind=kOutput, calls=%fused_computation.106 | convolution fusion | flops 420216832 | bytes 19567616 | tf_op jit(solution)/shard_map/hqk,khd->qhd/dot_general | solution.py:140
  303.8 8.2 %fusion.113 = bf16[1024,4,48]{0,2,1:T(8,128)(2,1)S(1)} fusion(bf16[1024,16,48]{0,2,1:T(8,128)(2,1)S(1)} %bitcast.158, f32[4,1024,1024]{1,2,0:T(8,128)} %fusion.120, f32[4,1024]{1,0:T(4,128)S(1)} %copy-done.18, pred[1024]{0:T(1024)(128)(4,1)S(1)} %copy-done.49, f32[1024,4,48]{0,2,1:T(8,128)S(1)} %copy-done.14, f32[1024,4]{0,1:T(4,128)S(1)} %copy-done.29, ...), kind=kOutput, calls=%fused_computation.108 | convolution fusion | flops 420216832 | bytes 19567616 | tf_op jit(solution)/shard_map/hqk,khd->qhd/dot_general | solution.py:140
  313.7 2.7 fusion.47
  (203 shorter events, 41.2 us)
Async XLA Ops:
  6.5 106.3 %copy-start = (bf16[768,2304]{1,0:T(8,128)(2,1)S(1)}, bf16[768,2304]{1,0:T(8,128)(2,1)}, u32[]{:S(2)}) copy-start(bf16[768,2304]{1,0:T(8,128)(2,1)} %param.12) | copy-start | bytes 10616836
  21.8 75.0 %all-to-all-start.1 = ((bf16[32,32,1536]{2,1,0:T(8,128)(2,1)}), bf16[32,32,1536]{2,1,0:T(8,128)(2,1)}, u32[]{:S(2)}, u32[]{:S(2)}) async-start(bf16[32,32,1536]{2,1,0:T(8,128)(2,1)} %bitcast.152), calls=%async_computation.1 | async-start | bytes 6291456 | tf_op jit(solution)/shard_map/all_to_all | solution.py:31
  25.4 177.0 %all-gather.2.cloned.1.call-start = ((), (), s32[]{:S(2)}) async-start(), calls=%async_computation.2 | async-start | bytes 3538944 | tf_op jit(solution)/shard_map/all_gather | solution.py:85
  103.2 9.6 %copy-start.54 = (f32[768]{0:T(1024)S(1)}, f32[768]{0:T(1024)}, u32[]{:S(2)}) copy-start(f32[768]{0:T(1024)} %param.11) | copy-start | bytes 9220
  144.0 11.7 %copy-start.5 = (bf16[1024,768]{1,0:T(8,128)(2,1)S(1)}, bf16[1024,768]{1,0:T(8,128)(2,1)}, u32[]{:S(2)}) copy-start(bf16[1024,768]{1,0:T(8,128)(2,1)} %get-tuple-element.13) | copy-start | bytes 4718596
  149.7 35.4 %copy-start.41 = (pred[4,8]{1,0:T(4,128)(4,1)}, pred[4,8]{1,0:T(4,128)(4,1)S(1)}, u32[]{:S(2)}) copy-start(pred[4,8]{1,0:T(4,128)(4,1)S(1)} %get-tuple-element.28) | copy-start | bytes 100
  149.7 84.3 %copy-start.39 = (pred[4,8]{1,0:T(4,128)(4,1)}, pred[4,8]{1,0:T(4,128)(4,1)S(1)}, u32[]{:S(2)}) copy-start(pred[4,8]{1,0:T(4,128)(4,1)S(1)} %get-tuple-element.27) | copy-start | bytes 100
  149.7 88.2 %copy-start.37 = (pred[4,8]{1,0:T(4,128)(4,1)}, pred[4,8]{1,0:T(4,128)(4,1)S(1)}, u32[]{:S(2)}) copy-start(pred[4,8]{1,0:T(4,128)(4,1)S(1)} %get-tuple-element.26) | copy-start | bytes 100
  149.7 93.6 %copy-start.35 = (pred[4,8]{1,0:T(4,128)(4,1)}, pred[4,8]{1,0:T(4,128)(4,1)S(1)}, u32[]{:S(2)}) copy-start(pred[4,8]{1,0:T(4,128)(4,1)S(1)} %get-tuple-element.25) | copy-start | bytes 100
  155.5 54.2 %copy-start.47 = (pred[1024]{0:T(1024)(128)(4,1)}, pred[1024]{0:T(1024)(128)(4,1)S(1)}, u32[]{:S(2)}) copy-start(pred[1024]{0:T(1024)(128)(4,1)S(1)} %add_compare_fusion.1) | copy-start | bytes 3076
  167.6 8.9 %copy-start.6 = (bf16[1024,768]{0,1:T(8,128)(2,1)S(1)}, bf16[1024,768]{0,1:T(8,128)(2,1)}, u32[]{:S(2)}) copy-start(bf16[1024,768]{0,1:T(8,128)(2,1)} %copy.28) | copy-start | bytes 4718596
  209.7 24.2 %copy-start.31 = (f32[4,1024]{1,0:T(4,128)}, f32[4,1024]{1,0:T(4,128)S(1)}, u32[]{:S(2)}) copy-start(f32[4,1024]{1,0:T(4,128)S(1)} %select_n.189) | copy-start | bytes 49156
  233.8 9.3 %copy-start.21 = (f32[4,1024]{1,0:T(4,128)}, f32[4,1024]{1,0:T(4,128)S(1)}, u32[]{:S(2)}) copy-start(f32[4,1024]{1,0:T(4,128)S(1)} %get-tuple-element.8) | copy-start | bytes 49156
  249.2 19.0 %copy-start.19 = (f32[4,1024]{1,0:T(4,128)}, f32[4,1024]{1,0:T(4,128)S(1)}, u32[]{:S(2)}) copy-start(f32[4,1024]{1,0:T(4,128)S(1)} %select_n.195) | copy-start | bytes 49156
  249.2 18.9 %copy-start.17 = (f32[4,1024]{1,0:T(4,128)}, f32[4,1024]{1,0:T(4,128)S(1)}, u32[]{:S(2)}) copy-start(f32[4,1024]{1,0:T(4,128)S(1)} %select_n.207) | copy-start | bytes 49156
  249.3 19.1 %copy-start.27 = (f32[4,1024]{1,0:T(4,128)S(1)}, f32[4,1024]{1,0:T(4,128)}, u32[]{:S(2)}) copy-start(f32[4,1024]{1,0:T(4,128)} %get-tuple-element.5) | copy-start | bytes 49156
  249.3 19.3 %copy-start.40 = (pred[4,8]{1,0:T(4,128)(4,1)S(1)}, pred[4,8]{1,0:T(4,128)(4,1)}, u32[]{:S(2)}) copy-start(pred[4,8]{1,0:T(4,128)(4,1)} %copy-done.39) | copy-start | bytes 100
  249.3 19.3 %copy-start.42 = (pred[4,8]{1,0:T(4,128)(4,1)S(1)}, pred[4,8]{1,0:T(4,128)(4,1)}, u32[]{:S(2)}) copy-start(pred[4,8]{1,0:T(4,128)(4,1)} %copy-done.41) | copy-start | bytes 100
  249.3 19.3 %copy-start.43 = (f32[4,128]{1,0:T(4,128)S(1)}, f32[4,128]{1,0:T(4,128)}, u32[]{:S(2)}) copy-start(f32[4,128]{1,0:T(4,128)} %fusion.35) | copy-start | bytes 6148
  249.3 19.3 %copy-start.45 = (f32[4,128]{1,0:T(4,128)S(1)}, f32[4,128]{1,0:T(4,128)}, u32[]{:S(2)}) copy-start(f32[4,128]{1,0:T(4,128)} %fusion.37) | copy-start | bytes 6148
  277.7 9.7 %copy-start.7 = (bf16[1024,768]{0,1:T(8,128)(2,1)S(1)}, bf16[1024,768]{0,1:T(8,128)(2,1)}, u32[]{:S(2)}) copy-start(bf16[1024,768]{0,1:T(8,128)(2,1)} %copy.26) | copy-start | bytes 4718596
  277.7 9.7 %copy-start.12 = (f32[1024,4,48]{0,2,1:T(8,128)S(1)}, f32[1024,4,48]{0,2,1:T(8,128)}, u32[]{:S(2)}) copy-start(f32[1024,4,48]{0,2,1:T(8,128)} %copy.37) | copy-start | bytes 2359300
  277.7 9.7 %copy-start.20 = (f32[4,1024]{1,0:T(4,128)S(1)}, f32[4,1024]{1,0:T(4,128)}, u32[]{:S(2)}) copy-start(f32[4,1024]{1,0:T(4,128)} %copy-done.19) | copy-start | bytes 49156
  277.7 9.8 %copy-start.28 = (f32[1024,4]{0,1:T(4,128)S(1)}, f32[1024,4]{0,1:T(4,128)}, u32[]{:S(2)}) copy-start(f32[1024,4]{0,1:T(4,128)} %div.51) | copy-start | bytes 49156
  277.7 9.8 %copy-start.49 = (pred[1024]{0:T(1024)(128)(4,1)S(1)}, pred[1024]{0:T(1024)(128)(4,1)}, u32[]{:S(2)}) copy-start(pred[1024]{0:T(1024)(128)(4,1)} %copy-done.47) | copy-start | bytes 3076
  277.8 9.8 %copy-start.52 = (pred[1024,4]{0,1:T(4,128)(4,1)S(1)}, pred[1024,4]{0,1:T(4,128)(4,1)}, u32[]{:S(2)}) copy-start(pred[1024,4]{0,1:T(4,128)(4,1)} %broadcast_in_dim.371) | copy-start | bytes 12292
  287.5 8.1 %copy-start.13 = (f32[1024,4,48]{0,2,1:T(8,128)S(1)}, f32[1024,4,48]{0,2,1:T(8,128)}, u32[]{:S(2)}) copy-start(f32[1024,4,48]{0,2,1:T(8,128)} %copy.40) | copy-start | bytes 2359300
  287.5 8.1 %copy-start.30 = (f32[1024,4]{0,1:T(4,128)S(1)}, f32[1024,4]{0,1:T(4,128)}, u32[]{:S(2)}) copy-start(f32[1024,4]{0,1:T(4,128)} %div.54) | copy-start | bytes 49156
  287.5 8.1 %copy-start.51 = (pred[1024,4]{0,1:T(4,128)(4,1)S(1)}, pred[1024,4]{0,1:T(4,128)(4,1)}, u32[]{:S(2)}) copy-start(pred[1024,4]{0,1:T(4,128)(4,1)} %broadcast_in_dim.382) | copy-start | bytes 12292
  295.7 8.1 %copy-start.14 = (f32[1024,4,48]{0,2,1:T(8,128)S(1)}, f32[1024,4,48]{0,2,1:T(8,128)}, u32[]{:S(2)}) copy-start(f32[1024,4,48]{0,2,1:T(8,128)} %copy.43) | copy-start | bytes 2359300
  295.7 8.1 %copy-start.18 = (f32[4,1024]{1,0:T(4,128)S(1)}, f32[4,1024]{1,0:T(4,128)}, u32[]{:S(2)}) copy-start(f32[4,1024]{1,0:T(4,128)} %copy-done.17) | copy-start | bytes 49156
  295.7 8.1 %copy-start.29 = (f32[1024,4]{0,1:T(4,128)S(1)}, f32[1024,4]{0,1:T(4,128)}, u32[]{:S(2)}) copy-start(f32[1024,4]{0,1:T(4,128)} %div.57) | copy-start | bytes 49156
  (25 other events, 59.6 us)
Sparse Core Ops, SparseCore 0:
  149.1 32.0 all-gather.1
where the time goes:
time: 329 us; the launch traced here: 323 us
  matrix products  107 us (33%)
  local copies, waits for them, and re-layouts  83.9 us (26%)
  waiting for transfers between devices  69.2 us (21%)
  other arithmetic  30.6 us (9%)
  between operations  15.3 us (5%)
  blocking collectives  14.4 us (4%)
  starting transfers between devices  3.57 us (1%)
    all_to_all x1, waiting for transfers between devices, body(): lax.all_to_all(embeddings.reshape(device_count, block_rows, embeddings.sh...  69.2 us
    dot_general x4, matrix products, body(): jnp.einsum('qhd,khd->hqk', query_matrix[:, chosen], key_matrix[:, chosen]...  48.1 us
    dot_general x4, matrix products, body(): jnp.einsum('hqk,khd->qhd', local_weights.astype(jnp.bfloat16), value_matr...  34 us
    reduce_sum x1, other arithmetic, body(): nearby_total = jnp.sum(local_weights, axis=-1)  18.9 us
    all_to_all x1, blocking collectives, body(): lax.all_to_all(parted_slot, ('tile', 'seq'), split_axis=0, concat_axis=0,...  14.4 us
    another operation x2, local copies, waits for them, and re-layouts, body(): query_matrix.reshape(dilated_row_index, DILATION_RATE, HEAD_COUNT, head_f...  12.8 us
    another operation x2, local copies, waits for them, and re-layouts, body(): key_matrix.reshape(dilated_row_index, DILATION_RATE, HEAD_COUNT, head_fea...  12.4 us
    another operation x2, local copies, waits for them, and re-layouts, body(): value_matrix.reshape(dilated_row_index, DILATION_RATE, HEAD_COUNT, head_f...  12.4 us
  transfers between devices with their start and end apart: 2, of which 1 were waited for; matrix products, arithmetic and copies ran while one was open for 17% of the time, Pallas kernels for 0%

commit v1 on v0

--- a/solution.py
+++ b/solution.py
@@ -27,9 +27,12 @@
     model_width = in_weight.shape[1]
     my_index = lax.axis_index("tile") * seq_count + lax.axis_index("seq")
     parted_slot = slot.reshape(device_count, block_rows)
+    projected = jnp.dot(embeddings, in_weight, preferred_element_type=jnp.float32).astype(
+        jnp.bfloat16
+    )
     arrived_raw, arrived_slot = (
         lax.all_to_all(
-            embeddings.reshape(device_count, block_rows, embeddings.shape[1]),
+            projected.reshape(device_count, block_rows, model_width),
             ("tile", "seq"),
             split_axis=0,
             concat_axis=0,
@@ -37,11 +40,7 @@
         ),
         lax.all_to_all(parted_slot, ("tile", "seq"), split_axis=0, concat_axis=0, tiled=True),
     )
-    arrived = jnp.dot(
-        arrived_raw.reshape(sequence_rows, embeddings.shape[1]),
-        in_weight,
-        preferred_element_type=jnp.float32,
-    ).astype(jnp.bfloat16)
+    arrived = arrived_raw.reshape(sequence_rows, model_width)
     local_slot = arrived_slot.reshape(sequence_rows) - my_index * sequence_rows
     features = jnp.zeros((sequence_rows, model_width), jnp.bfloat16).at[local_slot].set(arrived)
     slide_length = lengths[0]

time: 329 us -> 291 us (0.88)
  waiting for transfers between devices: 69.2 us -> 36.3 us
  blocking collectives: 14.4 us -> 0 us
  starting transfers between devices: 3.57 us -> 12.5 us
    all_to_all x1 -> x2, waiting for transfers between devices: 69.2 us -> 36.3 us  [the longest x1 35.5 us: body(): lax.all_to_all(projected.reshape(device_count, block_rows, model_width),...]
    all_to_all x1 -> x0, blocking collectives: 14.4 us -> none  [body(): lax.all_to_all(parted_slot, ('tile', 'seq'), split_axis=0, concat_axis=0,...]
    all_to_all x1 -> x2, starting transfers between devices: 3.53 us -> 12.5 us  [the longest x1 7.3 us: body(): lax.all_to_all(parted_slot, ('tile', 'seq'), split_axis=0, concat_axis=0,...]
  transfers between devices with their start and end apart: 2 -> 3, of which waited for: 1 -> 2; matrix products, arithmetic and copies ran while one was open for 17% -> 21% of each run, Pallas kernels for 0% -> 0%
where the time goes in v1:
time: 291 us; the launch traced here: 286 us
  matrix products  106 us (36%)
  local copies, waits for them, and re-layouts  84.4 us (29%)
  waiting for transfers between devices  36.3 us (12%)
  other arithmetic  30.6 us (11%)
  between operations  15.3 us (5%)
  starting transfers between devices  12.5 us (4%)
    dot_general x4, matrix products, body(): jnp.einsum('qhd,khd->hqk', query_matrix[:, chosen], key_matrix[:, chosen]...  48.1 us
    all_to_all x1, waiting for transfers between devices, body(): lax.all_to_all(projected.reshape(device_count, block_rows, model_width),...  35.5 us
    dot_general x4, matrix products, body(): jnp.einsum('hqk,khd->qhd', local_weights.astype(jnp.bfloat16), value_matr...  34 us
    reduce_sum x1, other arithmetic, body(): nearby_total = jnp.sum(local_weights, axis=-1)  18.9 us
    another operation x2, local copies, waits for them, and re-layouts, body(): query_matrix.reshape(dilated_row_index, DILATION_RATE, HEAD_COUNT, head_f...  12.7 us
    another operation x2, local copies, waits for them, and re-layouts, body(): key_matrix.reshape(dilated_row_index, DILATION_RATE, HEAD_COUNT, head_fea...  12.4 us
    another operation x2, local copies, waits for them, and re-layouts, body(): value_matrix.reshape(dilated_row_index, DILATION_RATE, HEAD_COUNT, head_f...  12.4 us
    broadcast_in_dim x16, local copies, waits for them, and re-layouts, body(): jnp.where(group_mask.T[None, :, :, None], distant_accumulator[:, None, :,...  8.75 us
  transfers between devices with their start and end apart: 3, of which 2 were waited for; matrix products, arithmetic and copies ran while one was open for 21% of the time, Pallas kernels for 0%

profile of v1, /device:TPU:0, one launch (start us, length us, event | category | flops | bytes accessed | tf_op | source)
XLA Modules:
  0.0 285.5 jit_solution(8275202056268026142)
XLA Ops:
  8.1 7.3 %all-to-all-start = ((s32[32,1,32]{2,1,0:T(1,128)}), s32[32,1,32]{2,1,0:T(1,128)S(1)}, u32[]{:S(2)}, u32[]{:S(2)}) async-start(s32[32,1,32]{2,1,0:T(1,128)} %all_to_all.9), calls=%async_computation | async-start | bytes 32768 | tf_op jit(solution)/shard_map/all_to_all | solution.py:41
  15.4 6.4 %convolution_convert_fusion.1 = bf16[1024,768]{1,0:T(8,128)(2,1)} fusion(bf16[1024,1536]{1,0:T(8,128)(2,1)} %param.7, bf16[1536,768]{1,0:T(8,128)(2,1)} %param.10), kind=kOutput, calls=%fused_computation.55 | convolution fusion | flops 2416705536 | bytes 7077888 | tf_op jit(solution)/shard_map/dot_general | solution.py:30
  22.5 5.2 %all-to-all-start.1 = ((bf16[32,32,768]{2,1,0:T(8,128)(2,1)}), bf16[32,32,768]{2,1,0:T(8,128)(2,1)}, u32[]{:S(2)}, u32[]{:S(2)}) async-start(bf16[32,32,768]{2,1,0:T(8,128)(2,1)} %bitcast.158), calls=%async_computation.1 | async-start | bytes 3145728 | tf_op jit(solution)/shard_map/all_to_all | solution.py:34
  29.9 35.5 %all-to-all-done.1 = bf16[32,32,768]{2,1,0:T(8,128)(2,1)} async-done(((bf16[32,32,768]{2,1,0:T(8,128)(2,1)}), bf16[32,32,768]{2,1,0:T(8,128)(2,1)}, u32[]{:S(2)}, u32[]{:S(2)}) %all-to-all-start.1) | async-done | bytes 1572896 | tf_op jit(solution)/shard_map/all_to_all | solution.py:34
  65.4 7.0 %scatter_custom_fusion = bf16[1024,768]{1,0:T(8,128)(2,1)} fusion(s32[1024]{0:T(1024)S(1)} %bitcast.168, bf16[1024,768]{1,0:T(8,128)(2,1)} %bitcast.3, bf16[]{:T(256)} %constant.20.clone.1), kind=kCustom, calls=%fused_computation.109 | custom fusion | bytes 1573376 | tf_op jit(solution)/shard_map/scatter | solution.py:45
  72.4 1.8 convert_reduce_fusion
  75.0 4.9 %convolution_convert_fusion = bf16[1024,2304]{1,0:T(8,128)(2,1)S(1)} fusion(bf16[768,2304]{1,0:T(8,128)(2,1)S(1)} %copy-done, bf16[1024,768]{1,0:T(8,128)(2,1)S(1)} %copy-done.2, f32[768]{0:T(1024)S(1)} %copy-done.55, f32[1024]{0:T(1024)S(1)} %add_rsqrt_fusion, f32[1024]{0:T(1024)S(1)} %broadcast_multiply_fusion), kind=kOutput, calls=%fused_computation.32 | convolution fusion | flops 3630170112 | bytes 9841664 | tf_op jit(solution)/shard_map/dot_general | solution.py:57
  81.4 6.0 %reshape_reshape.10 = bf16[128,8,16,48]{3,2,1,0:T(8,128)(2,1)} reshape(bf16[1024,768]{1,0:T(8,128)(2,1)S(1)} %get-tuple-element.12) | data formatting | bytes 3145728 | tf_op jit(solution)/shard_map/reshape;reshape | solution.py:72
  87.4 6.4 %copy.30 = bf16[128,8,16,48]{0,3,2,1:T(8,128)(2,1)} copy(bf16[128,8,16,48]{3,2,1,0:T(8,128)(2,1)} %reshape_reshape.10) | data formatting | bytes 3145728 | tf_op jit(solution)/shard_map/reshape;reshape | solution.py:72
  93.8 6.0 %reshape_reshape.11 = bf16[128,8,16,48]{3,2,1,0:T(8,128)(2,1)} reshape(bf16[1024,768]{1,0:T(8,128)(2,1)S(1)} %get-tuple-element.14) | data formatting | bytes 3145728 | tf_op jit(solution)/shard_map/reshape;reshape | solution.py:75
  99.8 6.4 %copy.31 = bf16[128,8,16,48]{0,3,2,1:T(8,128)(2,1)} copy(bf16[128,8,16,48]{3,2,1,0:T(8,128)(2,1)} %reshape_reshape.11) | data formatting | bytes 3145728 | tf_op jit(solution)/shard_map/reshape;reshape | solution.py:75
  106.2 2.1 gather_fusion.1
  108.3 2.0 gather_fusion.2
  117.9 6.0 %reshape_reshape.9 = bf16[128,8,16,48]{3,2,1,0:T(8,128)(2,1)} reshape(bf16[1024,768]{1,0:T(8,128)(2,1)S(1)} %copy-done.5) | data formatting | bytes 3145728 | tf_op jit(solution)/shard_map/reshape;reshape | solution.py:69
  123.9 1.7 copy.27
  125.6 2.6 copy.28
  129.8 6.7 %copy.29 = bf16[128,8,16,48]{0,3,2,1:T(8,128)(2,1)} copy(bf16[128,8,16,48]{3,2,1,0:T(8,128)(2,1)} %reshape_reshape.9) | data formatting | bytes 3145728 | tf_op jit(solution)/shard_map/reshape;reshape | solution.py:69
  136.6 2.0 gather_fusion
  138.6 7.8 %fusion = (f32[4,1024]{1,0:T(4,128)S(1)}, f32[4,1024,1024]{1,2,0:T(8,128)}) fusion(pred[1024]{0:T(1024)(128)(4,1)S(1)} %add_compare_fusion.1, bf16[1024,16,48]{0,2,1:T(8,128)(2,1)S(1)} %bitcast.144, bf16[1024,16,48]{0,2,1:T(8,128)(2,1)S(1)} %bitcast.148), kind=kOutput, calls=%fused_computation.12 | convolution fusion | flops 415232000 | bytes 18760704 | tf_op jit(solution)/shard_map/qhd,khd->hqk/dot_general | solution.py:98
  148.4 8.1 %fusion.124 = f32[4,1024,1024]{1,2,0:T(8,128)} fusion(bf16[1024,16,48]{0,2,1:T(8,128)(2,1)S(1)} %bitcast.145, bf16[1024,16,48]{0,2,1:T(8,128)(2,1)S(1)} %bitcast.149), kind=kOutput, calls=%fused_computation.117 | convolution fusion | flops 402653184 | bytes 18743296 | tf_op jit(solution)/shard_map/qhd,khd->hqk/dot_general | solution.py:98
  156.5 8.1 %fusion.120 = f32[4,1024,1024]{1,2,0:T(8,128)} fusion(bf16[1024,16,48]{0,2,1:T(8,128)(2,1)S(1)} %bitcast.146, bf16[1024,16,48]{0,2,1:T(8,128)(2,1)S(1)} %bitcast.150), kind=kOutput, calls=%fused_computation.113 | convolution fusion | flops 402653184 | bytes 18743296 | tf_op jit(solution)/shard_map/qhd,khd->hqk/dot_general | solution.py:98
  164.6 2.2 fusion.159
  171.8 24.1 %fusion.4 = (f32[4,1024]{1,0:T(4,128)}, f32[4,1024]{1,0:T(4,128)S(1)}, f32[4,1024]{1,0:T(4,128)S(1)}, f32[4,1024]{1,0:T(4,128)S(1)}, f32[4,1024,1024]{1,2,0:T(8,128)}) fusion(f32[4,1024,1024]{1,2,0:T(8,128)} %get-tuple-element.30, f32[4,1024]{1,0:T(4,128)S(1)} %select_n.189, pred[1024]{0:T(1024)(128)(4,1)S(1)} %add_compare_fusion.1, ...), kind=kOutput, calls=%fused_computation.16 | convolution fusion | flops 457162752 | bytes 69157888 | tf_op jit(solution)/shard_map/qhd,khd->hqk/dot_general | solution.py:98
  196.3 1.8 fusion.32
  201.8 2.2 convolution_bitcast_fusion.1
  205.5 1.8 fusion.34
  211.4 18.9 %fusion.6 = (f32[4,1024]{1,0:T(4,128)S(1)}, f32[4,1024]{1,0:T(4,128)S(1)}, f32[4,1024]{1,0:T(4,128)S(1)}) fusion(f32[4,1024,1024]{1,2,0:T(8,128)} %get-tuple-element.33, f32[4,1024]{1,0:T(4,128)S(1)} %select_n.195, pred[1024]{0:T(1024)(128)(4,1)S(1)} %copy-done.49, f32[4,1024]{1,0:T(4,128)S(1)} %select_n.201, f32[4,1024,1024]{1,2,0:T(8,128)} %fusion.124, ...), kind=kLoop, calls=%fused_computation.18 | loop fusion | flops 50319360 | bytes 50430976 | tf_op jit(solution)/shard_map/reduce_sum | solution.py:138
  239.8 9.7 %fusion.95 = bf16[1024,4,48]{0,2,1:T(8,128)(2,1)S(1)} fusion(bf16[1024,16,48]{0,2,1:T(8,128)(2,1)} %bitcast.154, f32[4,1024,1024]{1,2,0:T(8,128)} %get-tuple-element.30, f32[4,1024]{1,0:T(4,128)} %copy-done.32, pred[1024]{0:T(1024)(128)(4,1)} %copy-done.48, f32[1024,4,48]{0,2,1:T(8,128)S(1)} %copy.34, f32[1024,4]{0,1:T(4,128)} %div.48, ...), kind=kOutput, calls=%fused_computation.102 | convolution fusion | flops 420216832 | bytes 19567616 | tf_op jit(solution)/shard_map/hqk,khd->qhd/dot_general | solution.py:139
  249.6 8.1 %fusion.101 = bf16[1024,4,48]{0,2,1:T(8,128)(2,1)S(1)} fusion(bf16[1024,16,48]{0,2,1:T(8,128)(2,1)S(1)} %bitcast.155, f32[4,1024,1024]{1,2,0:T(8,128)} %get-tuple-element.33, f32[4,1024]{1,0:T(4,128)S(1)} %copy-done.20, pred[1024]{0:T(1024)(128)(4,1)S(1)} %copy-done.50, f32[1024,4,48]{0,2,1:T(8,128)S(1)} %copy-done.12, f32[1024,4]{0,1:T(4,128)S(1)} %copy-done.29, ...), kind=kOutput, calls=%fused_computation.104 | convolution fusion | flops 420216832 | bytes 19567616 | tf_op jit(solution)/shard_map/hqk,khd->qhd/dot_general | solution.py:139
  257.7 8.1 %fusion.107 = bf16[1024,4,48]{0,2,1:T(8,128)(2,1)S(1)} fusion(bf16[1024,16,48]{0,2,1:T(8,128)(2,1)S(1)} %bitcast.156, f32[4,1024,1024]{1,2,0:T(8,128)} %fusion.124, f32[4,1024]{1,0:T(4,128)S(1)} %select_n.201, pred[1024]{0:T(1024)(128)(4,1)S(1)} %copy-done.50, f32[1024,4,48]{0,2,1:T(8,128)S(1)} %copy-done.13, f32[1024,4]{0,1:T(4,128)S(1)} %copy-done.31, ...), kind=kOutput, calls=%fused_computation.106 | convolution fusion | flops 420216832 | bytes 19567616 | tf_op jit(solution)/shard_map/hqk,khd->qhd/dot_general | solution.py:139
  265.8 8.2 %fusion.113 = bf16[1024,4,48]{0,2,1:T(8,128)(2,1)S(1)} fusion(bf16[1024,16,48]{0,2,1:T(8,128)(2,1)S(1)} %bitcast.157, f32[4,1024,1024]{1,2,0:T(8,128)} %fusion.120, f32[4,1024]{1,0:T(4,128)S(1)} %copy-done.18, pred[1024]{0:T(1024)(128)(4,1)S(1)} %copy-done.50, f32[1024,4,48]{0,2,1:T(8,128)S(1)} %copy-done.14, f32[1024,4]{0,1:T(4,128)S(1)} %copy-done.30, ...), kind=kOutput, calls=%fused_computation.108 | convolution fusion | flops 420216832 | bytes 19567616 | tf_op jit(solution)/shard_map/hqk,khd->qhd/dot_general | solution.py:139
  275.8 2.7 fusion.47
  (206 shorter events, 42.7 us)
Async XLA Ops:
  6.5 68.4 %copy-start = (bf16[768,2304]{1,0:T(8,128)(2,1)S(1)}, bf16[768,2304]{1,0:T(8,128)(2,1)}, u32[]{:S(2)}) copy-start(bf16[768,2304]{1,0:T(8,128)(2,1)} %param.12) | copy-start | bytes 10616836
  8.1 14.5 %all-to-all-start = ((s32[32,1,32]{2,1,0:T(1,128)}), s32[32,1,32]{2,1,0:T(1,128)S(1)}, u32[]{:S(2)}, u32[]{:S(2)}) async-start(s32[32,1,32]{2,1,0:T(1,128)} %all_to_all.9), calls=%async_computation | async-start | bytes 32768 | tf_op jit(solution)/shard_map/all_to_all | solution.py:41
  22.5 42.9 %all-to-all-start.1 = ((bf16[32,32,768]{2,1,0:T(8,128)(2,1)}), bf16[32,32,768]{2,1,0:T(8,128)(2,1)}, u32[]{:S(2)}, u32[]{:S(2)}) async-start(bf16[32,32,768]{2,1,0:T(8,128)(2,1)} %bitcast.158), calls=%async_computation.1 | async-start | bytes 3145728 | tf_op jit(solution)/shard_map/all_to_all | solution.py:34
  27.7 136.9 %all-gather.2.cloned.1.call-start = ((), (), s32[]{:S(2)}) async-start(), calls=%async_computation.2 | async-start | bytes 3538944 | tf_op jit(solution)/shard_map/all_gather | solution.py:84
  65.4 9.6 %copy-start.55 = (f32[768]{0:T(1024)S(1)}, f32[768]{0:T(1024)}, u32[]{:S(2)}) copy-start(f32[768]{0:T(1024)} %param.11) | copy-start | bytes 9220
  106.2 11.7 %copy-start.5 = (bf16[1024,768]{1,0:T(8,128)(2,1)S(1)}, bf16[1024,768]{1,0:T(8,128)(2,1)}, u32[]{:S(2)}) copy-start(bf16[1024,768]{1,0:T(8,128)(2,1)} %get-tuple-element.13) | copy-start | bytes 4718596
  111.9 35.4 %copy-start.42 = (pred[4,8]{1,0:T(4,128)(4,1)}, pred[4,8]{1,0:T(4,128)(4,1)S(1)}, u32[]{:S(2)}) copy-start(pred[4,8]{1,0:T(4,128)(4,1)S(1)} %get-tuple-element.28) | copy-start | bytes 100
  111.9 84.2 %copy-start.40 = (pred[4,8]{1,0:T(4,128)(4,1)}, pred[4,8]{1,0:T(4,128)(4,1)S(1)}, u32[]{:S(2)}) copy-start(pred[4,8]{1,0:T(4,128)(4,1)S(1)} %get-tuple-element.27) | copy-start | bytes 100
  111.9 88.1 %copy-start.38 = (pred[4,8]{1,0:T(4,128)(4,1)}, pred[4,8]{1,0:T(4,128)(4,1)S(1)}, u32[]{:S(2)}) copy-start(pred[4,8]{1,0:T(4,128)(4,1)S(1)} %get-tuple-element.26) | copy-start | bytes 100
  111.9 93.4 %copy-start.36 = (pred[4,8]{1,0:T(4,128)(4,1)}, pred[4,8]{1,0:T(4,128)(4,1)S(1)}, u32[]{:S(2)}) copy-start(pred[4,8]{1,0:T(4,128)(4,1)S(1)} %get-tuple-element.25) | copy-start | bytes 100
  117.8 54.1 %copy-start.48 = (pred[1024]{0:T(1024)(128)(4,1)}, pred[1024]{0:T(1024)(128)(4,1)S(1)}, u32[]{:S(2)}) copy-start(pred[1024]{0:T(1024)(128)(4,1)S(1)} %add_compare_fusion.1) | copy-start | bytes 3076
  129.8 8.8 %copy-start.6 = (bf16[1024,768]{0,1:T(8,128)(2,1)S(1)}, bf16[1024,768]{0,1:T(8,128)(2,1)}, u32[]{:S(2)}) copy-start(bf16[1024,768]{0,1:T(8,128)(2,1)} %copy.28) | copy-start | bytes 4718596
  171.8 24.1 %copy-start.32 = (f32[4,1024]{1,0:T(4,128)}, f32[4,1024]{1,0:T(4,128)S(1)}, u32[]{:S(2)}) copy-start(f32[4,1024]{1,0:T(4,128)S(1)} %select_n.189) | copy-start | bytes 49156
  195.9 9.2 %copy-start.21 = (f32[4,1024]{1,0:T(4,128)}, f32[4,1024]{1,0:T(4,128)S(1)}, u32[]{:S(2)}) copy-start(f32[4,1024]{1,0:T(4,128)S(1)} %get-tuple-element.8) | copy-start | bytes 49156
  211.3 19.0 %copy-start.19 = (f32[4,1024]{1,0:T(4,128)}, f32[4,1024]{1,0:T(4,128)S(1)}, u32[]{:S(2)}) copy-start(f32[4,1024]{1,0:T(4,128)S(1)} %select_n.195) | copy-start | bytes 49156
  211.3 18.9 %copy-start.17 = (f32[4,1024]{1,0:T(4,128)}, f32[4,1024]{1,0:T(4,128)S(1)}, u32[]{:S(2)}) copy-start(f32[4,1024]{1,0:T(4,128)S(1)} %select_n.207) | copy-start | bytes 49156
  211.3 19.1 %copy-start.28 = (f32[4,1024]{1,0:T(4,128)S(1)}, f32[4,1024]{1,0:T(4,128)}, u32[]{:S(2)}) copy-start(f32[4,1024]{1,0:T(4,128)} %get-tuple-element.5) | copy-start | bytes 49156
  211.3 19.3 %copy-start.41 = (pred[4,8]{1,0:T(4,128)(4,1)S(1)}, pred[4,8]{1,0:T(4,128)(4,1)}, u32[]{:S(2)}) copy-start(pred[4,8]{1,0:T(4,128)(4,1)} %copy-done.40) | copy-start | bytes 100
  211.3 19.3 %copy-start.43 = (pred[4,8]{1,0:T(4,128)(4,1)S(1)}, pred[4,8]{1,0:T(4,128)(4,1)}, u32[]{:S(2)}) copy-start(pred[4,8]{1,0:T(4,128)(4,1)} %copy-done.42) | copy-start | bytes 100
  211.3 19.3 %copy-start.44 = (f32[4,128]{1,0:T(4,128)S(1)}, f32[4,128]{1,0:T(4,128)}, u32[]{:S(2)}) copy-start(f32[4,128]{1,0:T(4,128)} %fusion.35) | copy-start | bytes 6148
  211.4 19.3 %copy-start.46 = (f32[4,128]{1,0:T(4,128)S(1)}, f32[4,128]{1,0:T(4,128)}, u32[]{:S(2)}) copy-start(f32[4,128]{1,0:T(4,128)} %fusion.37) | copy-start | bytes 6148
  239.8 9.7 %copy-start.7 = (bf16[1024,768]{0,1:T(8,128)(2,1)S(1)}, bf16[1024,768]{0,1:T(8,128)(2,1)}, u32[]{:S(2)}) copy-start(bf16[1024,768]{0,1:T(8,128)(2,1)} %copy.26) | copy-start | bytes 4718596
  239.8 9.7 %copy-start.12 = (f32[1024,4,48]{0,2,1:T(8,128)S(1)}, f32[1024,4,48]{0,2,1:T(8,128)}, u32[]{:S(2)}) copy-start(f32[1024,4,48]{0,2,1:T(8,128)} %copy.37) | copy-start | bytes 2359300
  239.8 9.7 %copy-start.20 = (f32[4,1024]{1,0:T(4,128)S(1)}, f32[4,1024]{1,0:T(4,128)}, u32[]{:S(2)}) copy-start(f32[4,1024]{1,0:T(4,128)} %copy-done.19) | copy-start | bytes 49156
  239.8 9.8 %copy-start.29 = (f32[1024,4]{0,1:T(4,128)S(1)}, f32[1024,4]{0,1:T(4,128)}, u32[]{:S(2)}) copy-start(f32[1024,4]{0,1:T(4,128)} %div.51) | copy-start | bytes 49156
  239.8 9.8 %copy-start.50 = (pred[1024]{0:T(1024)(128)(4,1)S(1)}, pred[1024]{0:T(1024)(128)(4,1)}, u32[]{:S(2)}) copy-start(pred[1024]{0:T(1024)(128)(4,1)} %copy-done.48) | copy-start | bytes 3076
  239.8 9.8 %copy-start.53 = (pred[1024,4]{0,1:T(4,128)(4,1)S(1)}, pred[1024,4]{0,1:T(4,128)(4,1)}, u32[]{:S(2)}) copy-start(pred[1024,4]{0,1:T(4,128)(4,1)} %broadcast_in_dim.371) | copy-start | bytes 12292
  249.6 8.1 %copy-start.13 = (f32[1024,4,48]{0,2,1:T(8,128)S(1)}, f32[1024,4,48]{0,2,1:T(8,128)}, u32[]{:S(2)}) copy-start(f32[1024,4,48]{0,2,1:T(8,128)} %copy.40) | copy-start | bytes 2359300
  249.6 8.1 %copy-start.31 = (f32[1024,4]{0,1:T(4,128)S(1)}, f32[1024,4]{0,1:T(4,128)}, u32[]{:S(2)}) copy-start(f32[1024,4]{0,1:T(4,128)} %div.54) | copy-start | bytes 49156
  249.6 8.1 %copy-start.52 = (pred[1024,4]{0,1:T(4,128)(4,1)S(1)}, pred[1024,4]{0,1:T(4,128)(4,1)}, u32[]{:S(2)}) copy-start(pred[1024,4]{0,1:T(4,128)(4,1)} %broadcast_in_dim.382) | copy-start | bytes 12292
  257.7 8.1 %copy-start.14 = (f32[1024,4,48]{0,2,1:T(8,128)S(1)}, f32[1024,4,48]{0,2,1:T(8,128)}, u32[]{:S(2)}) copy-start(f32[1024,4,48]{0,2,1:T(8,128)} %copy.43) | copy-start | bytes 2359300
  257.7 8.1 %copy-start.18 = (f32[4,1024]{1,0:T(4,128)S(1)}, f32[4,1024]{1,0:T(4,128)}, u32[]{:S(2)}) copy-start(f32[4,1024]{1,0:T(4,128)} %copy-done.17) | copy-start | bytes 49156
  (27 other events, 72.9 us)
Sparse Core Ops, SparseCore 0:
  111.3 31.9 all-gather.1

commit v2 on v1

v2 whole, which is shorter than its diff:
```python
import functools

import jax
import jax.numpy as jnp
from jax import lax
from jax.experimental import pallas as pl
from jax.sharding import PartitionSpec as P

HEAD_COUNT = 16
DILATION_RATE = 8


big_negative = -1e30
norm_epsilon = 1e-05


def normalize(features, gain):
    wide = features.astype(jnp.float32)
    average = jnp.mean(wide, axis=-1, keepdims=True)
    centered = wide - average
    spread = jnp.mean(centered * centered, axis=-1, keepdims=True)
    return (centered * lax.rsqrt(spread + norm_epsilon) * gain).astype(jnp.bfloat16)


def nearby_kernel(q_ref, kt_ref, v_ref, bias_ref, o_ref, *, groups, group_rows, scale):
    offset = pl.program_id(0) % DILATION_RATE
    keys = kt_ref[0]
    values = v_ref[0]
    bias = bias_ref[...]
    for group in range(groups):

        @pl.when(group != offset)
        def _():
            rows = pl.ds(group * group_rows, group_rows)
            scores = jnp.dot(q_ref[0, rows, :], keys, preferred_element_type=jnp.float32)
            scores = scores * scale + bias
            top = jnp.max(scores, axis=1, keepdims=True)
            weights = jnp.exp(scores - top)
            total = jnp.sum(weights, axis=1, keepdims=True)
            summed = jnp.dot(
                weights.astype(jnp.bfloat16), values, preferred_element_type=jnp.float32
            )
            o_ref[0, rows, :] = (summed / total).astype(o_ref.dtype)


def dilated_kernel(
    q_ref, kt_ref, v_ref, bias_ref, fk_ref, fv_ref, fbias_ref, prev_ref, o_ref, *, scale
):
    del prev_ref
    queries = q_ref[0]
    near = jnp.dot(queries, kt_ref[0], preferred_element_type=jnp.float32)
    near = near * scale + bias_ref[...]
    far = jnp.dot(queries, fk_ref[0, 0], preferred_element_type=jnp.float32)
    far = far * scale + fbias_ref[0]
    top = jnp.maximum(
        jnp.max(near, axis=1, keepdims=True), jnp.max(far, axis=1, keepdims=True)
    )
    near_w = jnp.exp(near - top)
    far_w = jnp.exp(far - top)
    total = jnp.sum(near_w, axis=1, keepdims=True) + jnp.sum(far_w, axis=1, keepdims=True)
    summed = jnp.dot(near_w.astype(jnp.bfloat16), v_ref[0], preferred_element_type=jnp.float32)
    summed = summed + lax.dot_general(
        far_w.astype(jnp.bfloat16),
        fv_ref[0, 0],
        (((1,), (1,)), ((), ())),
        preferred_element_type=jnp.float32,
    )
    o_ref[0] = (summed / total).astype(o_ref.dtype)


def body(embeddings, slot, lengths, in_weight, norm_gain, qkv_weight, out_weight):
    seq_count = lax.axis_size("seq")
    device_count = lax.axis_size("tile") * seq_count
    rows = embeddings.shape[0]
    block_rows = rows // device_count
    width = in_weight.shape[1]
    head_size = width // HEAD_COUNT
    group_rows = rows // DILATION_RATE
    far_count = group_rows * seq_count
    scale = head_size ** (-0.5)
    my_index = lax.axis_index("tile") * seq_count + lax.axis_index("seq")

    projected = jnp.dot(embeddings, in_weight, preferred_element_type=jnp.float32).astype(
        jnp.bfloat16
    )
    arrived = lax.all_to_all(
        projected.reshape(device_count, block_rows, width),
        ("tile", "seq"),
        split_axis=0,
        concat_axis=0,
        tiled=True,
    ).reshape(rows, width)
    arrived_slot = lax.all_to_all(
        slot.reshape(device_count, block_rows), ("tile", "seq"), split_axis=0, concat_axis=0, tiled=True
    ).reshape(rows)
    local_slot = arrived_slot - my_index * rows
    stored_slot = (local_slot % DILATION_RATE) * group_rows + local_slot // DILATION_RATE
    placement = (
        stored_slot[None, :] == jnp.arange(rows, dtype=jnp.int32)[:, None]
    ).astype(jnp.bfloat16)
    features = jnp.dot(placement, arrived, preferred_element_type=jnp.float32).astype(
        jnp.bfloat16
    )

    slide_length = lengths[0]
    stored = jnp.arange(rows, dtype=jnp.int32)
    local_position = (stored % group_rows) * DILATION_RATE + stored // group_rows
    position_ok = lax.axis_index("seq") * rows + local_position < slide_length
    near_bias = jnp.where(position_ok, 0.0, big_negative).astype(jnp.float32).reshape(1, rows)

    normed = normalize(features, norm_gain)
    projections = jnp.dot(normed, qkv_weight, preferred_element_type=jnp.float32).astype(
        jnp.bfloat16
    )
    split = projections.reshape(rows, 3, HEAD_COUNT, head_size)
    queries = split[:, 0].transpose(1, 0, 2)
    keys_t = split[:, 1].transpose(1, 2, 0)
    values = split[:, 2].transpose(1, 0, 2)

    offsets = [head % DILATION_RATE for head in range(HEAD_COUNT)]
    own_far = jnp.stack(
        [
            jnp.stack(
                [keys_t[h, :, o * group_rows : (o + 1) * group_rows] for h, o in enumerate(offsets)]
            ),
            jnp.stack(
                [
                    values[h, o * group_rows : (o + 1) * group_rows, :].T
                    for h, o in enumerate(offsets)
                ]
            ),
        ]
    )
    far = lax.all_gather(own_far, "seq", axis=3, tiled=True)
    far_position = (
        jnp.arange(far_count, dtype=jnp.int32)[None, :] * DILATION_RATE
        + jnp.asarray(offsets, jnp.int32)[:, None]
    )
    far_bias = (
        jnp.where(far_position < slide_length, 0.0, big_negative)
        .astype(jnp.float32)
        .reshape(HEAD_COUNT, 1, far_count)
    )

    head_block = pl.BlockSpec((1, rows, head_size), lambda h: (h, 0, 0))
    keys_block = pl.BlockSpec((1, head_size, rows), lambda h: (h, 0, 0))
    bias_block = pl.BlockSpec((1, rows), lambda h: (0, 0))
    nearby = pl.pallas_call(
        functools.partial(
            nearby_kernel, groups=DILATION_RATE, group_rows=group_rows, scale=scale
        ),
        grid=(HEAD_COUNT,),
        in_specs=[head_block, keys_block, head_block, bias_block],
        out_specs=head_block,
        out_shape=jax.ShapeDtypeStruct((HEAD_COUNT, rows, head_size), jnp.bfloat16),
    )(queries, keys_t, values, near_bias)

    group_block = pl.BlockSpec((1, group_rows, head_size), lambda h: (h, h % DILATION_RATE, 0))
    attended = pl.pallas_call(
        functools.partial(dilated_kernel, scale=scale),
        grid=(HEAD_COUNT,),
        in_specs=[
            group_block,
            keys_block,
            head_block,
            bias_block,
            pl.BlockSpec((1, 1, head_size, far_count), lambda h: (0, h, 0, 0)),
            pl.BlockSpec((1, 1, head_size, far_count), lambda h: (1, h, 0, 0)),
            pl.BlockSpec((1, 1, far_count), lambda h: (h, 0, 0)),
            pl.BlockSpec(memory_space=pl.ANY),
        ],
        out_specs=group_block,
        out_shape=jax.ShapeDtypeStruct((HEAD_COUNT, rows, head_size), jnp.bfloat16),
        input_output_aliases={7: 0},
    )(queries, keys_t, values, near_bias, far, far, far_bias, nearby)

    output = jnp.einsum(
        "hnd,hde->ne",
        attended,
        out_weight.reshape(HEAD_COUNT, head_size, width),
        preferred_element_type=jnp.float32,
    ) + features.astype(jnp.float32)
    output = jnp.where(position_ok[:, None], output, 0.0).astype(jnp.bfloat16)
    output = output.reshape(DILATION_RATE, group_rows, width).transpose(1, 0, 2)
    return output.reshape(1, rows, width)


def solution(mesh):
    return jax.shard_map(
        body,
        mesh=mesh,
        in_specs=(P(("tile", "seq"), None), P(("tile", "seq")), P("tile"), P(), P(), P(), P()),
        out_specs=P("tile", "seq", None),
        check_vma=False,
    )
```

time: 291 us -> 190 us (0.65); the launches traced: 286 us -> 189 us
  matrix products: 106 us -> 20.8 us
  Pallas kernels: 0 us -> 74.3 us
  local copies, waits for them, and re-layouts: 84.4 us -> 26.9 us
  other arithmetic: 30.6 us -> 4.24 us
    dot_general x17 -> x2, matrix products: 95.2 us -> 8.57 us  [the longest x1 5.14 us: body(): jnp.einsum('hnd,hde->ne', attended, out_weight.reshape(HEAD_COUNT, head_s...]
    pallas_call x0 -> x2, Pallas kernels: none -> 74.3 us  [the longest x1 58.5 us: body(): pl.pallas_call(functools.partial(nearby_kernel, groups=DILATION_RATE, gro...]
    another operation x6 -> x1, local copies, waits for them, and re-layouts: 37.5 us -> 0.02 us  [body(): jnp.stack([keys_t[h, :, o * group_rows:(o + 1) * group_rows] for h, o in...]
    reduce_sum x6 -> x0, other arithmetic: 25.3 us -> none  [the longest x1 18.9 us: body(): nearby_total = jnp.sum(local_weights, axis=-1)]
    transpose x6 -> x4, local copies, waits for them, and re-layouts: 0.51 us -> 15.5 us  [the longest x2 8.82 us: body(): values = split[:, 2].transpose(1, 0, 2)]
    broadcast_in_dim x32 -> x0, local copies, waits for them, and re-layouts: 14.1 us -> none  [the longest x16 8.75 us: body(): jnp.where(group_mask.T[None, :, :, None], distant_accumulator[:, None, :,...]
    slice x5 -> x0, local copies, waits for them, and re-layouts: 9.61 us -> none  [the longest x2 4.08 us: body(): projections[:, model_width:2 * model_width]]
    scatter x1 -> x0, local copies, waits for them, and re-layouts: 7.02 us -> none  [body(): jnp.zeros((sequence_rows, model_width), jnp.bfloat16).at[local_slot]]
  transfers between devices with their start and end apart: 3 -> 3, of which waited for: 2 -> 2; matrix products, arithmetic and copies ran while one was open for 21% -> 10% of each run, Pallas kernels for 0% -> 31%
where the time goes in v2:
time: 190 us; the launch traced here: 189 us
  Pallas kernels  74.3 us (39%)
  waiting for transfers between devices  36.4 us (19%)
  local copies, waits for them, and re-layouts  26.9 us (14%)
  matrix products  20.8 us (11%)
  between operations  14.3 us (8%)
  starting transfers between devices  12.5 us (7%)
  other arithmetic  4.24 us (2%)
    pallas_call x1, Pallas kernels, body(): pl.pallas_call(functools.partial(nearby_kernel, groups=DILATION_RATE, gro...  58.5 us
    all_to_all x1, waiting for transfers between devices, body(): lax.all_to_all(projected.reshape(device_count, block_rows, width), ('tile...  35.6 us
    pallas_call x1, Pallas kernels, body(): pl.pallas_call(functools.partial(dilated_kernel, scale=scale), grid=(HEAD...  15.8 us
    transpose x2, local copies, waits for them, and re-layouts, body(): values = split[:, 2].transpose(1, 0, 2)  8.82 us
    all_to_all x1, starting transfers between devices, body(): lax.all_to_all(slot.reshape(device_count, block_rows), ('tile', 'seq'), s...  7.3 us
    convert_element_type x1, local copies, waits for them, and re-layouts, body(): jnp.dot(normed, qkv_weight, preferred_element_type=jnp.float32)  6.64 us
    dot_general x1, matrix products, body(): jnp.dot(embeddings, in_weight, preferred_element_type=jnp.float32)  6.36 us
    dot_general x1, matrix products, body(): jnp.dot(normed, qkv_weight, preferred_element_type=jnp.float32)  5.86 us
  transfers between devices with their start and end apart: 3, of which 2 were waited for; matrix products, arithmetic and copies ran while one was open for 10% of the time, Pallas kernels for 31%

profile of v2, /device:TPU:0, one launch (start us, length us, event | category | flops | bytes accessed | tf_op | source)
XLA Modules:
  0.0 189.4 jit_solution(7677420792908897283)
XLA Ops:
  6.5 1.5 all_to_all.9
  8.1 7.3 %all-to-all-start = ((s32[32,1,32]{2,1,0:T(1,128)}), s32[32,1,32]{2,1,0:T(1,128)S(1)}, u32[]{:S(2)}, u32[]{:S(2)}) async-start(s32[32,1,32]{2,1,0:T(1,128)} %all_to_all.9), calls=%async_computation | async-start | bytes 32768 | tf_op jit(solution)/shard_map/all_to_all | solution.py:93
  15.4 6.4 %convolution_convert_fusion.1 = bf16[1024,768]{1,0:T(8,128)(2,1)} fusion(bf16[1024,1536]{1,0:T(8,128)(2,1)} %param.8, bf16[1536,768]{1,0:T(8,128)(2,1)} %param.11), kind=kOutput, calls=%fused_computation.15 | convolution fusion | flops 2416705536 | bytes 7077888 | tf_op jit(solution)/shard_map/dot_general | solution.py:83
  21.7 0.8 all-to-all-done
  22.5 0.6 copy-done.4
  23.1 5.2 %all-to-all-start.1 = ((bf16[32,32,768]{2,1,0:T(8,128)(2,1)}), bf16[32,32,768]{2,1,0:T(8,128)(2,1)}, u32[]{:S(2)}, u32[]{:S(2)}) async-start(bf16[32,32,768]{2,1,0:T(8,128)(2,1)} %bitcast.165), calls=%async_computation.1 | async-start | bytes 3145728 | tf_op jit(solution)/shard_map/all_to_all | solution.py:86
  28.3 0.0 all-gather.2.cloned.1.call-start
  28.3 0.8 subtract_reduce_fusion
  29.1 0.7 sub.36
  29.8 0.7 fusion.27
  30.4 35.6 %all-to-all-done.1 = bf16[32,32,768]{2,1,0:T(8,128)(2,1)} async-done(((bf16[32,32,768]{2,1,0:T(8,128)(2,1)}), bf16[32,32,768]{2,1,0:T(8,128)(2,1)}, u32[]{:S(2)}, u32[]{:S(2)}) %all-to-all-start.1) | async-done | bytes 1572896 | tf_op jit(solution)/shard_map/all_to_all | solution.py:86
  66.0 3.4 %convert_reduce_fusion = (f32[1024]{0:T(1024)S(1)}, bf16[1024,768]{1,0:T(8,128)(2,1)S(1)}) fusion(bf16[1024,768]{1,0:T(8,128)(2,1)} %bitcast.2, s32[1024]{0:T(1024)S(1)} %fusion.27), kind=kOutput, calls=%fused_computation.3 | convolution fusion | flops 1614019584 | bytes 3153920 | tf_op jit(solution)/shard_map/dot_general | solution.py:101
  69.4 0.0 copy-start.3
  69.4 0.0 copy-start.6
  69.5 0.6 fusion.3
  70.1 0.5 copy-done.3
  70.6 0.0 copy-done
  70.6 5.9 %convolution_convert_fusion = bf16[1024,2304]{1,0:T(8,128)(2,1)} fusion(bf16[768,2304]{1,0:T(8,128)(2,1)S(1)} %copy-done, bf16[1024,768]{1,0:T(8,128)(2,1)S(1)} %get-tuple-element.9, f32[768]{0:T(1024)S(1)} %copy-done.6, f32[1024]{0:T(1024)S(1)} %add_rsqrt_fusion, f32[1024]{0:T(1024)S(1)} %broadcast_multiply_fusion), kind=kOutput, calls=%fused_computation | convolution fusion | flops 3630170112 | bytes 9841664 | tf_op jit(solution)/shard_map/dot_general | solution.py:112
  76.4 6.6 %copy.10 = bf16[1024,2304]{0,1:T(8,128)(2,1)} copy(bf16[1024,2304]{1,0:T(8,128)(2,1)} %convolution_convert_fusion) | data formatting | bytes 9437184 | tf_op jit(solution)/shard_map/convert_element_type | solution.py:112
  83.1 4.2 %slice_bitcast_fusion = (bf16[16,1024,48]{1,2,0:T(8,128)(2,1)S(1)}, bf16[16,48,1024]{2,1,0:T(8,128)(2,1)S(1)}, bf16[16,1024,48]{1,2,0:T(8,128)(2,1)}) fusion(bf16[1024,3,16,48]{0,3,2,1:T(8,128)(2,1)} %bitcast.164), kind=kLoop, calls=%fused_computation.16 | loop fusion | bytes 9437184 | tf_op jit(solution)/shard_map/transpose | solution.py:118
  87.8 0.6 copy-done.1
  88.4 0.5 copy-done.2
  88.9 0.8 pad_maximum_fusion
  89.7 0.0 all-gather.2.cloned.1.call-update
  90.4 0.6 compare_select_fusion.1.bias_ref
  91.0 0.8 compare_select_fusion.fbias_ref
  91.7 4.7 %copy.14.v_ref = bf16[16,1024,48]{2,1,0:T(8,128)(2,1)} copy(bf16[16,1024,48]{1,2,0:T(8,128)(2,1)} %copy-done.2) | data formatting | bytes 3145728 | tf_op jit(solution)/shard_map/transpose | solution.py:118
  96.4 4.7 %copy.13.q_ref = bf16[16,1024,48]{2,1,0:T(8,128)(2,1)} copy(bf16[16,1024,48]{1,2,0:T(8,128)(2,1)} %get-tuple-element.7) | data formatting | bytes 3145728 | tf_op jit(solution)/shard_map/transpose | solution.py:116
  101.1 58.5 %shard_map.82.prev_ref = bf16[16,1024,48]{2,1,0:T(8,128)(2,1)} custom-call(bf16[16,1024,48]{2,1,0:T(8,128)(2,1)} %copy.13.q_ref, bf16[16,48,1024]{2,1,0:T(8,128)(2,1)} %copy-done.1, bf16[16,1024,48]{2,1,0:T(8,128)(2,1)} %copy.14.v_ref, f32[1,1024]{1,0:T(1,128)} %compare_select_fusion.1.bias_ref), custom_call_target="tpu_custom_call" | custom-call | tf_op jit(solution)/shard_map/pallas_call | solution.py:148
  159.6 15.8 %shard_map.83 = bf16[16,1024,48]{2,1,0:T(8,128)(2,1)} custom-call(bf16[16,1024,48]{2,1,0:T(8,128)(2,1)} %copy.13.q_ref, bf16[16,48,1024]{2,1,0:T(8,128)(2,1)} %copy-done.1, bf16[16,1024,48]{2,1,0:T(8,128)(2,1)} %copy.14.v_ref, f32[1,1024]{1,0:T(1,128)} %compare_select_fusion.1.bias_ref, ...), custom_call_target="tpu_custom_call", output_to_operand_aliasing={{}: (7, {})} | custom-call | tf_op jit(solution)/shard_map/pallas_call | solution.py:159
  175.4 5.1 %fusion.7 = bf16[1024,768]{1,0:T(8,128)(2,1)S(1)} fusion(bf16[1024,768]{1,0:T(8,128)(2,1)} %copy-done.3, bf16[16,1024,48]{2,1,0:T(8,128)(2,1)} %shard_map.83, bf16[16,48,768]{2,1,0:T(8,128)(2,1)} %bitcast.169, pred[1024]{0:T(1024)(128)(4,1)S(1)} %fusion.25), kind=kOutput, calls=%fused_computation.12 | convolution fusion | flops 1211105280 | bytes 5899264 | tf_op jit(solution)/shard_map/hnd,hde->ne/dot_general | solution.py:177
  180.5 2.0 %copy.19 = bf16[128,8,768]{2,1,0:T(8,128)(2,1)} copy(bf16[128,8,768]{2,0,1:T(8,128)(2,1)S(1)} %bitcast.166) | data formatting | bytes 3145728 | tf_op jit(solution)/shard_map/transpose | solution.py:184
  (43 shorter events, 0.4 us)
Async XLA Ops:
  6.5 64.1 %copy-start = (bf16[768,2304]{1,0:T(8,128)(2,1)S(1)}, bf16[768,2304]{1,0:T(8,128)(2,1)}, u32[]{:S(2)}) copy-start(bf16[768,2304]{1,0:T(8,128)(2,1)} %param.13) | copy-start | bytes 10616836
  8.1 14.4 %all-to-all-start = ((s32[32,1,32]{2,1,0:T(1,128)}), s32[32,1,32]{2,1,0:T(1,128)S(1)}, u32[]{:S(2)}, u32[]{:S(2)}) async-start(s32[32,1,32]{2,1,0:T(1,128)} %all_to_all.9), calls=%async_computation | async-start | bytes 32768 | tf_op jit(solution)/shard_map/all_to_all | solution.py:93
  22.5 0.6 copy-start.4
  23.1 42.9 %all-to-all-start.1 = ((bf16[32,32,768]{2,1,0:T(8,128)(2,1)}), bf16[32,32,768]{2,1,0:T(8,128)(2,1)}, u32[]{:S(2)}, u32[]{:S(2)}) async-start(bf16[32,32,768]{2,1,0:T(8,128)(2,1)} %bitcast.165), calls=%async_computation.1 | async-start | bytes 3145728 | tf_op jit(solution)/shard_map/all_to_all | solution.py:86
  28.3 131.3 %all-gather.2.cloned.1.call-start = ((), (), s32[]{:S(2)}) async-start(), calls=%async_computation.2 | async-start | bytes 3538944 | tf_op jit(solution)/shard_map/all_gather | solution.py:134
  69.4 1.1 copy-start.3
  69.4 1.1 copy-start.6
  87.3 1.1 copy-start.1
  87.3 1.6 copy-start.2
  87.3 3.7 %copy-start.5 = (s32[16]{0:T(128)S(1)}, s32[16]{0:T(128)}, u32[]{:S(2)}) copy-start(s32[16]{0:T(128)} %constant.80.clone) | copy-start | bytes 196
Sparse Core Ops, SparseCore 0:
  89.8 32.0 all-gather.1

commit v3 on v2

--- a/solution.py
+++ b/solution.py
@@ -22,20 +22,20 @@
     return (centered * lax.rsqrt(spread + norm_epsilon) * gain).astype(jnp.bfloat16)
 
 
-def nearby_kernel(q_ref, kt_ref, v_ref, bias_ref, o_ref, *, groups, group_rows, scale):
+def nearby_kernel(qt_ref, kt_ref, vt_ref, bias_ref, o_ref, *, groups, group_rows, factor):
     offset = pl.program_id(0) % DILATION_RATE
-    keys = kt_ref[0]
-    values = v_ref[0]
+    keys = kt_ref[...]
+    values = vt_ref[...].T
     bias = bias_ref[...]
     for group in range(groups):
 
         @pl.when(group != offset)
         def _():
             rows = pl.ds(group * group_rows, group_rows)
-            scores = jnp.dot(q_ref[0, rows, :], keys, preferred_element_type=jnp.float32)
-            scores = scores * scale + bias
+            queries = qt_ref[:, rows].T
+            scores = jnp.dot(queries, keys, preferred_element_type=jnp.float32) + bias
             top = jnp.max(scores, axis=1, keepdims=True)
-            weights = jnp.exp(scores - top)
+            weights = jnp.exp2((scores - top) * factor)
             total = jnp.sum(weights, axis=1, keepdims=True)
             summed = jnp.dot(
                 weights.astype(jnp.bfloat16), values, preferred_element_type=jnp.float32
@@ -44,26 +44,23 @@
 
 
 def dilated_kernel(
-    q_ref, kt_ref, v_ref, bias_ref, fk_ref, fv_ref, fbias_ref, prev_ref, o_ref, *, scale
+    qt_ref, kt_ref, vt_ref, bias_ref, fk_ref, fv_ref, fbias_ref, prev_ref, o_ref, *, factor
 ):
     del prev_ref
-    queries = q_ref[0]
-    near = jnp.dot(queries, kt_ref[0], preferred_element_type=jnp.float32)
-    near = near * scale + bias_ref[...]
-    far = jnp.dot(queries, fk_ref[0, 0], preferred_element_type=jnp.float32)
-    far = far * scale + fbias_ref[0]
+    queries = qt_ref[...].T
+    near = jnp.dot(queries, kt_ref[...], preferred_element_type=jnp.float32) + bias_ref[...]
+    far = jnp.dot(queries, fk_ref[0, 0], preferred_element_type=jnp.float32) + fbias_ref[0]
     top = jnp.maximum(
         jnp.max(near, axis=1, keepdims=True), jnp.max(far, axis=1, keepdims=True)
     )
-    near_w = jnp.exp(near - top)
-    far_w = jnp.exp(far - top)
+    near_w = jnp.exp2((near - top) * factor)
+    far_w = jnp.exp2((far - top) * factor)
     total = jnp.sum(near_w, axis=1, keepdims=True) + jnp.sum(far_w, axis=1, keepdims=True)
-    summed = jnp.dot(near_w.astype(jnp.bfloat16), v_ref[0], preferred_element_type=jnp.float32)
-    summed = summed + lax.dot_general(
-        far_w.astype(jnp.bfloat16),
-        fv_ref[0, 0],
-        (((1,), (1,)), ((), ())),
-        preferred_element_type=jnp.float32,
+    summed = jnp.dot(
+        near_w.astype(jnp.bfloat16), vt_ref[...].T, preferred_element_type=jnp.float32
+    )
+    summed = summed + jnp.dot(
+        far_w.astype(jnp.bfloat16), fv_ref[0, 0].T, preferred_element_type=jnp.float32
     )
     o_ref[0] = (summed / total).astype(o_ref.dtype)
 
@@ -109,26 +106,23 @@
     near_bias = jnp.where(position_ok, 0.0, big_negative).astype(jnp.float32).reshape(1, rows)
 
     normed = normalize(features, norm_gain)
-    projections = jnp.dot(normed, qkv_weight, preferred_element_type=jnp.float32).astype(
-        jnp.bfloat16
-    )
-    split = projections.reshape(rows, 3, HEAD_COUNT, head_size)
-    queries = split[:, 0].transpose(1, 0, 2)
-    keys_t = split[:, 1].transpose(1, 2, 0)
-    values = split[:, 2].transpose(1, 0, 2)
+    projected_t = lax.dot_general(
+        qkv_weight, normed, (((0,), (1,)), ((), ())), preferred_element_type=jnp.float32
+    ).astype(jnp.bfloat16)
 
     offsets = [head % DILATION_RATE for head in range(HEAD_COUNT)]
     own_far = jnp.stack(
         [
             jnp.stack(
-                [keys_t[h, :, o * group_rows : (o + 1) * group_rows] for h, o in enumerate(offsets)]
-            ),
-            jnp.stack(
                 [
-                    values[h, o * group_rows : (o + 1) * group_rows, :].T
+                    projected_t[
+                        (part * HEAD_COUNT + h) * head_size : (part * HEAD_COUNT + h + 1) * head_size,
+                        o * group_rows : (o + 1) * group_rows,
+                    ]
                     for h, o in enumerate(offsets)
                 ]
-            ),
+            )
+            for part in (1, 2)
         ]
     )
     far = lax.all_gather(own_far, "seq", axis=3, tiled=True)
@@ -143,26 +137,29 @@
     )
 
     head_block = pl.BlockSpec((1, rows, head_size), lambda h: (h, 0, 0))
-    keys_block = pl.BlockSpec((1, head_size, rows), lambda h: (h, 0, 0))
+    query_block = pl.BlockSpec((head_size, rows), lambda h: (h, 0))
+    keys_block = pl.BlockSpec((head_size, rows), lambda h: (HEAD_COUNT + h, 0))
+    values_block = pl.BlockSpec((head_size, rows), lambda h: (2 * HEAD_COUNT + h, 0))
     bias_block = pl.BlockSpec((1, rows), lambda h: (0, 0))
+    factor = scale * 1.4426950408889634
     nearby = pl.pallas_call(
         functools.partial(
-            nearby_kernel, groups=DILATION_RATE, group_rows=group_rows, scale=scale
+            nearby_kernel, groups=DILATION_RATE, group_rows=group_rows, factor=factor
         ),
         grid=(HEAD_COUNT,),
-        in_specs=[head_block, keys_block, head_block, bias_block],
+        in_specs=[query_block, keys_block, values_block, bias_block],
         out_specs=head_block,
         out_shape=jax.ShapeDtypeStruct((HEAD_COUNT, rows, head_size), jnp.bfloat16),
-    )(queries, keys_t, values, near_bias)
+    )(projected_t, projected_t, projected_t, near_bias)
 
     group_block = pl.BlockSpec((1, group_rows, head_size), lambda h: (h, h % DILATION_RATE, 0))
     attended = pl.pallas_call(
-        functools.partial(dilated_kernel, scale=scale),
+        functools.partial(dilated_kernel, factor=factor),
         grid=(HEAD_COUNT,),
         in_specs=[
-            group_block,
+            pl.BlockSpec((head_size, group_rows), lambda h: (h, h % DILATION_RATE)),
             keys_block,
-            head_block,
+            values_block,
             bias_block,
             pl.BlockSpec((1, 1, head_size, far_count), lambda h: (0, h, 0, 0)),
             pl.BlockSpec((1, 1, head_size, far_count), lambda h: (1, h, 0, 0)),
@@ -172,7 +169,7 @@
         out_specs=group_block,
         out_shape=jax.ShapeDtypeStruct((HEAD_COUNT, rows, head_size), jnp.bfloat16),
         input_output_aliases={7: 0},
-    )(queries, keys_t, values, near_bias, far, far, far_bias, nearby)
+    )(projected_t, projected_t, projected_t, near_bias, far, far, far_bias, nearby)
 
     output = jnp.einsum(
         "hnd,hde->ne",

time: 190 us -> 181 us (0.953)
  local copies, waits for them, and re-layouts: 26.9 us -> 6.29 us
  Pallas kernels: 74.3 us -> 87.2 us
    transpose x3 -> x0, local copies, waits for them, and re-layouts: 13.5 us -> none  [the longest x2 8.82 us: body(): values = split[:, 2].transpose(1, 0, 2)]
    pallas_call x1, Pallas kernels: 58.5 us -> 69.6 us  [body(): pl.pallas_call(functools.partial(nearby_kernel, groups=DILATION_RATE, gro...]
    convert_element_type x1 -> x0, local copies, waits for them, and re-layouts: 6.64 us -> none  [body(): jnp.dot(normed, qkv_weight, preferred_element_type=jnp.float32)]
  transfers between devices with their start and end apart: 3 -> 3, of which waited for: 2 -> 2; matrix products, arithmetic and copies ran while one was open for 10% -> 5% of each run, Pallas kernels for 31% -> 39%
where the time goes in v3:
time: 181 us; the launch traced here: 180 us
  Pallas kernels  87.2 us (48%)
  waiting for transfers between devices  36.2 us (20%)
  matrix products  19.6 us (11%)
  between operations  14.2 us (8%)
  starting transfers between devices  12.7 us (7%)
  local copies, waits for them, and re-layouts  6.29 us (3%)
  other arithmetic  4.22 us (2%)
    pallas_call x1, Pallas kernels, body(): pl.pallas_call(functools.partial(nearby_kernel, groups=DILATION_RATE, gro...  69.6 us
    all_to_all x1, waiting for transfers between devices, body(): lax.all_to_all(projected.reshape(device_count, block_rows, width), ('tile...  35.4 us
    pallas_call x1, Pallas kernels, body(): pl.pallas_call(functools.partial(dilated_kernel, factor=factor), grid=(HE...  17.6 us
    all_to_all x1, starting transfers between devices, body(): lax.all_to_all(slot.reshape(device_count, block_rows), ('tile', 'seq'), s...  7.3 us
    dot_general x1, matrix products, body(): jnp.dot(embeddings, in_weight, preferred_element_type=jnp.float32)  6.36 us
    all_to_all x1, starting transfers between devices, body(): lax.all_to_all(projected.reshape(device_count, block_rows, width), ('tile...  5.16 us
    dot_general x1, matrix products, body(): jnp.einsum('hnd,hde->ne', attended, out_weight.reshape(HEAD_COUNT, head_s...  5.14 us
    dot_general x1, matrix products, body(): lax.dot_general(qkv_weight, normed, (((0,), (1,)), ((), ())), preferred_e...  4.64 us
  transfers between devices with their start and end apart: 3, of which 2 were waited for; matrix products, arithmetic and copies ran while one was open for 5% of the time, Pallas kernels for 39%

profile of v3, /device:TPU:0, one launch (start us, length us, event | category | flops | bytes accessed | tf_op | source)
XLA Modules:
  0.0 180.4 jit_solution(14749552440561826102)
XLA Ops:
  6.5 0.0 copy-start
  6.5 1.5 all_to_all.9
  8.1 7.3 %all-to-all-start = ((s32[32,1,32]{2,1,0:T(1,128)}), s32[32,1,32]{2,1,0:T(1,128)S(1)}, u32[]{:S(2)}, u32[]{:S(2)}) async-start(s32[32,1,32]{2,1,0:T(1,128)} %all_to_all.9), calls=%async_computation | async-start | bytes 32768 | tf_op jit(solution)/shard_map/all_to_all | solution.py:90
  15.4 6.4 %convolution_convert_fusion.1 = bf16[1024,768]{1,0:T(8,128)(2,1)} fusion(bf16[1024,1536]{1,0:T(8,128)(2,1)} %param.8, bf16[1536,768]{1,0:T(8,128)(2,1)} %param.11), kind=kOutput, calls=%fused_computation.16 | convolution fusion | flops 2416705536 | bytes 7077888 | tf_op jit(solution)/shard_map/dot_general | solution.py:80
  21.7 0.8 all-to-all-done
  22.5 0.0 copy-start.3
  22.5 5.2 %all-to-all-start.1 = ((bf16[32,32,768]{2,1,0:T(8,128)(2,1)}), bf16[32,32,768]{2,1,0:T(8,128)(2,1)}, u32[]{:S(2)}, u32[]{:S(2)}) async-start(bf16[32,32,768]{2,1,0:T(8,128)(2,1)} %bitcast.153), calls=%async_computation.1 | async-start | bytes 3145728 | tf_op jit(solution)/shard_map/all_to_all | solution.py:83
  27.7 0.2 all-gather.2.cloned.1.call-start
  27.9 0.0 copy-done.3
  27.9 0.8 subtract_reduce_fusion
  28.7 0.7 sub.36
  29.4 0.7 fusion.28
  30.0 35.4 %all-to-all-done.1 = bf16[32,32,768]{2,1,0:T(8,128)(2,1)} async-done(((bf16[32,32,768]{2,1,0:T(8,128)(2,1)}), bf16[32,32,768]{2,1,0:T(8,128)(2,1)}, u32[]{:S(2)}, u32[]{:S(2)}) %all-to-all-start.1) | async-done | bytes 1572896 | tf_op jit(solution)/shard_map/all_to_all | solution.py:83
  65.4 3.4 %convert_reduce_fusion = (f32[1024]{0:T(1024)S(1)}, bf16[1024,768]{1,0:T(8,128)(2,1)S(1)}) fusion(bf16[1024,768]{1,0:T(8,128)(2,1)} %bitcast.2, s32[1024]{0:T(1024)S(1)} %fusion.28), kind=kOutput, calls=%fused_computation.4 | convolution fusion | flops 1614019584 | bytes 3153920 | tf_op jit(solution)/shard_map/dot_general | solution.py:98
  68.9 0.0 copy-start.2
  68.9 0.6 fusion.4
  69.5 0.0 copy-done
  69.5 0.0 copy-done.5
  69.5 0.0 copy-start.4
  69.5 4.6 %fusion.qt_ref.kt_ref.vt_ref = bf16[2304,1024]{1,0:T(8,128)(2,1)S(1)} fusion(bf16[768,2304]{1,0:T(8,128)(2,1)S(1)} %copy-done, bf16[1024,768]{1,0:T(8,128)(2,1)S(1)} %get-tuple-element.38, f32[768]{0:T(1024)S(1)} %copy-done.5, f32[1024]{0:T(1024)S(1)} %add_rsqrt_fusion, f32[1024]{0:T(1024)S(1)} %broadcast_multiply_fusion), kind=kOutput, calls=%fused_computation.1 | convolution fusion | flops 3630170112 | bytes 9841664 | tf_op jit(solution)/shard_map/dot_general | solution.py:109
  74.2 0.0 copy-done.2
  74.2 0.0 copy-start.1
  74.5 1.8 copy-done.1
  76.3 0.8 pad_maximum_fusion
  77.1 0.0 all-gather.2.cloned.1.call-update
  77.8 0.6 compare_select_fusion.1.bias_ref
  78.4 0.0 copy-done.4
  78.4 0.7 compare_select_fusion.fbias_ref
  79.2 69.6 %shard_map.82.prev_ref = bf16[16,1024,48]{2,1,0:T(8,128)(2,1)} custom-call(bf16[2304,1024]{1,0:T(8,128)(2,1)} %copy-done.1, bf16[2304,1024]{1,0:T(8,128)(2,1)} %copy-done.1, bf16[2304,1024]{1,0:T(8,128)(2,1)} %copy-done.1, f32[1,1024]{1,0:T(1,128)} %compare_select_fusion.1.bias_ref), custom_call_target="tpu_custom_call" | custom-call | tf_op jit(solution)/shard_map/pallas_call | solution.py:145
  148.8 17.6 %shard_map.83 = bf16[16,1024,48]{2,1,0:T(8,128)(2,1)} custom-call(bf16[2304,1024]{1,0:T(8,128)(2,1)} %copy-done.1, bf16[2304,1024]{1,0:T(8,128)(2,1)} %copy-done.1, bf16[2304,1024]{1,0:T(8,128)(2,1)} %copy-done.1, f32[1,1024]{1,0:T(1,128)} %compare_select_fusion.1.bias_ref, ...), custom_call_target="tpu_custom_call", output_to_operand_aliasing={{}: (7, {})} | custom-call | tf_op jit(solution)/shard_map/pallas_call | solution.py:156
  166.4 5.1 %fusion.8 = bf16[1024,768]{1,0:T(8,128)(2,1)S(1)} fusion(bf16[1024,768]{1,0:T(8,128)(2,1)} %copy-done.2, bf16[16,1024,48]{2,1,0:T(8,128)(2,1)} %shard_map.83, bf16[16,48,768]{2,1,0:T(8,128)(2,1)} %bitcast.157, pred[1024]{0:T(1024)(128)(4,1)S(1)} %fusion.26), kind=kOutput, calls=%fused_computation.13 | convolution fusion | flops 1211105280 | bytes 5899264 | tf_op jit(solution)/shard_map/hnd,hde->ne/dot_general | solution.py:174
  171.5 2.0 %copy.16 = bf16[128,8,768]{2,1,0:T(8,128)(2,1)} copy(bf16[128,8,768]{2,0,1:T(8,128)(2,1)S(1)} %bitcast.154) | data formatting | bytes 3145728 | tf_op jit(solution)/shard_map/transpose | solution.py:181
  (22 shorter events, 0.3 us)
Async XLA Ops:
  6.5 63.0 %copy-start = (bf16[768,2304]{1,0:T(8,128)(2,1)S(1)}, bf16[768,2304]{1,0:T(8,128)(2,1)}, u32[]{:S(2)}) copy-start(bf16[768,2304]{1,0:T(8,128)(2,1)} %param.13) | copy-start | bytes 10616836
  8.1 14.5 %all-to-all-start = ((s32[32,1,32]{2,1,0:T(1,128)}), s32[32,1,32]{2,1,0:T(1,128)S(1)}, u32[]{:S(2)}, u32[]{:S(2)}) async-start(s32[32,1,32]{2,1,0:T(1,128)} %all_to_all.9), calls=%async_computation | async-start | bytes 32768 | tf_op jit(solution)/shard_map/all_to_all | solution.py:90
  22.5 5.4 %copy-start.3 = (s32[32,1,32]{2,1,0:T(1,128)}, s32[32,1,32]{2,1,0:T(1,128)S(1)}, u32[]{:S(2)}) copy-start(s32[32,1,32]{2,1,0:T(1,128)S(1)} %all-to-all-done) | copy-start | bytes 12292
  22.5 42.9 %all-to-all-start.1 = ((bf16[32,32,768]{2,1,0:T(8,128)(2,1)}), bf16[32,32,768]{2,1,0:T(8,128)(2,1)}, u32[]{:S(2)}, u32[]{:S(2)}) async-start(bf16[32,32,768]{2,1,0:T(8,128)(2,1)} %bitcast.153), calls=%async_computation.1 | async-start | bytes 3145728 | tf_op jit(solution)/shard_map/all_to_all | solution.py:83
  27.7 121.1 %all-gather.2.cloned.1.call-start = ((), (), s32[]{:S(2)}) async-start(), calls=%async_computation.2 | async-start | bytes 3538944 | tf_op jit(solution)/shard_map/all_gather | solution.py:128
  65.4 4.1 %copy-start.5 = (f32[768]{0:T(1024)S(1)}, f32[768]{0:T(1024)}, u32[]{:S(2)}) copy-start(f32[768]{0:T(1024)} %param.12) | copy-start | bytes 9220
  68.9 5.3 %copy-start.2 = (bf16[1024,768]{1,0:T(8,128)(2,1)}, bf16[1024,768]{1,0:T(8,128)(2,1)S(1)}, u32[]{:S(2)}) copy-start(bf16[1024,768]{1,0:T(8,128)(2,1)S(1)} %get-tuple-element.38) | copy-start | bytes 4718596
  69.5 8.9 %copy-start.4 = (s32[16]{0:T(128)S(1)}, s32[16]{0:T(128)}, u32[]{:S(2)}) copy-start(s32[16]{0:T(128)} %constant.80.clone) | copy-start | bytes 196
  74.2 2.1 %copy-start.1 = (bf16[2304,1024]{1,0:T(8,128)(2,1)}, bf16[2304,1024]{1,0:T(8,128)(2,1)S(1)}, u32[]{:S(2)}) copy-start(bf16[2304,1024]{1,0:T(8,128)(2,1)S(1)} %fusion.qt_ref.kt_ref.vt_ref) | copy-start | bytes 14155780
Sparse Core Ops, SparseCore 0:
  77.3 32.2 all-gather.1

commit v4 on v3

--- a/solution.py
+++ b/solution.py
@@ -22,47 +22,58 @@
     return (centered * lax.rsqrt(spread + norm_epsilon) * gain).astype(jnp.bfloat16)
 
 
+def extend(block, extra):
+    return jnp.concatenate([block, extra], axis=0)
+
+
+def ones_row(width):
+    row = lax.broadcasted_iota(jnp.int32, (16, width), 0)
+    return jnp.where(row == 0, 1.0, 0.0).astype(jnp.bfloat16)
+
+
 def nearby_kernel(qt_ref, kt_ref, vt_ref, bias_ref, o_ref, *, groups, group_rows, factor):
     offset = pl.program_id(0) % DILATION_RATE
-    keys = kt_ref[...]
-    values = vt_ref[...].T
-    bias = bias_ref[...]
+    keys = extend(kt_ref[...], bias_ref[...]).T
+    values_t = vt_ref[...]
+    ones = ones_row(group_rows)
     for group in range(groups):
 
         @pl.when(group != offset)
         def _():
             rows = pl.ds(group * group_rows, group_rows)
-            queries = qt_ref[:, rows].T
-            scores = jnp.dot(queries, keys, preferred_element_type=jnp.float32) + bias
-            top = jnp.max(scores, axis=1, keepdims=True)
-            weights = jnp.exp2((scores - top) * factor)
-            total = jnp.sum(weights, axis=1, keepdims=True)
-            summed = jnp.dot(
-                weights.astype(jnp.bfloat16), values, preferred_element_type=jnp.float32
+            queries_t = extend(qt_ref[:, rows], ones)
+            scores_t = jnp.dot(keys, queries_t, preferred_element_type=jnp.float32)
+            top = jnp.max(scores_t, axis=0, keepdims=True)
+            weights_t = jnp.exp2((scores_t - top) * factor)
+            total = jnp.sum(weights_t, axis=0, keepdims=True)
+            summed_t = jnp.dot(
+                values_t, weights_t.astype(jnp.bfloat16), preferred_element_type=jnp.float32
             )
-            o_ref[0, rows, :] = (summed / total).astype(o_ref.dtype)
+            o_ref[:, rows] = (summed_t / total).astype(o_ref.dtype)
 
 
 def dilated_kernel(
     qt_ref, kt_ref, vt_ref, bias_ref, fk_ref, fv_ref, fbias_ref, prev_ref, o_ref, *, factor
 ):
     del prev_ref
-    queries = qt_ref[...].T
-    near = jnp.dot(queries, kt_ref[...], preferred_element_type=jnp.float32) + bias_ref[...]
-    far = jnp.dot(queries, fk_ref[0, 0], preferred_element_type=jnp.float32) + fbias_ref[0]
+    queries_t = extend(qt_ref[...], ones_row(qt_ref.shape[1]))
+    near_keys = extend(kt_ref[...], bias_ref[...]).T
+    far_keys = extend(fk_ref[0, 0], fbias_ref[0]).T
+    near = jnp.dot(near_keys, queries_t, preferred_element_type=jnp.float32)
+    far = jnp.dot(far_keys, queries_t, preferred_element_type=jnp.float32)
     top = jnp.maximum(
-        jnp.max(near, axis=1, keepdims=True), jnp.max(far, axis=1, keepdims=True)
+        jnp.max(near, axis=0, keepdims=True), jnp.max(far, axis=0, keepdims=True)
     )
     near_w = jnp.exp2((near - top) * factor)
     far_w = jnp.exp2((far - top) * factor)
-    total = jnp.sum(near_w, axis=1, keepdims=True) + jnp.sum(far_w, axis=1, keepdims=True)
-    summed = jnp.dot(
-        near_w.astype(jnp.bfloat16), vt_ref[...].T, preferred_element_type=jnp.float32
-    )
-    summed = summed + jnp.dot(
-        far_w.astype(jnp.bfloat16), fv_ref[0, 0].T, preferred_element_type=jnp.float32
-    )
-    o_ref[0] = (summed / total).astype(o_ref.dtype)
+    total = jnp.sum(near_w, axis=0, keepdims=True) + jnp.sum(far_w, axis=0, keepdims=True)
+    summed_t = jnp.dot(
+        vt_ref[...], near_w.astype(jnp.bfloat16), preferred_element_type=jnp.float32
+    )
+    summed_t = summed_t + jnp.dot(
+        fv_ref[0, 0], far_w.astype(jnp.bfloat16), preferred_element_type=jnp.float32
+    )
+    o_ref[...] = (summed_t / total).astype(o_ref.dtype)
 
 
 def body(embeddings, slot, lengths, in_weight, norm_gain, qkv_weight, out_weight):
@@ -103,7 +114,10 @@
     stored = jnp.arange(rows, dtype=jnp.int32)
     local_position = (stored % group_rows) * DILATION_RATE + stored // group_rows
     position_ok = lax.axis_index("seq") * rows + local_position < slide_length
-    near_bias = jnp.where(position_ok, 0.0, big_negative).astype(jnp.float32).reshape(1, rows)
+    extra_row = lax.broadcasted_iota(jnp.int32, (16, 1), 0) == 0
+    near_bias = jnp.where(
+        extra_row & ~position_ok[None, :], big_negative, 0.0
+    ).astype(jnp.bfloat16)
 
     normed = normalize(features, norm_gain)
     projected_t = lax.dot_general(
@@ -130,17 +144,14 @@
         jnp.arange(far_count, dtype=jnp.int32)[None, :] * DILATION_RATE
         + jnp.asarray(offsets, jnp.int32)[:, None]
     )
-    far_bias = (
-        jnp.where(far_position < slide_length, 0.0, big_negative)
-        .astype(jnp.float32)
-        .reshape(HEAD_COUNT, 1, far_count)
-    )
-
-    head_block = pl.BlockSpec((1, rows, head_size), lambda h: (h, 0, 0))
+    far_bias = jnp.where(
+        extra_row[None] & (far_position >= slide_length)[:, None, :], big_negative, 0.0
+    ).astype(jnp.bfloat16)
+
     query_block = pl.BlockSpec((head_size, rows), lambda h: (h, 0))
     keys_block = pl.BlockSpec((head_size, rows), lambda h: (HEAD_COUNT + h, 0))
     values_block = pl.BlockSpec((head_size, rows), lambda h: (2 * HEAD_COUNT + h, 0))
-    bias_block = pl.BlockSpec((1, rows), lambda h: (0, 0))
+    bias_block = pl.BlockSpec((16, rows), lambda h: (0, 0))
     factor = scale * 1.4426950408889634
     nearby = pl.pallas_call(
         functools.partial(
@@ -148,34 +159,31 @@
         ),
         grid=(HEAD_COUNT,),
         in_specs=[query_block, keys_block, values_block, bias_block],
-        out_specs=head_block,
-        out_shape=jax.ShapeDtypeStruct((HEAD_COUNT, rows, head_size), jnp.bfloat16),
+        out_specs=query_block,
+        out_shape=jax.ShapeDtypeStruct((width, rows), jnp.bfloat16),
     )(projected_t, projected_t, projected_t, near_bias)
 
-    group_block = pl.BlockSpec((1, group_rows, head_size), lambda h: (h, h % DILATION_RATE, 0))
-    attended = pl.pallas_call(
+    group_block = pl.BlockSpec((head_size, group_rows), lambda h: (h, h % DILATION_RATE))
+    attended_t = pl.pallas_call(
         functools.partial(dilated_kernel, factor=factor),
         grid=(HEAD_COUNT,),
         in_specs=[
-            pl.BlockSpec((head_size, group_rows), lambda h: (h, h % DILATION_RATE)),
+            group_block,
             keys_block,
             values_block,
             bias_block,
             pl.BlockSpec((1, 1, head_size, far_count), lambda h: (0, h, 0, 0)),
             pl.BlockSpec((1, 1, head_size, far_count), lambda h: (1, h, 0, 0)),
-            pl.BlockSpec((1, 1, far_count), lambda h: (h, 0, 0)),
+            pl.BlockSpec((1, 16, far_count), lambda h: (h, 0, 0)),
             pl.BlockSpec(memory_space=pl.ANY),
         ],
         out_specs=group_block,
-        out_shape=jax.ShapeDtypeStruct((HEAD_COUNT, rows, head_size), jnp.bfloat16),
+        out_shape=jax.ShapeDtypeStruct((width, rows), jnp.bfloat16),
         input_output_aliases={7: 0},
     )(projected_t, projected_t, projected_t, near_bias, far, far, far_bias, nearby)
 
-    output = jnp.einsum(
-        "hnd,hde->ne",
-        attended,
-        out_weight.reshape(HEAD_COUNT, head_size, width),
-        preferred_element_type=jnp.float32,
+    output = lax.dot_general(
+        attended_t, out_weight, (((0,), (0,)), ((), ())), preferred_element_type=jnp.float32
     ) + features.astype(jnp.float32)
     output = jnp.where(position_ok[:, None], output, 0.0).astype(jnp.bfloat16)
     output = output.reshape(DILATION_RATE, group_rows, width).transpose(1, 0, 2)

time: 181 us -> 165 us (0.912)
  Pallas kernels: 87.2 us -> 72 us
    pallas_call x1, Pallas kernels: 69.6 us -> 56.8 us  [body(): pl.pallas_call(functools.partial(nearby_kernel, groups=DILATION_RATE, gro...]
    pallas_call x1, Pallas kernels: 17.6 us -> 15.2 us  [body(): pl.pallas_call(functools.partial(dilated_kernel, factor=factor), grid=(HE...]
  transfers between devices with their start and end apart: 3 -> 3, of which waited for: 2 -> 2; matrix products, arithmetic and copies ran while one was open for 5% -> 6% of each run, Pallas kernels for 39% -> 35%
where the time goes in v4:
time: 165 us; the launch traced here: 164 us
  Pallas kernels  72 us (44%)
  waiting for transfers between devices  36.1 us (22%)
  matrix products  18.2 us (11%)
  between operations  14.3 us (9%)
  starting transfers between devices  12.7 us (8%)
  local copies, waits for them, and re-layouts  6.31 us (4%)
  other arithmetic  4.69 us (3%)
    pallas_call x1, Pallas kernels, body(): pl.pallas_call(functools.partial(nearby_kernel, groups=DILATION_RATE, gro...  56.8 us
    all_to_all x1, waiting for transfers between devices, body(): lax.all_to_all(projected.reshape(device_count, block_rows, width), ('tile...  35.3 us
    pallas_call x1, Pallas kernels, body(): pl.pallas_call(functools.partial(dilated_kernel, factor=factor), grid=(HE...  15.2 us
    all_to_all x1, starting transfers between devices, body(): lax.all_to_all(slot.reshape(device_count, block_rows), ('tile', 'seq'), s...  7.3 us
    dot_general x1, matrix products, body(): jnp.dot(embeddings, in_weight, preferred_element_type=jnp.float32)  6.36 us
    all_to_all x1, starting transfers between devices, body(): lax.all_to_all(projected.reshape(device_count, block_rows, width), ('tile...  5.17 us
    dot_general x1, matrix products, body(): lax.dot_general(qkv_weight, normed, (((0,), (1,)), ((), ())), preferred_e...  4.64 us
    dot_general x1, matrix products, body(): lax.dot_general(attended_t, out_weight, (((0,), (0,)), ((), ())), preferr...  3.73 us
  transfers between devices with their start and end apart: 3, of which 2 were waited for; matrix products, arithmetic and copies ran while one was open for 6% of the time, Pallas kernels for 35%

profile of v4, /device:TPU:0, one launch (start us, length us, event | category | flops | bytes accessed | tf_op | source)
XLA Modules:
  0.0 164.3 jit_solution(4553923737133962419)
XLA Ops:
  6.5 0.0 copy-start
  6.5 1.5 all_to_all.9
  8.1 7.3 %all-to-all-start = ((s32[32,1,32]{2,1,0:T(1,128)}), s32[32,1,32]{2,1,0:T(1,128)S(1)}, u32[]{:S(2)}, u32[]{:S(2)}) async-start(s32[32,1,32]{2,1,0:T(1,128)} %all_to_all.9), calls=%async_computation | async-start | bytes 32768 | tf_op jit(solution)/shard_map/all_to_all | solution.py:101
  15.4 6.4 %convolution_convert_fusion.1 = bf16[1024,768]{1,0:T(8,128)(2,1)} fusion(bf16[1024,1536]{1,0:T(8,128)(2,1)} %param.8, bf16[1536,768]{1,0:T(8,128)(2,1)} %param.11), kind=kOutput, calls=%fused_computation.16 | convolution fusion | flops 2416705536 | bytes 7077888 | tf_op jit(solution)/shard_map/dot_general | solution.py:91
  21.7 0.8 all-to-all-done
  22.5 5.2 %all-to-all-start.1 = ((bf16[32,32,768]{2,1,0:T(8,128)(2,1)}), bf16[32,32,768]{2,1,0:T(8,128)(2,1)}, u32[]{:S(2)}, u32[]{:S(2)}) async-start(bf16[32,32,768]{2,1,0:T(8,128)(2,1)} %bitcast.149), calls=%async_computation.1 | async-start | bytes 3145728 | tf_op jit(solution)/shard_map/all_to_all | solution.py:94
  27.7 0.2 all-gather.2.cloned.1.call-start
  27.9 0.0 copy-done.3
  27.9 0.8 subtract_reduce_fusion
  28.7 0.7 sub.34
  29.4 0.7 fusion.25
  30.1 35.3 %all-to-all-done.1 = bf16[32,32,768]{2,1,0:T(8,128)(2,1)} async-done(((bf16[32,32,768]{2,1,0:T(8,128)(2,1)}), bf16[32,32,768]{2,1,0:T(8,128)(2,1)}, u32[]{:S(2)}, u32[]{:S(2)}) %all-to-all-start.1) | async-done | bytes 1572896 | tf_op jit(solution)/shard_map/all_to_all | solution.py:94
  65.4 3.4 %convert_reduce_fusion = (f32[1024]{0:T(1024)S(1)}, bf16[1024,768]{1,0:T(8,128)(2,1)S(1)}) fusion(bf16[1024,768]{1,0:T(8,128)(2,1)} %bitcast.2, s32[1024]{0:T(1024)S(1)} %fusion.25), kind=kOutput, calls=%fused_computation.4 | convolution fusion | flops 1614019584 | bytes 3153920 | tf_op jit(solution)/shard_map/dot_general | solution.py:109
  68.9 0.0 copy-start.2
  68.9 0.6 fusion.4
  69.5 0.0 copy-done
  69.5 0.0 copy-done.5
  69.5 0.0 copy-start.4
  69.5 4.6 %fusion.qt_ref.kt_ref.vt_ref = bf16[2304,1024]{1,0:T(8,128)(2,1)S(1)} fusion(bf16[768,2304]{1,0:T(8,128)(2,1)S(1)} %copy-done, bf16[1024,768]{1,0:T(8,128)(2,1)S(1)} %get-tuple-element.38, f32[768]{0:T(1024)S(1)} %copy-done.5, f32[1024]{0:T(1024)S(1)} %add_rsqrt_fusion, f32[1024]{0:T(1024)S(1)} %broadcast_multiply_fusion), kind=kOutput, calls=%fused_computation.1 | convolution fusion | flops 3630170112 | bytes 9841664 | tf_op jit(solution)/shard_map/dot_general | solution.py:123
  74.2 0.0 copy-done.2
  74.2 0.0 copy-start.1
  74.5 1.8 %copy-done.1 = bf16[2304,1024]{1,0:T(8,128)(2,1)} copy-done((bf16[2304,1024]{1,0:T(8,128)(2,1)}, bf16[2304,1024]{1,0:T(8,128)(2,1)S(1)}, u32[]{:S(2)}) %copy-start.1) | copy-done | bytes 4718616
  76.3 0.8 pad_maximum_fusion
  77.1 0.0 all-gather.2.cloned.1.call-update
  77.9 0.0 copy-done.4
  77.9 0.1 add_compare_fusion
  77.9 0.7 select_convert_fusion.1.bias_ref
  78.6 1.0 select_convert_fusion.fbias_ref
  79.7 56.8 %shard_map.82.prev_ref = bf16[768,1024]{1,0:T(8,128)(2,1)} custom-call(bf16[2304,1024]{1,0:T(8,128)(2,1)} %copy-done.1, bf16[2304,1024]{1,0:T(8,128)(2,1)} %copy-done.1, bf16[2304,1024]{1,0:T(8,128)(2,1)} %copy-done.1, bf16[16,1024]{1,0:T(8,128)(2,1)} %select_convert_fusion.1.bias_ref), custom_call_target="tpu_custom_call" | custom-call | tf_op jit(solution)/shard_map/pallas_call | solution.py:156
  136.5 15.2 %shard_map.83 = bf16[768,1024]{1,0:T(8,128)(2,1)} custom-call(bf16[2304,1024]{1,0:T(8,128)(2,1)} %copy-done.1, bf16[2304,1024]{1,0:T(8,128)(2,1)} %copy-done.1, bf16[2304,1024]{1,0:T(8,128)(2,1)} %copy-done.1, bf16[16,1024]{1,0:T(8,128)(2,1)} %select_convert_fusion.1.bias_ref, ...), custom_call_target="tpu_custom_call", output_to_operand_aliasing={{}: (7, {})} | custom-call | tf_op jit(solution)/shard_map/pallas_call | solution.py:167
  151.7 3.7 %fusion.8 = bf16[1024,768]{1,0:T(8,128)(2,1)S(1)} fusion(bf16[1024,768]{1,0:T(8,128)(2,1)} %copy-done.2, bf16[768,1024]{1,0:T(8,128)(2,1)} %shard_map.83, bf16[768,768]{1,0:T(8,128)(2,1)} %param.14, pred[1024]{0:T(1024)(128)(4,1)S(1)} %get-tuple-element.39), kind=kOutput, calls=%fused_computation.13 | convolution fusion | flops 1211105280 | bytes 5899264 | tf_op jit(solution)/shard_map/dot_general | solution.py:185
  155.4 2.0 %copy.14 = bf16[128,8,768]{2,1,0:T(8,128)(2,1)} copy(bf16[128,8,768]{2,0,1:T(8,128)(2,1)S(1)} %bitcast.150) | data formatting | bytes 3145728 | tf_op jit(solution)/shard_map/transpose | solution.py:189
  (24 shorter events, 0.3 us)
Async XLA Ops:
  6.5 63.0 %copy-start = (bf16[768,2304]{1,0:T(8,128)(2,1)S(1)}, bf16[768,2304]{1,0:T(8,128)(2,1)}, u32[]{:S(2)}) copy-start(bf16[768,2304]{1,0:T(8,128)(2,1)} %param.13) | copy-start | bytes 10616836
  8.1 14.4 %all-to-all-start = ((s32[32,1,32]{2,1,0:T(1,128)}), s32[32,1,32]{2,1,0:T(1,128)S(1)}, u32[]{:S(2)}, u32[]{:S(2)}) async-start(s32[32,1,32]{2,1,0:T(1,128)} %all_to_all.9), calls=%async_computation | async-start | bytes 32768 | tf_op jit(solution)/shard_map/all_to_all | solution.py:101
  22.5 5.4 %copy-start.3 = (s32[32,1,32]{2,1,0:T(1,128)}, s32[32,1,32]{2,1,0:T(1,128)S(1)}, u32[]{:S(2)}) copy-start(s32[32,1,32]{2,1,0:T(1,128)S(1)} %all-to-all-done) | copy-start | bytes 12292
  22.5 42.9 %all-to-all-start.1 = ((bf16[32,32,768]{2,1,0:T(8,128)(2,1)}), bf16[32,32,768]{2,1,0:T(8,128)(2,1)}, u32[]{:S(2)}, u32[]{:S(2)}) async-start(bf16[32,32,768]{2,1,0:T(8,128)(2,1)} %bitcast.149), calls=%async_computation.1 | async-start | bytes 3145728 | tf_op jit(solution)/shard_map/all_to_all | solution.py:94
  27.7 108.8 %all-gather.2.cloned.1.call-start = ((), (), s32[]{:S(2)}) async-start(), calls=%async_computation.2 | async-start | bytes 3538944 | tf_op jit(solution)/shard_map/all_gather | solution.py:142
  65.4 4.1 %copy-start.5 = (f32[768]{0:T(1024)S(1)}, f32[768]{0:T(1024)}, u32[]{:S(2)}) copy-start(f32[768]{0:T(1024)} %param.12) | copy-start | bytes 9220
  68.9 5.3 %copy-start.2 = (bf16[1024,768]{1,0:T(8,128)(2,1)}, bf16[1024,768]{1,0:T(8,128)(2,1)S(1)}, u32[]{:S(2)}) copy-start(bf16[1024,768]{1,0:T(8,128)(2,1)S(1)} %get-tuple-element.38) | copy-start | bytes 4718596
  69.5 8.3 %copy-start.4 = (s32[16]{0:T(128)S(1)}, s32[16]{0:T(128)}, u32[]{:S(2)}) copy-start(s32[16]{0:T(128)} %constant.81.clone) | copy-start | bytes 196
  74.2 2.1 %copy-start.1 = (bf16[2304,1024]{1,0:T(8,128)(2,1)}, bf16[2304,1024]{1,0:T(8,128)(2,1)S(1)}, u32[]{:S(2)}) copy-start(bf16[2304,1024]{1,0:T(8,128)(2,1)S(1)} %fusion.qt_ref.kt_ref.vt_ref) | copy-start | bytes 14155780
Sparse Core Ops, SparseCore 0:
  77.3 32.1 all-gather.1

commit v5 on v4

--- a/solution.py
+++ b/solution.py
@@ -4,9 +4,13 @@
 import jax.numpy as jnp
 from jax import lax
 from jax.experimental import pallas as pl
+from jax.experimental.pallas import tpu as pltpu
 from jax.sharding import PartitionSpec as P
 
 HEAD_COUNT = 16
+QUERY_BLOCK = 256
+PASS1 = 1024
+PASS2 = 512
 DILATION_RATE = 8
 
 
@@ -31,25 +35,48 @@
     return jnp.where(row == 0, 1.0, 0.0).astype(jnp.bfloat16)
 
 
-def nearby_kernel(qt_ref, kt_ref, vt_ref, bias_ref, o_ref, *, groups, group_rows, factor):
-    offset = pl.program_id(0) % DILATION_RATE
-    keys = extend(kt_ref[...], bias_ref[...]).T
-    values_t = vt_ref[...]
-    ones = ones_row(group_rows)
-    for group in range(groups):
-
-        @pl.when(group != offset)
-        def _():
-            rows = pl.ds(group * group_rows, group_rows)
-            queries_t = extend(qt_ref[:, rows], ones)
-            scores_t = jnp.dot(keys, queries_t, preferred_element_type=jnp.float32)
+def nearby_kernel(
+    qt_ref, kt_ref, vt_ref, bias_ref, o_ref, keys_ref, *, groups, group_rows, factor
+):
+    keys_ref[...] = extend(kt_ref[...], bias_ref[...]).T
+    key_count = keys_ref.shape[0]
+    block = QUERY_BLOCK
+    ones = ones_row(block)
+    for first_row in range(0, groups * group_rows, block):
+        rows = pl.ds(first_row, block)
+        queries_t = extend(qt_ref[:, rows], ones)
+        if PASS1 >= key_count and PASS2 >= key_count:
+            scores_t = jnp.dot(keys_ref[...], queries_t, preferred_element_type=jnp.float32)
             top = jnp.max(scores_t, axis=0, keepdims=True)
             weights_t = jnp.exp2((scores_t - top) * factor)
             total = jnp.sum(weights_t, axis=0, keepdims=True)
             summed_t = jnp.dot(
-                values_t, weights_t.astype(jnp.bfloat16), preferred_element_type=jnp.float32
+                vt_ref[...], weights_t.astype(jnp.bfloat16), preferred_element_type=jnp.float32
             )
-            o_ref[:, rows] = (summed_t / total).astype(o_ref.dtype)
+        else:
+            top = None
+            for first in range(0, key_count, PASS1):
+                scores_t = jnp.dot(
+                    keys_ref[pl.ds(first, PASS1), :], queries_t, preferred_element_type=jnp.float32
+                )
+                part = jnp.max(scores_t, axis=0, keepdims=True)
+                top = part if top is None else jnp.maximum(top, part)
+            total = None
+            summed_t = None
+            for first in range(0, key_count, PASS2):
+                scores_t = jnp.dot(
+                    keys_ref[pl.ds(first, PASS2), :], queries_t, preferred_element_type=jnp.float32
+                )
+                weights_t = jnp.exp2((scores_t - top) * factor)
+                part = jnp.sum(weights_t, axis=0, keepdims=True)
+                step = jnp.dot(
+                    vt_ref[:, pl.ds(first, PASS2)],
+                    weights_t.astype(jnp.bfloat16),
+                    preferred_element_type=jnp.float32,
+                )
+                total = part if total is None else total + part
+                summed_t = step if summed_t is None else summed_t + step
+        o_ref[:, rows] = (summed_t / total).astype(o_ref.dtype)
 
 
 def dilated_kernel(
@@ -98,8 +125,9 @@
         concat_axis=0,
         tiled=True,
     ).reshape(rows, width)
-    arrived_slot = lax.all_to_all(
-        slot.reshape(device_count, block_rows), ("tile", "seq"), split_axis=0, concat_axis=0, tiled=True
+    every_slot = lax.all_gather(slot, ("tile", "seq"), tiled=True)
+    arrived_slot = lax.dynamic_slice_in_dim(
+        every_slot.reshape(device_count, device_count, block_rows), my_index, 1, axis=1
     ).reshape(rows)
     local_slot = arrived_slot - my_index * rows
     stored_slot = (local_slot % DILATION_RATE) * group_rows + local_slot // DILATION_RATE
@@ -161,6 +189,7 @@
         in_specs=[query_block, keys_block, values_block, bias_block],
         out_specs=query_block,
         out_shape=jax.ShapeDtypeStruct((width, rows), jnp.bfloat16),
+        scratch_shapes=[pltpu.VMEM((rows, head_size + 16), jnp.bfloat16)],
     )(projected_t, projected_t, projected_t, near_bias)
 
     group_block = pl.BlockSpec((head_size, group_rows), lambda h: (h, h % DILATION_RATE))

time: 165 us -> 172 us (1.042)
  blocking collectives: 0 us -> 63.9 us
  waiting for transfers between devices: 36.1 us -> 0.02 us
  Pallas kernels: 72 us -> 55.3 us
  starting transfers between devices: 12.7 us -> 7.45 us
    all_gather x0 -> x1, blocking collectives: none -> 63.9 us  [body(): every_slot = lax.all_gather(slot, ('tile', 'seq'), tiled=True)]
    all_to_all x1, waiting for transfers between devices: 35.3 us -> 0.01 us  [body(): lax.all_to_all(projected.reshape(device_count, block_rows, width), ('tile...]
    pallas_call x1, Pallas kernels: 56.8 us -> 40.1 us  [body(): pl.pallas_call(functools.partial(nearby_kernel, groups=DILATION_RATE, gro...]
    all_to_all x1 -> x0, starting transfers between devices: 7.3 us -> none  [body(): lax.all_to_all(slot.reshape(device_count, block_rows), ('tile', 'seq'), s...]
    all_to_all x1, starting transfers between devices: 5.17 us -> 7.41 us  [body(): lax.all_to_all(projected.reshape(device_count, block_rows, width), ('tile...]
    reshape x0 -> x1, local copies, waits for them, and re-layouts: none -> 1.9 us  [body(): every_slot.reshape(device_count, device_count, block_rows)]
  transfers between devices with their start and end apart: 3 -> 2, of which waited for: 2 -> 0; matrix products, arithmetic and copies ran while one was open for 6% -> 4% of each run, Pallas kernels for 35% -> 23%
where the time goes in v5:
time: 172 us; the launch traced here: 171 us
  blocking collectives  63.9 us (37%)
  Pallas kernels  55.3 us (32%)
  matrix products  18.3 us (11%)
  between operations  14.3 us (8%)
  starting transfers between devices  7.45 us (4%)
  local copies, waits for them, and re-layouts  6.66 us (4%)
  other arithmetic  4.86 us (3%)
    all_gather x1, blocking collectives, body(): every_slot = lax.all_gather(slot, ('tile', 'seq'), tiled=True)  63.9 us
    pallas_call x1, Pallas kernels, body(): pl.pallas_call(functools.partial(nearby_kernel, groups=DILATION_RATE, gro...  40.1 us
    pallas_call x1, Pallas kernels, body(): pl.pallas_call(functools.partial(dilated_kernel, factor=factor), grid=(HE...  15.2 us
    all_to_all x1, starting transfers between devices, body(): lax.all_to_all(projected.reshape(device_count, block_rows, width), ('tile...  7.41 us
    dot_general x1, matrix products, body(): jnp.dot(embeddings, in_weight, preferred_element_type=jnp.float32)  6.5 us
    dot_general x1, matrix products, body(): lax.dot_general(qkv_weight, normed, (((0,), (1,)), ((), ())), preferred_e...  4.63 us
    dot_general x1, matrix products, body(): lax.dot_general(attended_t, out_weight, (((0,), (0,)), ((), ())), preferr...  3.73 us
  transfers between devices with their start and end apart: 2, of which 0 were waited for; matrix products, arithmetic and copies ran while one was open for 4% of the time, Pallas kernels for 23%

profile of v5, /device:TPU:0, one launch (start us, length us, event | category | flops | bytes accessed | tf_op | source)
XLA Modules:
  0.0 170.8 jit_solution(14961292603473850438)
XLA Ops:
  6.5 0.0 copy-start
  6.5 6.5 %convolution_convert_fusion.1 = bf16[1024,768]{1,0:T(8,128)(2,1)} fusion(bf16[1024,1536]{1,0:T(8,128)(2,1)} %param.8, bf16[1536,768]{1,0:T(8,128)(2,1)} %param.11), kind=kOutput, calls=%fused_computation.16 | convolution fusion | flops 2416705536 | bytes 7077888 | tf_op jit(solution)/shard_map/dot_general | solution.py:118
  13.0 7.4 %all-to-all-start = ((bf16[32,32,768]{2,1,0:T(8,128)(2,1)}), bf16[32,32,768]{2,1,0:T(8,128)(2,1)}, u32[]{:S(2)}, u32[]{:S(2)}) async-start(bf16[32,32,768]{2,1,0:T(8,128)(2,1)} %bitcast.149), calls=%async_computation | async-start | bytes 3145728 | tf_op jit(solution)/shard_map/all_to_all | solution.py:121
  20.5 0.0 all-gather.2.cloned.1.call-start
  20.5 0.0 copy-done.3
  20.5 63.9 %all_gather.6 = s32[32768]{0:T(1024)} all-gather(s32[1024]{0:T(1024)S(1)} %copy-done.3), channel_id=1, replica_groups=mesh['tile'=4,'seq'=8] {'tile','seq'}, dimensions={0}, use_global_device_ids=true | all-gather | bytes 135168 | tf_op jit(solution)/shard_map/all_gather | solution.py:128
  84.5 1.9 %reshape.152 = s32[32,32,32]{2,1,0:T(8,128)} reshape(s32[32768]{0:T(1024)} %all_gather.6) | data formatting | bytes 262144 | tf_op jit(solution)/shard_map/reshape | solution.py:130
  86.4 1.0 subtract_reduce_fusion
  87.3 0.7 sub.34
  88.0 0.7 fusion.25
  88.7 0.0 all-to-all-done
  88.7 0.0 copy-start.5
  88.7 3.4 %convert_reduce_fusion = (f32[1024]{0:T(1024)S(1)}, bf16[1024,768]{1,0:T(8,128)(2,1)S(1)}) fusion(bf16[1024,768]{1,0:T(8,128)(2,1)} %bitcast.2, s32[1024]{0:T(1024)S(1)} %fusion.25), kind=kOutput, calls=%fused_computation.4 | convolution fusion | flops 1614019584 | bytes 3153920 | tf_op jit(solution)/shard_map/dot_general | solution.py:137
  92.1 0.0 copy-start.2
  92.2 0.6 fusion.4
  92.8 0.0 copy-done
  92.8 0.0 copy-done.5
  92.8 0.0 copy-start.4
  92.8 4.6 %fusion.qt_ref.kt_ref.vt_ref = bf16[2304,1024]{1,0:T(8,128)(2,1)S(1)} fusion(bf16[768,2304]{1,0:T(8,128)(2,1)S(1)} %copy-done, bf16[1024,768]{1,0:T(8,128)(2,1)S(1)} %get-tuple-element.38, f32[768]{0:T(1024)S(1)} %copy-done.5, f32[1024]{0:T(1024)S(1)} %add_rsqrt_fusion, f32[1024]{0:T(1024)S(1)} %broadcast_multiply_fusion), kind=kOutput, calls=%fused_computation.1 | convolution fusion | flops 3630170112 | bytes 9841664 | tf_op jit(solution)/shard_map/dot_general | solution.py:151
  97.5 0.0 copy-done.2
  97.5 0.0 copy-start.1
  97.8 1.8 %copy-done.1 = bf16[2304,1024]{1,0:T(8,128)(2,1)} copy-done((bf16[2304,1024]{1,0:T(8,128)(2,1)}, bf16[2304,1024]{1,0:T(8,128)(2,1)S(1)}, u32[]{:S(2)}) %copy-start.1) | copy-done | bytes 4718616
  99.6 0.8 pad_maximum_fusion
  100.4 0.0 all-gather.2.cloned.1.call-update
  101.1 0.0 copy-done.4
  101.1 0.1 add_compare_fusion
  101.2 0.7 select_convert_fusion.1.bias_ref
  101.9 1.0 select_convert_fusion.fbias_ref
  102.9 40.1 %shard_map.82.prev_ref = bf16[768,1024]{1,0:T(8,128)(2,1)} custom-call(bf16[2304,1024]{1,0:T(8,128)(2,1)} %copy-done.1, bf16[2304,1024]{1,0:T(8,128)(2,1)} %copy-done.1, bf16[2304,1024]{1,0:T(8,128)(2,1)} %copy-done.1, bf16[16,1024]{1,0:T(8,128)(2,1)} %select_convert_fusion.1.bias_ref), custom_call_target="tpu_custom_call" | custom-call | tf_op jit(solution)/shard_map/pallas_call | solution.py:184
  143.0 15.2 %shard_map.83 = bf16[768,1024]{1,0:T(8,128)(2,1)} custom-call(bf16[2304,1024]{1,0:T(8,128)(2,1)} %copy-done.1, bf16[2304,1024]{1,0:T(8,128)(2,1)} %copy-done.1, bf16[2304,1024]{1,0:T(8,128)(2,1)} %copy-done.1, bf16[16,1024]{1,0:T(8,128)(2,1)} %select_convert_fusion.1.bias_ref, ...), custom_call_target="tpu_custom_call", output_to_operand_aliasing={{}: (7, {})} | custom-call | tf_op jit(solution)/shard_map/pallas_call | solution.py:196
  158.2 3.7 %fusion.8 = bf16[1024,768]{1,0:T(8,128)(2,1)S(1)} fusion(bf16[1024,768]{1,0:T(8,128)(2,1)} %copy-done.2, bf16[768,1024]{1,0:T(8,128)(2,1)} %shard_map.83, bf16[768,768]{1,0:T(8,128)(2,1)} %param.14, pred[1024]{0:T(1024)(128)(4,1)S(1)} %get-tuple-element.39), kind=kOutput, calls=%fused_computation.13 | convolution fusion | flops 1211105280 | bytes 5899264 | tf_op jit(solution)/shard_map/dot_general | solution.py:214
  162.0 2.0 %copy.16 = bf16[128,8,768]{2,1,0:T(8,128)(2,1)} copy(bf16[128,8,768]{2,0,1:T(8,128)(2,1)S(1)} %bitcast.150) | data formatting | bytes 3145728 | tf_op jit(solution)/shard_map/transpose | solution.py:218
  (23 shorter events, 0.3 us)
Async XLA Ops:
  6.5 86.2 %copy-start = (bf16[768,2304]{1,0:T(8,128)(2,1)S(1)}, bf16[768,2304]{1,0:T(8,128)(2,1)}, u32[]{:S(2)}) copy-start(bf16[768,2304]{1,0:T(8,128)(2,1)} %param.13) | copy-start | bytes 10616836
  13.0 7.5 %copy-start.3 = (s32[1024]{0:T(1024)S(1)}, s32[1024]{0:T(1024)}, u32[]{:S(2)}) copy-start(s32[1024]{0:T(1024)} %param.9) | copy-start | bytes 12292
  13.0 75.7 %all-to-all-start = ((bf16[32,32,768]{2,1,0:T(8,128)(2,1)}), bf16[32,32,768]{2,1,0:T(8,128)(2,1)}, u32[]{:S(2)}, u32[]{:S(2)}) async-start(bf16[32,32,768]{2,1,0:T(8,128)(2,1)} %bitcast.149), calls=%async_computation | async-start | bytes 3145728 | tf_op jit(solution)/shard_map/all_to_all | solution.py:121
  20.5 122.5 %all-gather.2.cloned.1.call-start = ((), (), s32[]{:S(2)}) async-start(), calls=%async_computation.1 | async-start | bytes 3538944 | tf_op jit(solution)/shard_map/all_gather | solution.py:170
  88.7 4.1 %copy-start.5 = (f32[768]{0:T(1024)S(1)}, f32[768]{0:T(1024)}, u32[]{:S(2)}) copy-start(f32[768]{0:T(1024)} %param.12) | copy-start | bytes 9220
  92.1 5.3 %copy-start.2 = (bf16[1024,768]{1,0:T(8,128)(2,1)}, bf16[1024,768]{1,0:T(8,128)(2,1)S(1)}, u32[]{:S(2)}) copy-start(bf16[1024,768]{1,0:T(8,128)(2,1)S(1)} %get-tuple-element.38) | copy-start | bytes 4718596
  92.8 8.3 %copy-start.4 = (s32[16]{0:T(128)S(1)}, s32[16]{0:T(128)}, u32[]{:S(2)}) copy-start(s32[16]{0:T(128)} %constant.84.clone) | copy-start | bytes 196
  97.5 2.1 %copy-start.1 = (bf16[2304,1024]{1,0:T(8,128)(2,1)}, bf16[2304,1024]{1,0:T(8,128)(2,1)S(1)}, u32[]{:S(2)}) copy-start(bf16[2304,1024]{1,0:T(8,128)(2,1)S(1)} %fusion.qt_ref.kt_ref.vt_ref) | copy-start | bytes 14155780
Sparse Core Ops, SparseCore 0:
  100.5 32.3 all-gather.1

commit v6 on v5

--- a/solution.py
+++ b/solution.py
@@ -125,9 +125,8 @@
         concat_axis=0,
         tiled=True,
     ).reshape(rows, width)
-    every_slot = lax.all_gather(slot, ("tile", "seq"), tiled=True)
-    arrived_slot = lax.dynamic_slice_in_dim(
-        every_slot.reshape(device_count, device_count, block_rows), my_index, 1, axis=1
+    arrived_slot = lax.all_to_all(
+        slot.reshape(device_count, block_rows), ("tile", "seq"), split_axis=0, concat_axis=0, tiled=True
     ).reshape(rows)
     local_slot = arrived_slot - my_index * rows
     stored_slot = (local_slot % DILATION_RATE) * group_rows + local_slot // DILATION_RATE

time: 172 us -> 149 us (0.87)
  blocking collectives: 63.9 us -> 0 us
  waiting for transfers between devices: 0.02 us -> 36.1 us
  starting transfers between devices: 7.45 us -> 12.7 us
    all_gather x1 -> x0, blocking collectives: 63.9 us -> none  [body(): every_slot = lax.all_gather(slot, ('tile', 'seq'), tiled=True)]
    all_to_all x1, waiting for transfers between devices: 0.01 us -> 35.3 us  [body(): lax.all_to_all(projected.reshape(device_count, block_rows, width), ('tile...]
    all_to_all x0 -> x1, starting transfers between devices: none -> 7.3 us  [body(): lax.all_to_all(slot.reshape(device_count, block_rows), ('tile', 'seq'), s...]
    all_to_all x1, starting transfers between devices: 7.41 us -> 5.17 us  [body(): lax.all_to_all(projected.reshape(device_count, block_rows, width), ('tile...]
    reshape x1 -> x0, local copies, waits for them, and re-layouts: 1.9 us -> none  [body(): every_slot.reshape(device_count, device_count, block_rows)]
  transfers between devices with their start and end apart: 2 -> 3, of which waited for: 0 -> 2; matrix products, arithmetic and copies ran while one was open for 4% -> 7% of each run, Pallas kernels for 23% -> 27%
where the time goes in v6:
time: 149 us; the launch traced here: 148 us
  Pallas kernels  55.3 us (37%)
  waiting for transfers between devices  36.1 us (24%)
  matrix products  18.2 us (12%)
  between operations  14.3 us (10%)
  starting transfers between devices  12.7 us (9%)
  local copies, waits for them, and re-layouts  6.31 us (4%)
  other arithmetic  4.69 us (3%)
    pallas_call x1, Pallas kernels, body(): pl.pallas_call(functools.partial(nearby_kernel, groups=DILATION_RATE, gro...  40.1 us
    all_to_all x1, waiting for transfers between devices, body(): lax.all_to_all(projected.reshape(device_count, block_rows, width), ('tile...  35.3 us
    pallas_call x1, Pallas kernels, body(): pl.pallas_call(functools.partial(dilated_kernel, factor=factor), grid=(HE...  15.2 us
    all_to_all x1, starting transfers between devices, body(): lax.all_to_all(slot.reshape(device_count, block_rows), ('tile', 'seq'), s...  7.3 us
    dot_general x1, matrix products, body(): jnp.dot(embeddings, in_weight, preferred_element_type=jnp.float32)  6.36 us
    all_to_all x1, starting transfers between devices, body(): lax.all_to_all(projected.reshape(device_count, block_rows, width), ('tile...  5.17 us
    dot_general x1, matrix products, body(): lax.dot_general(qkv_weight, normed, (((0,), (1,)), ((), ())), preferred_e...  4.64 us
    dot_general x1, matrix products, body(): lax.dot_general(attended_t, out_weight, (((0,), (0,)), ((), ())), preferr...  3.73 us
  transfers between devices with their start and end apart: 3, of which 2 were waited for; matrix products, arithmetic and copies ran while one was open for 7% of the time, Pallas kernels for 27%

profile of v6, /device:TPU:0, one launch (start us, length us, event | category | flops | bytes accessed | tf_op | source)
XLA Modules:
  0.0 147.6 jit_solution(9672551752544378642)
XLA Ops:
  6.5 0.0 copy-start
  6.5 1.5 %all_to_all.9 = s32[32,1,32]{2,1,0:T(1,128)} reshape(s32[1024]{0:T(1024)} %param.9) | data formatting | bytes 8192 | tf_op jit(solution)/shard_map/all_to_all | solution.py:128
  8.1 7.3 %all-to-all-start = ((s32[32,1,32]{2,1,0:T(1,128)}), s32[32,1,32]{2,1,0:T(1,128)S(1)}, u32[]{:S(2)}, u32[]{:S(2)}) async-start(s32[32,1,32]{2,1,0:T(1,128)} %all_to_all.9), calls=%async_computation | async-start | bytes 32768 | tf_op jit(solution)/shard_map/all_to_all | solution.py:128
  15.4 6.4 %convolution_convert_fusion.1 = bf16[1024,768]{1,0:T(8,128)(2,1)} fusion(bf16[1024,1536]{1,0:T(8,128)(2,1)} %param.8, bf16[1536,768]{1,0:T(8,128)(2,1)} %param.11), kind=kOutput, calls=%fused_computation.16 | convolution fusion | flops 2416705536 | bytes 7077888 | tf_op jit(solution)/shard_map/dot_general | solution.py:118
  21.7 0.8 all-to-all-done
  22.5 5.2 %all-to-all-start.1 = ((bf16[32,32,768]{2,1,0:T(8,128)(2,1)}), bf16[32,32,768]{2,1,0:T(8,128)(2,1)}, u32[]{:S(2)}, u32[]{:S(2)}) async-start(bf16[32,32,768]{2,1,0:T(8,128)(2,1)} %bitcast.149), calls=%async_computation.1 | async-start | bytes 3145728 | tf_op jit(solution)/shard_map/all_to_all | solution.py:121
  27.7 0.2 all-gather.2.cloned.1.call-start
  27.9 0.0 copy-done.3
  27.9 0.8 subtract_reduce_fusion
  28.7 0.7 sub.34
  29.4 0.7 fusion.25
  30.1 35.3 %all-to-all-done.1 = bf16[32,32,768]{2,1,0:T(8,128)(2,1)} async-done(((bf16[32,32,768]{2,1,0:T(8,128)(2,1)}), bf16[32,32,768]{2,1,0:T(8,128)(2,1)}, u32[]{:S(2)}, u32[]{:S(2)}) %all-to-all-start.1) | async-done | bytes 1572896 | tf_op jit(solution)/shard_map/all_to_all | solution.py:121
  65.4 3.4 %convert_reduce_fusion = (f32[1024]{0:T(1024)S(1)}, bf16[1024,768]{1,0:T(8,128)(2,1)S(1)}) fusion(bf16[1024,768]{1,0:T(8,128)(2,1)} %bitcast.2, s32[1024]{0:T(1024)S(1)} %fusion.25), kind=kOutput, calls=%fused_computation.4 | convolution fusion | flops 1614019584 | bytes 3153920 | tf_op jit(solution)/shard_map/dot_general | solution.py:136
  68.9 0.0 copy-start.2
  68.9 0.6 fusion.4
  69.5 0.0 copy-done
  69.5 0.0 copy-done.5
  69.5 0.0 copy-start.4
  69.5 4.6 %fusion.qt_ref.kt_ref.vt_ref = bf16[2304,1024]{1,0:T(8,128)(2,1)S(1)} fusion(bf16[768,2304]{1,0:T(8,128)(2,1)S(1)} %copy-done, bf16[1024,768]{1,0:T(8,128)(2,1)S(1)} %get-tuple-element.38, f32[768]{0:T(1024)S(1)} %copy-done.5, f32[1024]{0:T(1024)S(1)} %add_rsqrt_fusion, f32[1024]{0:T(1024)S(1)} %broadcast_multiply_fusion), kind=kOutput, calls=%fused_computation.1 | convolution fusion | flops 3630170112 | bytes 9841664 | tf_op jit(solution)/shard_map/dot_general | solution.py:150
  74.2 0.0 copy-done.2
  74.2 0.0 copy-start.1
  74.5 1.8 %copy-done.1 = bf16[2304,1024]{1,0:T(8,128)(2,1)} copy-done((bf16[2304,1024]{1,0:T(8,128)(2,1)}, bf16[2304,1024]{1,0:T(8,128)(2,1)S(1)}, u32[]{:S(2)}) %copy-start.1) | copy-done | bytes 4718616
  76.3 0.8 pad_maximum_fusion
  77.1 0.0 all-gather.2.cloned.1.call-update
  77.9 0.0 copy-done.4
  77.9 0.1 add_compare_fusion
  77.9 0.7 select_convert_fusion.1.bias_ref
  78.6 1.0 select_convert_fusion.fbias_ref
  79.7 40.1 %shard_map.82.prev_ref = bf16[768,1024]{1,0:T(8,128)(2,1)} custom-call(bf16[2304,1024]{1,0:T(8,128)(2,1)} %copy-done.1, bf16[2304,1024]{1,0:T(8,128)(2,1)} %copy-done.1, bf16[2304,1024]{1,0:T(8,128)(2,1)} %copy-done.1, bf16[16,1024]{1,0:T(8,128)(2,1)} %select_convert_fusion.1.bias_ref), custom_call_target="tpu_custom_call" | custom-call | tf_op jit(solution)/shard_map/pallas_call | solution.py:183
  119.8 15.2 %shard_map.83 = bf16[768,1024]{1,0:T(8,128)(2,1)} custom-call(bf16[2304,1024]{1,0:T(8,128)(2,1)} %copy-done.1, bf16[2304,1024]{1,0:T(8,128)(2,1)} %copy-done.1, bf16[2304,1024]{1,0:T(8,128)(2,1)} %copy-done.1, bf16[16,1024]{1,0:T(8,128)(2,1)} %select_convert_fusion.1.bias_ref, ...), custom_call_target="tpu_custom_call", output_to_operand_aliasing={{}: (7, {})} | custom-call | tf_op jit(solution)/shard_map/pallas_call | solution.py:195
  135.0 3.7 %fusion.8 = bf16[1024,768]{1,0:T(8,128)(2,1)S(1)} fusion(bf16[1024,768]{1,0:T(8,128)(2,1)} %copy-done.2, bf16[768,1024]{1,0:T(8,128)(2,1)} %shard_map.83, bf16[768,768]{1,0:T(8,128)(2,1)} %param.14, pred[1024]{0:T(1024)(128)(4,1)S(1)} %get-tuple-element.39), kind=kOutput, calls=%fused_computation.13 | convolution fusion | flops 1211105280 | bytes 5899264 | tf_op jit(solution)/shard_map/dot_general | solution.py:213
  138.7 2.0 %copy.14 = bf16[128,8,768]{2,1,0:T(8,128)(2,1)} copy(bf16[128,8,768]{2,0,1:T(8,128)(2,1)S(1)} %bitcast.150) | data formatting | bytes 3145728 | tf_op jit(solution)/shard_map/transpose | solution.py:217
  (24 shorter events, 0.3 us)
Async XLA Ops:
  6.5 63.0 %copy-start = (bf16[768,2304]{1,0:T(8,128)(2,1)S(1)}, bf16[768,2304]{1,0:T(8,128)(2,1)}, u32[]{:S(2)}) copy-start(bf16[768,2304]{1,0:T(8,128)(2,1)} %param.13) | copy-start | bytes 10616836
  8.1 14.4 %all-to-all-start = ((s32[32,1,32]{2,1,0:T(1,128)}), s32[32,1,32]{2,1,0:T(1,128)S(1)}, u32[]{:S(2)}, u32[]{:S(2)}) async-start(s32[32,1,32]{2,1,0:T(1,128)} %all_to_all.9), calls=%async_computation | async-start | bytes 32768 | tf_op jit(solution)/shard_map/all_to_all | solution.py:128
  22.5 5.4 %copy-start.3 = (s32[32,1,32]{2,1,0:T(1,128)}, s32[32,1,32]{2,1,0:T(1,128)S(1)}, u32[]{:S(2)}) copy-start(s32[32,1,32]{2,1,0:T(1,128)S(1)} %all-to-all-done) | copy-start | bytes 12292
  22.5 42.9 %all-to-all-start.1 = ((bf16[32,32,768]{2,1,0:T(8,128)(2,1)}), bf16[32,32,768]{2,1,0:T(8,128)(2,1)}, u32[]{:S(2)}, u32[]{:S(2)}) async-start(bf16[32,32,768]{2,1,0:T(8,128)(2,1)} %bitcast.149), calls=%async_computation.1 | async-start | bytes 3145728 | tf_op jit(solution)/shard_map/all_to_all | solution.py:121
  27.7 92.1 %all-gather.2.cloned.1.call-start = ((), (), s32[]{:S(2)}) async-start(), calls=%async_computation.2 | async-start | bytes 3538944 | tf_op jit(solution)/shard_map/all_gather | solution.py:169
  65.4 4.1 %copy-start.5 = (f32[768]{0:T(1024)S(1)}, f32[768]{0:T(1024)}, u32[]{:S(2)}) copy-start(f32[768]{0:T(1024)} %param.12) | copy-start | bytes 9220
  68.9 5.3 %copy-start.2 = (bf16[1024,768]{1,0:T(8,128)(2,1)}, bf16[1024,768]{1,0:T(8,128)(2,1)S(1)}, u32[]{:S(2)}) copy-start(bf16[1024,768]{1,0:T(8,128)(2,1)S(1)} %get-tuple-element.38) | copy-start | bytes 4718596
  69.5 8.3 %copy-start.4 = (s32[16]{0:T(128)S(1)}, s32[16]{0:T(128)}, u32[]{:S(2)}) copy-start(s32[16]{0:T(128)} %constant.81.clone) | copy-start | bytes 196
  74.2 2.1 %copy-start.1 = (bf16[2304,1024]{1,0:T(8,128)(2,1)}, bf16[2304,1024]{1,0:T(8,128)(2,1)S(1)}, u32[]{:S(2)}) copy-start(bf16[2304,1024]{1,0:T(8,128)(2,1)S(1)} %fusion.qt_ref.kt_ref.vt_ref) | copy-start | bytes 14155780
Sparse Core Ops, SparseCore 0:
  77.3 31.9 all-gather.1

commit v7 on v6

--- a/solution.py
+++ b/solution.py
@@ -80,26 +80,35 @@
 
 
 def dilated_kernel(
-    qt_ref, kt_ref, vt_ref, bias_ref, fk_ref, fv_ref, fbias_ref, prev_ref, o_ref, *, factor
+    qt_ref, kt_ref, vt_ref, bias_ref, fk_ref, fv_ref, fbias_ref, prev_ref, o_ref,
+    near_ref, far_ref, *, factor
 ):
     del prev_ref
     queries_t = extend(qt_ref[...], ones_row(qt_ref.shape[1]))
-    near_keys = extend(kt_ref[...], bias_ref[...]).T
-    far_keys = extend(fk_ref[0, 0], fbias_ref[0]).T
-    near = jnp.dot(near_keys, queries_t, preferred_element_type=jnp.float32)
-    far = jnp.dot(far_keys, queries_t, preferred_element_type=jnp.float32)
-    top = jnp.maximum(
-        jnp.max(near, axis=0, keepdims=True), jnp.max(far, axis=0, keepdims=True)
-    )
-    near_w = jnp.exp2((near - top) * factor)
-    far_w = jnp.exp2((far - top) * factor)
-    total = jnp.sum(near_w, axis=0, keepdims=True) + jnp.sum(far_w, axis=0, keepdims=True)
-    summed_t = jnp.dot(
-        vt_ref[...], near_w.astype(jnp.bfloat16), preferred_element_type=jnp.float32
-    )
-    summed_t = summed_t + jnp.dot(
-        fv_ref[0, 0], far_w.astype(jnp.bfloat16), preferred_element_type=jnp.float32
-    )
+    near_ref[...] = extend(kt_ref[...], bias_ref[...]).T
+    far_ref[...] = extend(fk_ref[0, 0], fbias_ref[0]).T
+    sources = ((near_ref, lambda c: vt_ref[:, c]), (far_ref, lambda c: fv_ref[0, 0, :, c]))
+    top = None
+    for keys_ref, _ in sources:
+        for first in range(0, keys_ref.shape[0], PASS1):
+            scores_t = jnp.dot(
+                keys_ref[pl.ds(first, PASS1), :], queries_t, preferred_element_type=jnp.float32
+            )
+            part = jnp.max(scores_t, axis=0, keepdims=True)
+            top = part if top is None else jnp.maximum(top, part)
+    total = None
+    summed_t = None
+    for keys_ref, values in sources:
+        for first in range(0, keys_ref.shape[0], PASS2):
+            chunk = pl.ds(first, PASS2)
+            scores_t = jnp.dot(keys_ref[chunk, :], queries_t, preferred_element_type=jnp.float32)
+            weights_t = jnp.exp2((scores_t - top) * factor)
+            part = jnp.sum(weights_t, axis=0, keepdims=True)
+            step = jnp.dot(
+                values(chunk), weights_t.astype(jnp.bfloat16), preferred_element_type=jnp.float32
+            )
+            total = part if total is None else total + part
+            summed_t = step if summed_t is None else summed_t + step
     o_ref[...] = (summed_t / total).astype(o_ref.dtype)
 
 
@@ -207,6 +216,10 @@
         ],
         out_specs=group_block,
         out_shape=jax.ShapeDtypeStruct((width, rows), jnp.bfloat16),
+        scratch_shapes=[
+            pltpu.VMEM((rows, head_size + 16), jnp.bfloat16),
+            pltpu.VMEM((far_count, head_size + 16), jnp.bfloat16),
+        ],
         input_output_aliases={7: 0},
     )(projected_t, projected_t, projected_t, near_bias, far, far, far_bias, nearby)
 

time: 149 us -> 152 us (1.020)
  Pallas kernels: 55.3 us -> 58.7 us
    pallas_call x1, Pallas kernels: 15.2 us -> 18.7 us  [body(): pl.pallas_call(functools.partial(dilated_kernel, factor=factor), grid=(HE...]
where the time goes in v7:
time: 152 us; the launch traced here: 151 us
  Pallas kernels  58.7 us (39%)
  waiting for transfers between devices  36.1 us (24%)
  matrix products  18.2 us (12%)
  between operations  14.3 us (9%)
  starting transfers between devices  12.7 us (8%)
  local copies, waits for them, and re-layouts  6.31 us (4%)
  other arithmetic  4.69 us (3%)
    pallas_call x1, Pallas kernels, body(): pl.pallas_call(functools.partial(nearby_kernel, groups=DILATION_RATE, gro...  40.1 us
    all_to_all x1, waiting for transfers between devices, body(): lax.all_to_all(projected.reshape(device_count, block_rows, width), ('tile...  35.3 us
    pallas_call x1, Pallas kernels, body(): pl.pallas_call(functools.partial(dilated_kernel, factor=factor), grid=(HE...  18.7 us
    all_to_all x1, starting transfers between devices, body(): lax.all_to_all(slot.reshape(device_count, block_rows), ('tile', 'seq'), s...  7.3 us
    dot_general x1, matrix products, body(): jnp.dot(embeddings, in_weight, preferred_element_type=jnp.float32)  6.36 us
    all_to_all x1, starting transfers between devices, body(): lax.all_to_all(projected.reshape(device_count, block_rows, width), ('tile...  5.17 us
    dot_general x1, matrix products, body(): lax.dot_general(qkv_weight, normed, (((0,), (1,)), ((), ())), preferred_e...  4.64 us
    dot_general x1, matrix products, body(): lax.dot_general(attended_t, out_weight, (((0,), (0,)), ((), ())), preferr...  3.73 us
  transfers between devices with their start and end apart: 3, of which 2 were waited for; matrix products, arithmetic and copies ran while one was open for 7% of the time, Pallas kernels for 27%

profile of v7, /device:TPU:0, one launch (start us, length us, event | category | flops | bytes accessed | tf_op | source)
XLA Modules:
  0.0 151.0 jit_solution(2874227365038507296)
XLA Ops:
  6.5 0.0 copy-start
  6.5 1.5 %all_to_all.9 = s32[32,1,32]{2,1,0:T(1,128)} reshape(s32[1024]{0:T(1024)} %param.9) | data formatting | bytes 8192 | tf_op jit(solution)/shard_map/all_to_all | solution.py:137
  8.1 7.3 %all-to-all-start = ((s32[32,1,32]{2,1,0:T(1,128)}), s32[32,1,32]{2,1,0:T(1,128)S(1)}, u32[]{:S(2)}, u32[]{:S(2)}) async-start(s32[32,1,32]{2,1,0:T(1,128)} %all_to_all.9), calls=%async_computation | async-start | bytes 32768 | tf_op jit(solution)/shard_map/all_to_all | solution.py:137
  15.4 6.4 %convolution_convert_fusion.1 = bf16[1024,768]{1,0:T(8,128)(2,1)} fusion(bf16[1024,1536]{1,0:T(8,128)(2,1)} %param.8, bf16[1536,768]{1,0:T(8,128)(2,1)} %param.11), kind=kOutput, calls=%fused_computation.16 | convolution fusion | flops 2416705536 | bytes 7077888 | tf_op jit(solution)/shard_map/dot_general | solution.py:127
  21.7 0.8 all-to-all-done
  22.5 5.2 %all-to-all-start.1 = ((bf16[32,32,768]{2,1,0:T(8,128)(2,1)}), bf16[32,32,768]{2,1,0:T(8,128)(2,1)}, u32[]{:S(2)}, u32[]{:S(2)}) async-start(bf16[32,32,768]{2,1,0:T(8,128)(2,1)} %bitcast.149), calls=%async_computation.1 | async-start | bytes 3145728 | tf_op jit(solution)/shard_map/all_to_all | solution.py:130
  27.7 0.2 all-gather.2.cloned.1.call-start
  27.9 0.0 copy-done.3
  27.9 0.8 subtract_reduce_fusion
  28.7 0.7 sub.34
  29.4 0.7 fusion.25
  30.1 35.3 %all-to-all-done.1 = bf16[32,32,768]{2,1,0:T(8,128)(2,1)} async-done(((bf16[32,32,768]{2,1,0:T(8,128)(2,1)}), bf16[32,32,768]{2,1,0:T(8,128)(2,1)}, u32[]{:S(2)}, u32[]{:S(2)}) %all-to-all-start.1) | async-done | bytes 1572896 | tf_op jit(solution)/shard_map/all_to_all | solution.py:130
  65.4 3.4 %convert_reduce_fusion = (f32[1024]{0:T(1024)S(1)}, bf16[1024,768]{1,0:T(8,128)(2,1)S(1)}) fusion(bf16[1024,768]{1,0:T(8,128)(2,1)} %bitcast.2, s32[1024]{0:T(1024)S(1)} %fusion.25), kind=kOutput, calls=%fused_computation.4 | convolution fusion | flops 1614019584 | bytes 3153920 | tf_op jit(solution)/shard_map/dot_general | solution.py:145
  68.9 0.0 copy-start.2
  68.9 0.6 fusion.4
  69.5 0.0 copy-done
  69.5 0.0 copy-done.5
  69.5 0.0 copy-start.4
  69.5 4.6 %fusion.qt_ref.kt_ref.vt_ref = bf16[2304,1024]{1,0:T(8,128)(2,1)S(1)} fusion(bf16[768,2304]{1,0:T(8,128)(2,1)S(1)} %copy-done, bf16[1024,768]{1,0:T(8,128)(2,1)S(1)} %get-tuple-element.38, f32[768]{0:T(1024)S(1)} %copy-done.5, f32[1024]{0:T(1024)S(1)} %add_rsqrt_fusion, f32[1024]{0:T(1024)S(1)} %broadcast_multiply_fusion), kind=kOutput, calls=%fused_computation.1 | convolution fusion | flops 3630170112 | bytes 9841664 | tf_op jit(solution)/shard_map/dot_general | solution.py:159
  74.2 0.0 copy-done.2
  74.2 0.0 copy-start.1
  74.5 1.8 %copy-done.1 = bf16[2304,1024]{1,0:T(8,128)(2,1)} copy-done((bf16[2304,1024]{1,0:T(8,128)(2,1)}, bf16[2304,1024]{1,0:T(8,128)(2,1)S(1)}, u32[]{:S(2)}) %copy-start.1) | copy-done | bytes 4718616
  76.3 0.8 pad_maximum_fusion
  77.1 0.0 all-gather.2.cloned.1.call-update
  77.9 0.0 copy-done.4
  77.9 0.1 add_compare_fusion
  77.9 0.7 select_convert_fusion.1.bias_ref
  78.6 1.0 select_convert_fusion.fbias_ref
  79.7 40.1 %shard_map.82.prev_ref = bf16[768,1024]{1,0:T(8,128)(2,1)} custom-call(bf16[2304,1024]{1,0:T(8,128)(2,1)} %copy-done.1, bf16[2304,1024]{1,0:T(8,128)(2,1)} %copy-done.1, bf16[2304,1024]{1,0:T(8,128)(2,1)} %copy-done.1, bf16[16,1024]{1,0:T(8,128)(2,1)} %select_convert_fusion.1.bias_ref), custom_call_target="tpu_custom_call" | custom-call | tf_op jit(solution)/shard_map/pallas_call | solution.py:192
  119.8 18.7 %shard_map.83 = bf16[768,1024]{1,0:T(8,128)(2,1)} custom-call(bf16[2304,1024]{1,0:T(8,128)(2,1)} %copy-done.1, bf16[2304,1024]{1,0:T(8,128)(2,1)} %copy-done.1, bf16[2304,1024]{1,0:T(8,128)(2,1)} %copy-done.1, bf16[16,1024]{1,0:T(8,128)(2,1)} %select_convert_fusion.1.bias_ref, ...), custom_call_target="tpu_custom_call", output_to_operand_aliasing={{}: (7, {})} | custom-call | tf_op jit(solution)/shard_map/pallas_call | solution.py:204
  138.4 3.7 %fusion.8 = bf16[1024,768]{1,0:T(8,128)(2,1)S(1)} fusion(bf16[1024,768]{1,0:T(8,128)(2,1)} %copy-done.2, bf16[768,1024]{1,0:T(8,128)(2,1)} %shard_map.83, bf16[768,768]{1,0:T(8,128)(2,1)} %param.14, pred[1024]{0:T(1024)(128)(4,1)S(1)} %get-tuple-element.39), kind=kOutput, calls=%fused_computation.13 | convolution fusion | flops 1211105280 | bytes 5899264 | tf_op jit(solution)/shard_map/dot_general | solution.py:226
  142.2 2.0 %copy.14 = bf16[128,8,768]{2,1,0:T(8,128)(2,1)} copy(bf16[128,8,768]{2,0,1:T(8,128)(2,1)S(1)} %bitcast.150) | data formatting | bytes 3145728 | tf_op jit(solution)/shard_map/transpose | solution.py:230
  (24 shorter events, 0.3 us)
Async XLA Ops:
  6.5 63.0 %copy-start = (bf16[768,2304]{1,0:T(8,128)(2,1)S(1)}, bf16[768,2304]{1,0:T(8,128)(2,1)}, u32[]{:S(2)}) copy-start(bf16[768,2304]{1,0:T(8,128)(2,1)} %param.13) | copy-start | bytes 10616836
  8.1 14.4 %all-to-all-start = ((s32[32,1,32]{2,1,0:T(1,128)}), s32[32,1,32]{2,1,0:T(1,128)S(1)}, u32[]{:S(2)}, u32[]{:S(2)}) async-start(s32[32,1,32]{2,1,0:T(1,128)} %all_to_all.9), calls=%async_computation | async-start | bytes 32768 | tf_op jit(solution)/shard_map/all_to_all | solution.py:137
  22.5 5.4 %copy-start.3 = (s32[32,1,32]{2,1,0:T(1,128)}, s32[32,1,32]{2,1,0:T(1,128)S(1)}, u32[]{:S(2)}) copy-start(s32[32,1,32]{2,1,0:T(1,128)S(1)} %all-to-all-done) | copy-start | bytes 12292
  22.5 42.9 %all-to-all-start.1 = ((bf16[32,32,768]{2,1,0:T(8,128)(2,1)}), bf16[32,32,768]{2,1,0:T(8,128)(2,1)}, u32[]{:S(2)}, u32[]{:S(2)}) async-start(bf16[32,32,768]{2,1,0:T(8,128)(2,1)} %bitcast.149), calls=%async_computation.1 | async-start | bytes 3145728 | tf_op jit(solution)/shard_map/all_to_all | solution.py:130
  27.7 92.1 %all-gather.2.cloned.1.call-start = ((), (), s32[]{:S(2)}) async-start(), calls=%async_computation.2 | async-start | bytes 3538944 | tf_op jit(solution)/shard_map/all_gather | solution.py:178
  65.4 4.1 %copy-start.5 = (f32[768]{0:T(1024)S(1)}, f32[768]{0:T(1024)}, u32[]{:S(2)}) copy-start(f32[768]{0:T(1024)} %param.12) | copy-start | bytes 9220
  68.9 5.3 %copy-start.2 = (bf16[1024,768]{1,0:T(8,128)(2,1)}, bf16[1024,768]{1,0:T(8,128)(2,1)S(1)}, u32[]{:S(2)}) copy-start(bf16[1024,768]{1,0:T(8,128)(2,1)S(1)} %get-tuple-element.38) | copy-start | bytes 4718596
  69.5 8.3 %copy-start.4 = (s32[16]{0:T(128)S(1)}, s32[16]{0:T(128)}, u32[]{:S(2)}) copy-start(s32[16]{0:T(128)} %constant.81.clone) | copy-start | bytes 196
  74.2 2.1 %copy-start.1 = (bf16[2304,1024]{1,0:T(8,128)(2,1)}, bf16[2304,1024]{1,0:T(8,128)(2,1)S(1)}, u32[]{:S(2)}) copy-start(bf16[2304,1024]{1,0:T(8,128)(2,1)S(1)} %fusion.qt_ref.kt_ref.vt_ref) | copy-start | bytes 14155780
Sparse Core Ops, SparseCore 0:
  77.3 31.9 all-gather.1

commit v8 on v6

--- a/solution.py
+++ b/solution.py
@@ -8,7 +8,7 @@
 from jax.sharding import PartitionSpec as P
 
 HEAD_COUNT = 16
-QUERY_BLOCK = 256
+QUERY_BLOCK = 1024
 PASS1 = 1024
 PASS2 = 512
 DILATION_RATE = 8

time: 149 us -> 138 us (0.926)
  Pallas kernels: 55.3 us -> 44.5 us
    pallas_call x1, Pallas kernels: 40.1 us -> 29.3 us  [body(): pl.pallas_call(functools.partial(nearby_kernel, groups=DILATION_RATE, gro...]
  transfers between devices with their start and end apart: 3 -> 3, of which waited for: 2 -> 3; matrix products, arithmetic and copies ran while one was open for 7% -> 8% of each run, Pallas kernels for 27% -> 21%
where the time goes in v8:
time: 138 us; the launch traced here: 137 us
  Pallas kernels  44.5 us (32%)
  waiting for transfers between devices  36.5 us (26%)
  matrix products  18.2 us (13%)
  between operations  14.3 us (10%)
  starting transfers between devices  12.7 us (9%)
  local copies, waits for them, and re-layouts  6.31 us (5%)
  other arithmetic  4.69 us (3%)
    all_to_all x1, waiting for transfers between devices, body(): lax.all_to_all(projected.reshape(device_count, block_rows, width), ('tile...  35.3 us
    pallas_call x1, Pallas kernels, body(): pl.pallas_call(functools.partial(nearby_kernel, groups=DILATION_RATE, gro...  29.3 us
    pallas_call x1, Pallas kernels, body(): pl.pallas_call(functools.partial(dilated_kernel, factor=factor), grid=(HE...  15.2 us
    all_to_all x1, starting transfers between devices, body(): lax.all_to_all(slot.reshape(device_count, block_rows), ('tile', 'seq'), s...  7.3 us
    dot_general x1, matrix products, body(): jnp.dot(embeddings, in_weight, preferred_element_type=jnp.float32)  6.36 us
    all_to_all x1, starting transfers between devices, body(): lax.all_to_all(projected.reshape(device_count, block_rows, width), ('tile...  5.17 us
    dot_general x1, matrix products, body(): lax.dot_general(qkv_weight, normed, (((0,), (1,)), ((), ())), preferred_e...  4.64 us
    dot_general x1, matrix products, body(): lax.dot_general(attended_t, out_weight, (((0,), (0,)), ((), ())), preferr...  3.73 us
  transfers between devices with their start and end apart: 3, of which 3 were waited for; matrix products, arithmetic and copies ran while one was open for 8% of the time, Pallas kernels for 21%

profile of v8, /device:TPU:0, one launch (start us, length us, event | category | flops | bytes accessed | tf_op | source)
XLA Modules:
  0.0 137.1 jit_solution(16704093692435116430)
XLA Ops:
  6.5 0.0 copy-start
  6.5 1.5 %all_to_all.9 = s32[32,1,32]{2,1,0:T(1,128)} reshape(s32[1024]{0:T(1024)} %param.9) | data formatting | bytes 8192 | tf_op jit(solution)/shard_map/all_to_all | solution.py:128
  8.1 7.3 %all-to-all-start = ((s32[32,1,32]{2,1,0:T(1,128)}), s32[32,1,32]{2,1,0:T(1,128)S(1)}, u32[]{:S(2)}, u32[]{:S(2)}) async-start(s32[32,1,32]{2,1,0:T(1,128)} %all_to_all.9), calls=%async_computation | async-start | bytes 32768 | tf_op jit(solution)/shard_map/all_to_all | solution.py:128
  15.4 6.4 %convolution_convert_fusion.1 = bf16[1024,768]{1,0:T(8,128)(2,1)} fusion(bf16[1024,1536]{1,0:T(8,128)(2,1)} %param.8, bf16[1536,768]{1,0:T(8,128)(2,1)} %param.11), kind=kOutput, calls=%fused_computation.16 | convolution fusion | flops 2416705536 | bytes 7077888 | tf_op jit(solution)/shard_map/dot_general | solution.py:118
  21.7 0.8 all-to-all-done
  22.5 5.2 %all-to-all-start.1 = ((bf16[32,32,768]{2,1,0:T(8,128)(2,1)}), bf16[32,32,768]{2,1,0:T(8,128)(2,1)}, u32[]{:S(2)}, u32[]{:S(2)}) async-start(bf16[32,32,768]{2,1,0:T(8,128)(2,1)} %bitcast.149), calls=%async_computation.1 | async-start | bytes 3145728 | tf_op jit(solution)/shard_map/all_to_all | solution.py:121
  27.7 0.2 all-gather.2.cloned.1.call-start
  27.9 0.0 copy-done.3
  27.9 0.8 subtract_reduce_fusion
  28.7 0.7 sub.34
  29.4 0.7 fusion.25
  30.1 35.3 %all-to-all-done.1 = bf16[32,32,768]{2,1,0:T(8,128)(2,1)} async-done(((bf16[32,32,768]{2,1,0:T(8,128)(2,1)}), bf16[32,32,768]{2,1,0:T(8,128)(2,1)}, u32[]{:S(2)}, u32[]{:S(2)}) %all-to-all-start.1) | async-done | bytes 1572896 | tf_op jit(solution)/shard_map/all_to_all | solution.py:121
  65.4 3.4 %convert_reduce_fusion = (f32[1024]{0:T(1024)S(1)}, bf16[1024,768]{1,0:T(8,128)(2,1)S(1)}) fusion(bf16[1024,768]{1,0:T(8,128)(2,1)} %bitcast.2, s32[1024]{0:T(1024)S(1)} %fusion.25), kind=kOutput, calls=%fused_computation.4 | convolution fusion | flops 1614019584 | bytes 3153920 | tf_op jit(solution)/shard_map/dot_general | solution.py:136
  68.9 0.0 copy-start.2
  68.9 0.6 fusion.4
  69.5 0.0 copy-done
  69.5 0.0 copy-done.5
  69.5 0.0 copy-start.4
  69.5 4.6 %fusion.qt_ref.kt_ref.vt_ref = bf16[2304,1024]{1,0:T(8,128)(2,1)S(1)} fusion(bf16[768,2304]{1,0:T(8,128)(2,1)S(1)} %copy-done, bf16[1024,768]{1,0:T(8,128)(2,1)S(1)} %get-tuple-element.38, f32[768]{0:T(1024)S(1)} %copy-done.5, f32[1024]{0:T(1024)S(1)} %add_rsqrt_fusion, f32[1024]{0:T(1024)S(1)} %broadcast_multiply_fusion), kind=kOutput, calls=%fused_computation.1 | convolution fusion | flops 3630170112 | bytes 9841664 | tf_op jit(solution)/shard_map/dot_general | solution.py:150
  74.2 0.0 copy-done.2
  74.2 0.0 copy-start.1
  74.5 1.8 %copy-done.1 = bf16[2304,1024]{1,0:T(8,128)(2,1)} copy-done((bf16[2304,1024]{1,0:T(8,128)(2,1)}, bf16[2304,1024]{1,0:T(8,128)(2,1)S(1)}, u32[]{:S(2)}) %copy-start.1) | copy-done | bytes 4718616
  76.3 0.8 pad_maximum_fusion
  77.1 0.0 all-gather.2.cloned.1.call-update
  77.9 0.1 add_compare_fusion
  77.9 0.7 select_convert_fusion.1.bias_ref
  78.6 1.0 select_convert_fusion.fbias_ref
  79.7 29.3 %shard_map.82.prev_ref = bf16[768,1024]{1,0:T(8,128)(2,1)} custom-call(bf16[2304,1024]{1,0:T(8,128)(2,1)} %copy-done.1, bf16[2304,1024]{1,0:T(8,128)(2,1)} %copy-done.1, bf16[2304,1024]{1,0:T(8,128)(2,1)} %copy-done.1, bf16[16,1024]{1,0:T(8,128)(2,1)} %select_convert_fusion.1.bias_ref), custom_call_target="tpu_custom_call" | custom-call | tf_op jit(solution)/shard_map/pallas_call | solution.py:183
  109.0 0.3 all-gather.2.cloned.1.call-done.fk_ref.fv_ref
  109.3 15.2 %shard_map.83 = bf16[768,1024]{1,0:T(8,128)(2,1)} custom-call(bf16[2304,1024]{1,0:T(8,128)(2,1)} %copy-done.1, bf16[2304,1024]{1,0:T(8,128)(2,1)} %copy-done.1, bf16[2304,1024]{1,0:T(8,128)(2,1)} %copy-done.1, bf16[16,1024]{1,0:T(8,128)(2,1)} %select_convert_fusion.1.bias_ref, ...), custom_call_target="tpu_custom_call", output_to_operand_aliasing={{}: (7, {})} | custom-call | tf_op jit(solution)/shard_map/pallas_call | solution.py:195
  124.5 3.7 %fusion.8 = bf16[1024,768]{1,0:T(8,128)(2,1)S(1)} fusion(bf16[1024,768]{1,0:T(8,128)(2,1)} %copy-done.2, bf16[768,1024]{1,0:T(8,128)(2,1)} %shard_map.83, bf16[768,768]{1,0:T(8,128)(2,1)} %param.14, pred[1024]{0:T(1024)(128)(4,1)S(1)} %get-tuple-element.39), kind=kOutput, calls=%fused_computation.13 | convolution fusion | flops 1211105280 | bytes 5899264 | tf_op jit(solution)/shard_map/dot_general | solution.py:213
  128.3 2.0 %copy.14 = bf16[128,8,768]{2,1,0:T(8,128)(2,1)} copy(bf16[128,8,768]{2,0,1:T(8,128)(2,1)S(1)} %bitcast.150) | data formatting | bytes 3145728 | tf_op jit(solution)/shard_map/transpose | solution.py:217
  (24 shorter events, 0.3 us)
Async XLA Ops:
  6.5 63.0 %copy-start = (bf16[768,2304]{1,0:T(8,128)(2,1)S(1)}, bf16[768,2304]{1,0:T(8,128)(2,1)}, u32[]{:S(2)}) copy-start(bf16[768,2304]{1,0:T(8,128)(2,1)} %param.13) | copy-start | bytes 10616836
  8.1 14.4 %all-to-all-start = ((s32[32,1,32]{2,1,0:T(1,128)}), s32[32,1,32]{2,1,0:T(1,128)S(1)}, u32[]{:S(2)}, u32[]{:S(2)}) async-start(s32[32,1,32]{2,1,0:T(1,128)} %all_to_all.9), calls=%async_computation | async-start | bytes 32768 | tf_op jit(solution)/shard_map/all_to_all | solution.py:128
  22.5 5.4 %copy-start.3 = (s32[32,1,32]{2,1,0:T(1,128)}, s32[32,1,32]{2,1,0:T(1,128)S(1)}, u32[]{:S(2)}) copy-start(s32[32,1,32]{2,1,0:T(1,128)S(1)} %all-to-all-done) | copy-start | bytes 12292
  22.5 42.9 %all-to-all-start.1 = ((bf16[32,32,768]{2,1,0:T(8,128)(2,1)}), bf16[32,32,768]{2,1,0:T(8,128)(2,1)}, u32[]{:S(2)}, u32[]{:S(2)}) async-start(bf16[32,32,768]{2,1,0:T(8,128)(2,1)} %bitcast.149), calls=%async_computation.1 | async-start | bytes 3145728 | tf_op jit(solution)/shard_map/all_to_all | solution.py:121
  27.7 81.6 %all-gather.2.cloned.1.call-start = ((), (), s32[]{:S(2)}) async-start(), calls=%async_computation.2 | async-start | bytes 3538944 | tf_op jit(solution)/shard_map/all_gather | solution.py:169
  65.4 4.1 %copy-start.5 = (f32[768]{0:T(1024)S(1)}, f32[768]{0:T(1024)}, u32[]{:S(2)}) copy-start(f32[768]{0:T(1024)} %param.12) | copy-start | bytes 9220
  68.9 5.3 %copy-start.2 = (bf16[1024,768]{1,0:T(8,128)(2,1)}, bf16[1024,768]{1,0:T(8,128)(2,1)S(1)}, u32[]{:S(2)}) copy-start(bf16[1024,768]{1,0:T(8,128)(2,1)S(1)} %get-tuple-element.38) | copy-start | bytes 4718596
  69.5 8.3 %copy-start.4 = (s32[16]{0:T(128)S(1)}, s32[16]{0:T(128)}, u32[]{:S(2)}) copy-start(s32[16]{0:T(128)} %constant.81.clone) | copy-start | bytes 196
  74.2 2.1 %copy-start.1 = (bf16[2304,1024]{1,0:T(8,128)(2,1)}, bf16[2304,1024]{1,0:T(8,128)(2,1)S(1)}, u32[]{:S(2)}) copy-start(bf16[2304,1024]{1,0:T(8,128)(2,1)S(1)} %fusion.qt_ref.kt_ref.vt_ref) | copy-start | bytes 14155780
Sparse Core Ops, SparseCore 0:
  77.3 31.9 all-gather.1

commit v9 on v8

--- a/solution.py
+++ b/solution.py
@@ -83,24 +83,25 @@
     qt_ref, kt_ref, vt_ref, bias_ref, fk_ref, fv_ref, fbias_ref, prev_ref, o_ref, *, factor
 ):
     del prev_ref
-    queries_t = extend(qt_ref[...], ones_row(qt_ref.shape[1]))
-    near_keys = extend(kt_ref[...], bias_ref[...]).T
-    far_keys = extend(fk_ref[0, 0], fbias_ref[0]).T
-    near = jnp.dot(near_keys, queries_t, preferred_element_type=jnp.float32)
-    far = jnp.dot(far_keys, queries_t, preferred_element_type=jnp.float32)
-    top = jnp.maximum(
-        jnp.max(near, axis=0, keepdims=True), jnp.max(far, axis=0, keepdims=True)
-    )
-    near_w = jnp.exp2((near - top) * factor)
-    far_w = jnp.exp2((far - top) * factor)
-    total = jnp.sum(near_w, axis=0, keepdims=True) + jnp.sum(far_w, axis=0, keepdims=True)
-    summed_t = jnp.dot(
-        vt_ref[...], near_w.astype(jnp.bfloat16), preferred_element_type=jnp.float32
-    )
-    summed_t = summed_t + jnp.dot(
-        fv_ref[0, 0], far_w.astype(jnp.bfloat16), preferred_element_type=jnp.float32
-    )
-    o_ref[...] = (summed_t / total).astype(o_ref.dtype)
+    for pair in range(2):
+        queries_t = extend(qt_ref[pair], ones_row(qt_ref.shape[2]))
+        near_keys = extend(kt_ref[pair], bias_ref[...]).T
+        far_keys = extend(fk_ref[0, pair, 0], fbias_ref[0]).T
+        near = jnp.dot(near_keys, queries_t, preferred_element_type=jnp.float32)
+        far = jnp.dot(far_keys, queries_t, preferred_element_type=jnp.float32)
+        top = jnp.maximum(
+            jnp.max(near, axis=0, keepdims=True), jnp.max(far, axis=0, keepdims=True)
+        )
+        near_w = jnp.exp2((near - top) * factor)
+        far_w = jnp.exp2((far - top) * factor)
+        total = jnp.sum(near_w, axis=0, keepdims=True) + jnp.sum(far_w, axis=0, keepdims=True)
+        summed_t = jnp.dot(
+            vt_ref[pair], near_w.astype(jnp.bfloat16), preferred_element_type=jnp.float32
+        )
+        summed_t = summed_t + jnp.dot(
+            fv_ref[0, pair, 0], far_w.astype(jnp.bfloat16), preferred_element_type=jnp.float32
+        )
+        o_ref[pair] = (summed_t / total).astype(o_ref.dtype)
 
 
 def body(embeddings, slot, lengths, in_weight, norm_gain, qkv_weight, out_weight):
@@ -191,24 +192,33 @@
         scratch_shapes=[pltpu.VMEM((rows, head_size + 16), jnp.bfloat16)],
     )(projected_t, projected_t, projected_t, near_bias)
 
-    group_block = pl.BlockSpec((head_size, group_rows), lambda h: (h, h % DILATION_RATE))
+    half = HEAD_COUNT // 2
+    paired = projected_t.reshape(6, half * head_size, rows)
+    far_paired = far.reshape(2, 2, half, head_size, far_count)
+    group_block = pl.BlockSpec(
+        (2, head_size, group_rows), lambda i: (0, i, i % DILATION_RATE)
+    )
+    far_block = (1, 2, 1, head_size, far_count)
     attended_t = pl.pallas_call(
         functools.partial(dilated_kernel, factor=factor),
-        grid=(HEAD_COUNT,),
+        grid=(half,),
         in_specs=[
-            group_block,
-            keys_block,
-            values_block,
+            pl.BlockSpec((2, head_size, group_rows), lambda i: (0, i, i % DILATION_RATE)),
+            pl.BlockSpec((2, head_size, rows), lambda i: (1, i, 0)),
+            pl.BlockSpec((2, head_size, rows), lambda i: (2, i, 0)),
             bias_block,
-            pl.BlockSpec((1, 1, head_size, far_count), lambda h: (0, h, 0, 0)),
-            pl.BlockSpec((1, 1, head_size, far_count), lambda h: (1, h, 0, 0)),
-            pl.BlockSpec((1, 16, far_count), lambda h: (h, 0, 0)),
+            pl.BlockSpec(far_block, lambda i: (0, 0, i, 0, 0)),
+            pl.BlockSpec(far_block, lambda i: (1, 0, i, 0, 0)),
+            pl.BlockSpec((1, 16, far_count), lambda i: (i, 0, 0)),
             pl.BlockSpec(memory_space=pl.ANY),
         ],
         out_specs=group_block,
-        out_shape=jax.ShapeDtypeStruct((width, rows), jnp.bfloat16),
+        out_shape=jax.ShapeDtypeStruct((2, half * head_size, rows), jnp.bfloat16),
         input_output_aliases={7: 0},
-    )(projected_t, projected_t, projected_t, near_bias, far, far, far_bias, nearby)
+    )(
+        paired, paired, paired, near_bias, far_paired, far_paired, far_bias,
+        nearby.reshape(2, half * head_size, rows),
+    ).reshape(width, rows)
 
     output = lax.dot_general(
         attended_t, out_weight, (((0,), (0,)), ((), ())), preferred_element_type=jnp.float32

time: 138 us -> 134 us (0.971)
  Pallas kernels: 44.5 us -> 40.7 us
    pallas_call x1, Pallas kernels: 15.2 us -> 11.4 us  [body(): pl.pallas_call(functools.partial(dilated_kernel, factor=factor), grid=(ha...]
  transfers between devices with their start and end apart: 3 -> 3, of which waited for: 3 -> 3; matrix products, arithmetic and copies ran while one was open for 8% -> 8% of each run, Pallas kernels for 21% -> 22%
where the time goes in v9:
time: 134 us; the launch traced here: 133 us
  Pallas kernels  40.7 us (30%)
  waiting for transfers between devices  36.5 us (27%)
  matrix products  18.2 us (14%)
  between operations  14.3 us (11%)
  starting transfers between devices  12.7 us (9%)
  local copies, waits for them, and re-layouts  6.29 us (5%)
  other arithmetic  4.66 us (3%)
    all_to_all x1, waiting for transfers between devices, body(): lax.all_to_all(projected.reshape(device_count, block_rows, width), ('tile...  35.4 us
    pallas_call x1, Pallas kernels, body(): pl.pallas_call(functools.partial(nearby_kernel, groups=DILATION_RATE, gro...  29.3 us
    pallas_call x1, Pallas kernels, body(): pl.pallas_call(functools.partial(dilated_kernel, factor=factor), grid=(ha...  11.4 us
    all_to_all x1, starting transfers between devices, body(): lax.all_to_all(slot.reshape(device_count, block_rows), ('tile', 'seq'), s...  7.3 us
    dot_general x1, matrix products, body(): jnp.dot(embeddings, in_weight, preferred_element_type=jnp.float32)  6.36 us
    all_to_all x1, starting transfers between devices, body(): lax.all_to_all(projected.reshape(device_count, block_rows, width), ('tile...  5.16 us
    dot_general x1, matrix products, body(): lax.dot_general(qkv_weight, normed, (((0,), (1,)), ((), ())), preferred_e...  4.64 us
    dot_general x1, matrix products, body(): lax.dot_general(attended_t, out_weight, (((0,), (0,)), ((), ())), preferr...  3.73 us
  transfers between devices with their start and end apart: 3, of which 3 were waited for; matrix products, arithmetic and copies ran while one was open for 8% of the time, Pallas kernels for 22%

profile of v9, /device:TPU:0, one launch (start us, length us, event | category | flops | bytes accessed | tf_op | source)
XLA Modules:
  0.0 133.3 jit_solution(8584673253533573782)
XLA Ops:
  6.5 0.0 copy-start
  6.5 1.5 %all_to_all.9 = s32[32,1,32]{2,1,0:T(1,128)} reshape(s32[1024]{0:T(1024)} %param.9) | data formatting | bytes 8192 | tf_op jit(solution)/shard_map/all_to_all | solution.py:129
  8.1 7.3 %all-to-all-start = ((s32[32,1,32]{2,1,0:T(1,128)}), s32[32,1,32]{2,1,0:T(1,128)S(1)}, u32[]{:S(2)}, u32[]{:S(2)}) async-start(s32[32,1,32]{2,1,0:T(1,128)} %all_to_all.9), calls=%async_computation | async-start | bytes 32768 | tf_op jit(solution)/shard_map/all_to_all | solution.py:129
  15.4 6.4 %convolution_convert_fusion.1 = bf16[1024,768]{1,0:T(8,128)(2,1)} fusion(bf16[1024,1536]{1,0:T(8,128)(2,1)} %param.8, bf16[1536,768]{1,0:T(8,128)(2,1)} %param.11), kind=kOutput, calls=%fused_computation.15 | convolution fusion | flops 2416705536 | bytes 7077888 | tf_op jit(solution)/shard_map/dot_general | solution.py:119
  21.7 0.8 all-to-all-done
  22.5 5.2 %all-to-all-start.1 = ((bf16[32,32,768]{2,1,0:T(8,128)(2,1)}), bf16[32,32,768]{2,1,0:T(8,128)(2,1)}, u32[]{:S(2)}, u32[]{:S(2)}) async-start(bf16[32,32,768]{2,1,0:T(8,128)(2,1)} %bitcast.180), calls=%async_computation.1 | async-start | bytes 3145728 | tf_op jit(solution)/shard_map/all_to_all | solution.py:122
  27.7 0.2 all-gather.2.cloned.1.call-start
  27.9 0.0 copy-done.3
  27.9 0.8 subtract_reduce_fusion
  28.7 0.7 sub.34
  29.4 0.7 fusion.24
  30.0 35.4 %all-to-all-done.1 = bf16[32,32,768]{2,1,0:T(8,128)(2,1)} async-done(((bf16[32,32,768]{2,1,0:T(8,128)(2,1)}), bf16[32,32,768]{2,1,0:T(8,128)(2,1)}, u32[]{:S(2)}, u32[]{:S(2)}) %all-to-all-start.1) | async-done | bytes 1572896 | tf_op jit(solution)/shard_map/all_to_all | solution.py:122
  65.4 3.4 %convert_reduce_fusion = (f32[1024]{0:T(1024)S(1)}, bf16[1024,768]{1,0:T(8,128)(2,1)S(1)}) fusion(bf16[1024,768]{1,0:T(8,128)(2,1)} %bitcast.2, s32[1024]{0:T(1024)S(1)} %fusion.24), kind=kOutput, calls=%fused_computation.3 | convolution fusion | flops 1614019584 | bytes 3153920 | tf_op jit(solution)/shard_map/dot_general | solution.py:137
  68.9 0.0 copy-start.2
  68.9 0.6 fusion.3
  69.5 0.0 copy-done
  69.5 0.0 copy-done.5
  69.5 0.0 copy-start.4
  69.5 4.6 %convolution_convert_fusion = bf16[1024,2304]{0,1:T(8,128)(2,1)S(1)} fusion(bf16[768,2304]{1,0:T(8,128)(2,1)S(1)} %copy-done, bf16[1024,768]{1,0:T(8,128)(2,1)S(1)} %get-tuple-element.38, f32[768]{0:T(1024)S(1)} %copy-done.5, f32[1024]{0:T(1024)S(1)} %add_rsqrt_fusion, f32[1024]{0:T(1024)S(1)} %broadcast_multiply_fusion), kind=kOutput, calls=%fused_computation | convolution fusion | flops 3630170112 | bytes 9841664 | tf_op jit(solution)/shard_map/dot_general | solution.py:151
  74.2 0.0 copy-done.2
  74.2 0.0 copy-start.1
  74.5 1.8 %copy-done.1 = bf16[1024,2304]{0,1:T(8,128)(2,1)} copy-done((bf16[1024,2304]{0,1:T(8,128)(2,1)}, bf16[1024,2304]{0,1:T(8,128)(2,1)S(1)}, u32[]{:S(2)}) %copy-start.1) | copy-done | bytes 4718616
  76.3 0.8 pad_maximum_fusion
  77.1 0.0 all-gather.2.cloned.1.call-update
  77.9 0.1 add_compare_fusion
  78.0 0.7 select_convert_fusion.1.bias_ref
  78.6 1.0 select_convert_fusion.fbias_ref
  79.7 29.3 %shard_map.82 = bf16[768,1024]{1,0:T(8,128)(2,1)} custom-call(bf16[2304,1024]{1,0:T(8,128)(2,1)} %bitcast.170, bf16[2304,1024]{1,0:T(8,128)(2,1)} %bitcast.171, bf16[2304,1024]{1,0:T(8,128)(2,1)} %bitcast.172, bf16[16,1024]{1,0:T(8,128)(2,1)} %select_convert_fusion.1.bias_ref), custom_call_target="tpu_custom_call" | custom-call | tf_op jit(solution)/shard_map/pallas_call | solution.py:184
  109.0 0.3 all-gather.2.cloned.1.call-done
  109.3 11.4 %shard_map.83 = bf16[2,384,1024]{2,1,0:T(8,128)(2,1)} custom-call(bf16[6,384,1024]{2,1,0:T(8,128)(2,1)} %bitcast.173, bf16[6,384,1024]{2,1,0:T(8,128)(2,1)} %bitcast.174, bf16[6,384,1024]{2,1,0:T(8,128)(2,1)} %bitcast.175, bf16[16,1024]{1,0:T(8,128)(2,1)} %select_convert_fusion.1.bias_ref, ...), custom_call_target="tpu_custom_call", output_to_operand_aliasing={{}: (7, {})} | custom-call | tf_op jit(solution)/shard_map/pallas_call | solution.py:202
  120.7 3.7 %fusion.7 = bf16[1024,768]{1,0:T(8,128)(2,1)S(1)} fusion(bf16[1024,768]{1,0:T(8,128)(2,1)} %copy-done.2, bf16[768,1024]{1,0:T(8,128)(2,1)} %bitcast.179, bf16[768,768]{1,0:T(8,128)(2,1)} %param.14, pred[1024]{0:T(1024)(128)(4,1)S(1)} %fusion.22), kind=kOutput, calls=%fused_computation.12 | convolution fusion | flops 1211105280 | bytes 5899264 | tf_op jit(solution)/shard_map/dot_general | solution.py:223
  124.4 2.0 %copy.14 = bf16[128,8,768]{2,1,0:T(8,128)(2,1)} copy(bf16[128,8,768]{2,0,1:T(8,128)(2,1)S(1)} %bitcast.181) | data formatting | bytes 3145728 | tf_op jit(solution)/shard_map/transpose | solution.py:227
  (25 shorter events, 0.3 us)
Async XLA Ops:
  6.5 63.0 %copy-start = (bf16[768,2304]{1,0:T(8,128)(2,1)S(1)}, bf16[768,2304]{1,0:T(8,128)(2,1)}, u32[]{:S(2)}) copy-start(bf16[768,2304]{1,0:T(8,128)(2,1)} %param.13) | copy-start | bytes 10616836
  8.1 14.5 %all-to-all-start = ((s32[32,1,32]{2,1,0:T(1,128)}), s32[32,1,32]{2,1,0:T(1,128)S(1)}, u32[]{:S(2)}, u32[]{:S(2)}) async-start(s32[32,1,32]{2,1,0:T(1,128)} %all_to_all.9), calls=%async_computation | async-start | bytes 32768 | tf_op jit(solution)/shard_map/all_to_all | solution.py:129
  22.5 5.4 %copy-start.3 = (s32[32,1,32]{2,1,0:T(1,128)}, s32[32,1,32]{2,1,0:T(1,128)S(1)}, u32[]{:S(2)}) copy-start(s32[32,1,32]{2,1,0:T(1,128)S(1)} %all-to-all-done) | copy-start | bytes 12292
  22.5 42.9 %all-to-all-start.1 = ((bf16[32,32,768]{2,1,0:T(8,128)(2,1)}), bf16[32,32,768]{2,1,0:T(8,128)(2,1)}, u32[]{:S(2)}, u32[]{:S(2)}) async-start(bf16[32,32,768]{2,1,0:T(8,128)(2,1)} %bitcast.180), calls=%async_computation.1 | async-start | bytes 3145728 | tf_op jit(solution)/shard_map/all_to_all | solution.py:122
  27.7 81.6 %all-gather.2.cloned.1.call-start = ((), (), s32[]{:S(2)}) async-start(), calls=%async_computation.2 | async-start | bytes 3538944 | tf_op jit(solution)/shard_map/all_gather | solution.py:170
  65.4 4.1 %copy-start.5 = (f32[768]{0:T(1024)S(1)}, f32[768]{0:T(1024)}, u32[]{:S(2)}) copy-start(f32[768]{0:T(1024)} %param.12) | copy-start | bytes 9220
  68.9 5.3 %copy-start.2 = (bf16[1024,768]{1,0:T(8,128)(2,1)}, bf16[1024,768]{1,0:T(8,128)(2,1)S(1)}, u32[]{:S(2)}) copy-start(bf16[1024,768]{1,0:T(8,128)(2,1)S(1)} %get-tuple-element.38) | copy-start | bytes 4718596
  69.5 8.3 %copy-start.4 = (s32[16]{0:T(128)S(1)}, s32[16]{0:T(128)}, u32[]{:S(2)}) copy-start(s32[16]{0:T(128)} %constant.81.clone) | copy-start | bytes 196
  74.2 2.1 %copy-start.1 = (bf16[1024,2304]{0,1:T(8,128)(2,1)}, bf16[1024,2304]{0,1:T(8,128)(2,1)S(1)}, u32[]{:S(2)}) copy-start(bf16[1024,2304]{0,1:T(8,128)(2,1)S(1)} %convolution_convert_fusion) | copy-start | bytes 14155780
Sparse Core Ops, SparseCore 0:
  77.3 31.9 all-gather.1

commit v10 on v9

--- a/solution.py
+++ b/solution.py
@@ -79,6 +79,10 @@
         o_ref[:, rows] = (summed_t / total).astype(o_ref.dtype)
 
 
+def joined(ref, pair):
+    return jnp.concatenate([ref[chunk, 0, pair, 0] for chunk in range(ref.shape[0])], axis=1)
+
+
 def dilated_kernel(
     qt_ref, kt_ref, vt_ref, bias_ref, fk_ref, fv_ref, fbias_ref, prev_ref, o_ref, *, factor
 ):
@@ -86,7 +90,7 @@
     for pair in range(2):
         queries_t = extend(qt_ref[pair], ones_row(qt_ref.shape[2]))
         near_keys = extend(kt_ref[pair], bias_ref[...]).T
-        far_keys = extend(fk_ref[0, pair, 0], fbias_ref[0]).T
+        far_keys = extend(joined(fk_ref, pair), fbias_ref[0]).T
         near = jnp.dot(near_keys, queries_t, preferred_element_type=jnp.float32)
         far = jnp.dot(far_keys, queries_t, preferred_element_type=jnp.float32)
         top = jnp.maximum(
@@ -99,7 +103,7 @@
             vt_ref[pair], near_w.astype(jnp.bfloat16), preferred_element_type=jnp.float32
         )
         summed_t = summed_t + jnp.dot(
-            fv_ref[0, pair, 0], far_w.astype(jnp.bfloat16), preferred_element_type=jnp.float32
+            joined(fv_ref, pair), far_w.astype(jnp.bfloat16), preferred_element_type=jnp.float32
         )
         o_ref[pair] = (summed_t / total).astype(o_ref.dtype)
 
@@ -167,7 +171,13 @@
             for part in (1, 2)
         ]
     )
-    far = lax.all_gather(own_far, "seq", axis=3, tiled=True)
+    far = lax.all_to_all(
+        jnp.broadcast_to(own_far[None], (seq_count,) + own_far.shape),
+        "seq",
+        split_axis=0,
+        concat_axis=0,
+        tiled=True,
+    )
     far_position = (
         jnp.arange(far_count, dtype=jnp.int32)[None, :] * DILATION_RATE
         + jnp.asarray(offsets, jnp.int32)[:, None]
@@ -194,11 +204,11 @@
 
     half = HEAD_COUNT // 2
     paired = projected_t.reshape(6, half * head_size, rows)
-    far_paired = far.reshape(2, 2, half, head_size, far_count)
+    far_paired = far.reshape(seq_count, 2, 2, half, head_size, group_rows)
     group_block = pl.BlockSpec(
         (2, head_size, group_rows), lambda i: (0, i, i % DILATION_RATE)
     )
-    far_block = (1, 2, 1, head_size, far_count)
+    far_block = (seq_count, 1, 2, 1, head_size, group_rows)
     attended_t = pl.pallas_call(
         functools.partial(dilated_kernel, factor=factor),
         grid=(half,),
@@ -207,8 +217,8 @@
             pl.BlockSpec((2, head_size, rows), lambda i: (1, i, 0)),
             pl.BlockSpec((2, head_size, rows), lambda i: (2, i, 0)),
             bias_block,
-            pl.BlockSpec(far_block, lambda i: (0, 0, i, 0, 0)),
-            pl.BlockSpec(far_block, lambda i: (1, 0, i, 0, 0)),
+            pl.BlockSpec(far_block, lambda i: (0, 0, 0, i, 0, 0)),
+            pl.BlockSpec(far_block, lambda i: (0, 1, 0, i, 0, 0)),
             pl.BlockSpec((1, 16, far_count), lambda i: (i, 0, 0)),
             pl.BlockSpec(memory_space=pl.ANY),
         ],

time: 134 us -> 132 us (0.985)
  between operations: 14.3 us -> 0.88 us
  waiting for transfers between devices: 36.5 us -> 42.2 us
  starting transfers between devices: 12.7 us -> 17.2 us
  local copies, waits for them, and re-layouts: 6.29 us -> 8.64 us
    all_to_all x0 -> x1, waiting for transfers between devices: none -> 5.85 us  [body(): lax.all_to_all(jnp.broadcast_to(own_far[None], (seq_count,) + own_far.sha...]
    all_to_all x0 -> x1, starting transfers between devices: none -> 4.76 us  [body(): lax.all_to_all(jnp.broadcast_to(own_far[None], (seq_count,) + own_far.sha...]
    broadcast_in_dim x0 -> x1, local copies, waits for them, and re-layouts: none -> 2.36 us  [body(): jnp.broadcast_to(own_far[None], (seq_count,) + own_far.shape)]
where the time goes in v10:
time: 132 us
  waiting for transfers between devices  42.2 us (32%)
  Pallas kernels  40.6 us (31%)
  matrix products  18.2 us (14%)
  starting transfers between devices  17.2 us (13%)
  local copies, waits for them, and re-layouts  8.64 us (7%)
  other arithmetic  3.96 us (3%)
    all_to_all x1, waiting for transfers between devices, body(): lax.all_to_all(projected.reshape(device_count, block_rows, width), ('tile...  35.6 us
    pallas_call x1, Pallas kernels, body(): pl.pallas_call(functools.partial(nearby_kernel, groups=DILATION_RATE, gro...  29.3 us
    pallas_call x1, Pallas kernels, body(): pl.pallas_call(functools.partial(dilated_kernel, factor=factor), grid=(ha...  11.3 us
    all_to_all x1, starting transfers between devices, body(): lax.all_to_all(slot.reshape(device_count, block_rows), ('tile', 'seq'), s...  7.3 us
    dot_general x1, matrix products, body(): jnp.dot(embeddings, in_weight, preferred_element_type=jnp.float32)  6.36 us
    all_to_all x1, waiting for transfers between devices, body(): lax.all_to_all(jnp.broadcast_to(own_far[None], (seq_count,) + own_far.sha...  5.85 us
    all_to_all x1, starting transfers between devices, body(): lax.all_to_all(projected.reshape(device_count, block_rows, width), ('tile...  5.16 us
    all_to_all x1, starting transfers between devices, body(): lax.all_to_all(jnp.broadcast_to(own_far[None], (seq_count,) + own_far.sha...  4.76 us
  transfers between devices with their start and end apart: 3, of which 3 were waited for; matrix products, arithmetic and copies ran while one was open for 8% of the time, Pallas kernels for 22%

profile of v10, /device:TPU:0, one launch (start us, length us, event | category | flops | bytes accessed | tf_op | source)
XLA Modules:
  0.0 131.7 jit_solution(11110224673410278580)
XLA Ops:
  0.0 0.0 copy-start
  0.0 1.5 %all_to_all.12 = s32[32,1,32]{2,1,0:T(1,128)} reshape(s32[1024]{0:T(1024)} %param.9) | data formatting | bytes 8192 | tf_op jit(solution)/shard_map/all_to_all | solution.py:133
  1.5 7.3 %all-to-all-start = ((s32[32,1,32]{2,1,0:T(1,128)}), s32[32,1,32]{2,1,0:T(1,128)S(1)}, u32[]{:S(2)}, u32[]{:S(2)}) async-start(s32[32,1,32]{2,1,0:T(1,128)} %all_to_all.12), calls=%async_computation | async-start | bytes 32768 | tf_op jit(solution)/shard_map/all_to_all | solution.py:133
  8.8 6.4 %convolution_convert_fusion.1 = bf16[1024,768]{1,0:T(8,128)(2,1)} fusion(bf16[1024,1536]{1,0:T(8,128)(2,1)} %param.8, bf16[1536,768]{1,0:T(8,128)(2,1)} %param.11), kind=kOutput, calls=%fused_computation.15 | convolution fusion | flops 2416705536 | bytes 7077888 | tf_op jit(solution)/shard_map/dot_general | solution.py:123
  15.2 0.8 all-to-all-done
  16.0 0.0 copy-start.3
  16.0 5.2 %all-to-all-start.1 = ((bf16[32,32,768]{2,1,0:T(8,128)(2,1)}), bf16[32,32,768]{2,1,0:T(8,128)(2,1)}, u32[]{:S(2)}, u32[]{:S(2)}) async-start(bf16[32,32,768]{2,1,0:T(8,128)(2,1)} %bitcast.178), calls=%async_computation.1 | async-start | bytes 3145728 | tf_op jit(solution)/shard_map/all_to_all | solution.py:126
  21.2 0.0 copy-done.3
  21.2 0.8 subtract_reduce_fusion
  21.9 0.7 sub.34
  22.6 0.7 fusion.24
  23.3 35.6 %all-to-all-done.1 = bf16[32,32,768]{2,1,0:T(8,128)(2,1)} async-done(((bf16[32,32,768]{2,1,0:T(8,128)(2,1)}), bf16[32,32,768]{2,1,0:T(8,128)(2,1)}, u32[]{:S(2)}, u32[]{:S(2)}) %all-to-all-start.1) | async-done | bytes 1572896 | tf_op jit(solution)/shard_map/all_to_all | solution.py:126
  58.9 3.4 %convert_reduce_fusion = (f32[1024]{0:T(1024)S(1)}, bf16[1024,768]{1,0:T(8,128)(2,1)S(1)}) fusion(bf16[1024,768]{1,0:T(8,128)(2,1)} %bitcast.2, s32[1024]{0:T(1024)S(1)} %fusion.24), kind=kOutput, calls=%fused_computation.3 | convolution fusion | flops 1614019584 | bytes 3153920 | tf_op jit(solution)/shard_map/dot_general | solution.py:141
  62.3 0.0 copy-start.2
  62.3 0.6 fusion.3
  63.0 0.0 copy-done
  63.0 0.0 copy-done.5
  63.0 4.6 %convolution_convert_fusion = bf16[1024,2304]{0,1:T(8,128)(2,1)S(1)} fusion(bf16[768,2304]{1,0:T(8,128)(2,1)S(1)} %copy-done, bf16[1024,768]{1,0:T(8,128)(2,1)S(1)} %get-tuple-element.38, f32[768]{0:T(1024)S(1)} %copy-done.5, f32[1024]{0:T(1024)S(1)} %add_rsqrt_fusion, f32[1024]{0:T(1024)S(1)} %broadcast_multiply_fusion), kind=kOutput, calls=%fused_computation | convolution fusion | flops 3630170112 | bytes 9841664 | tf_op jit(solution)/shard_map/dot_general | solution.py:155
  67.6 0.0 copy-done.2
  67.6 0.0 copy-start.1
  68.0 1.8 %copy-done.1 = bf16[1024,2304]{0,1:T(8,128)(2,1)} copy-done((bf16[1024,2304]{0,1:T(8,128)(2,1)}, bf16[1024,2304]{0,1:T(8,128)(2,1)S(1)}, u32[]{:S(2)}) %copy-start.1) | copy-done | bytes 4718616
  69.8 2.4 %broadcast_in_dim.48 = bf16[8,2,16,48,128]{4,3,2,1,0:T(8,128)(2,1)} broadcast(bf16[2,16,48,128]{3,2,1,0:T(8,128)(2,1)S(1)} %pad_maximum_fusion), dimensions={1,2,3,4} | broadcast | bytes 3538944 | tf_op jit(solution)/shard_map/broadcast_in_dim | solution.py:175
  72.2 4.8 %all-to-all-start.2 = ((bf16[8,2,16,48,128]{4,3,2,1,0:T(8,128)(2,1)}), bf16[8,2,16,48,128]{4,3,2,1,0:T(8,128)(2,1)}, u32[]{:S(2)}, u32[]{:S(2)}) async-start(bf16[8,2,16,48,128]{4,3,2,1,0:T(8,128)(2,1)} %broadcast_in_dim.48), calls=%async_computation.2 | async-start | bytes 6291456 | tf_op jit(solution)/shard_map/all_to_all | solution.py:174
  77.7 0.0 copy-done.4
  77.7 0.1 add_compare_fusion
  77.8 0.7 select_convert_fusion.1.bias_ref
  78.4 1.0 select_convert_fusion.fbias_ref
  79.5 29.3 %shard_map.82 = bf16[768,1024]{1,0:T(8,128)(2,1)} custom-call(bf16[2304,1024]{1,0:T(8,128)(2,1)} %bitcast.170, bf16[2304,1024]{1,0:T(8,128)(2,1)} %bitcast.171, bf16[2304,1024]{1,0:T(8,128)(2,1)} %bitcast.172, bf16[16,1024]{1,0:T(8,128)(2,1)} %select_convert_fusion.1.bias_ref), custom_call_target="tpu_custom_call" | custom-call | tf_op jit(solution)/shard_map/pallas_call | solution.py:194
  108.8 5.8 %all-to-all-done.2 = bf16[8,2,16,48,128]{4,3,2,1,0:T(8,128)(2,1)} async-done(((bf16[8,2,16,48,128]{4,3,2,1,0:T(8,128)(2,1)}), bf16[8,2,16,48,128]{4,3,2,1,0:T(8,128)(2,1)}, u32[]{:S(2)}, u32[]{:S(2)}) %all-to-all-start.2) | async-done | bytes 3145760 | tf_op jit(solution)/shard_map/all_to_all | solution.py:174
  114.7 11.3 %shard_map.83 = bf16[2,384,1024]{2,1,0:T(8,128)(2,1)} custom-call(bf16[6,384,1024]{2,1,0:T(8,128)(2,1)} %bitcast.173, bf16[6,384,1024]{2,1,0:T(8,128)(2,1)} %bitcast.174, bf16[6,384,1024]{2,1,0:T(8,128)(2,1)} %bitcast.175, bf16[16,1024]{1,0:T(8,128)(2,1)} %select_convert_fusion.1.bias_ref, ...), custom_call_target="tpu_custom_call", output_to_operand_aliasing={{}: (7, {})} | custom-call | tf_op jit(solution)/shard_map/pallas_call | solution.py:212
  126.0 3.7 %fusion.7 = bf16[1024,768]{1,0:T(8,128)(2,1)S(1)} fusion(bf16[1024,768]{1,0:T(8,128)(2,1)} %copy-done.2, bf16[768,1024]{1,0:T(8,128)(2,1)} %bitcast.177, bf16[768,768]{1,0:T(8,128)(2,1)} %param.14, pred[1024]{0:T(1024)(128)(4,1)S(1)} %fusion.22), kind=kOutput, calls=%fused_computation.12 | convolution fusion | flops 1211105280 | bytes 5899264 | tf_op jit(solution)/shard_map/dot_general | solution.py:233
  129.7 2.0 %copy.14 = bf16[128,8,768]{2,1,0:T(8,128)(2,1)} copy(bf16[128,8,768]{2,0,1:T(8,128)(2,1)S(1)} %bitcast.179) | data formatting | bytes 3145728 | tf_op jit(solution)/shard_map/transpose | solution.py:237
  (25 shorter events, 0.4 us)
Async XLA Ops:
  0.0 63.0 %copy-start = (bf16[768,2304]{1,0:T(8,128)(2,1)S(1)}, bf16[768,2304]{1,0:T(8,128)(2,1)}, u32[]{:S(2)}) copy-start(bf16[768,2304]{1,0:T(8,128)(2,1)} %param.13) | copy-start | bytes 10616836
  1.5 14.5 %all-to-all-start = ((s32[32,1,32]{2,1,0:T(1,128)}), s32[32,1,32]{2,1,0:T(1,128)S(1)}, u32[]{:S(2)}, u32[]{:S(2)}) async-start(s32[32,1,32]{2,1,0:T(1,128)} %all_to_all.12), calls=%async_computation | async-start | bytes 32768 | tf_op jit(solution)/shard_map/all_to_all | solution.py:133
  16.0 5.2 %copy-start.3 = (s32[32,1,32]{2,1,0:T(1,128)}, s32[32,1,32]{2,1,0:T(1,128)S(1)}, u32[]{:S(2)}) copy-start(s32[32,1,32]{2,1,0:T(1,128)S(1)} %all-to-all-done) | copy-start | bytes 12292
  16.0 42.9 %all-to-all-start.1 = ((bf16[32,32,768]{2,1,0:T(8,128)(2,1)}), bf16[32,32,768]{2,1,0:T(8,128)(2,1)}, u32[]{:S(2)}, u32[]{:S(2)}) async-start(bf16[32,32,768]{2,1,0:T(8,128)(2,1)} %bitcast.178), calls=%async_computation.1 | async-start | bytes 3145728 | tf_op jit(solution)/shard_map/all_to_all | solution.py:126
  58.9 4.1 %copy-start.5 = (f32[768]{0:T(1024)S(1)}, f32[768]{0:T(1024)}, u32[]{:S(2)}) copy-start(f32[768]{0:T(1024)} %param.12) | copy-start | bytes 9220
  62.3 5.3 %copy-start.2 = (bf16[1024,768]{1,0:T(8,128)(2,1)}, bf16[1024,768]{1,0:T(8,128)(2,1)S(1)}, u32[]{:S(2)}) copy-start(bf16[1024,768]{1,0:T(8,128)(2,1)S(1)} %get-tuple-element.38) | copy-start | bytes 4718596
  67.6 2.1 %copy-start.1 = (bf16[1024,2304]{0,1:T(8,128)(2,1)}, bf16[1024,2304]{0,1:T(8,128)(2,1)S(1)}, u32[]{:S(2)}) copy-start(bf16[1024,2304]{0,1:T(8,128)(2,1)S(1)} %convolution_convert_fusion) | copy-start | bytes 14155780
  72.2 5.5 %copy-start.4 = (s32[16]{0:T(128)S(1)}, s32[16]{0:T(128)}, u32[]{:S(2)}) copy-start(s32[16]{0:T(128)} %constant.81.clone) | copy-start | bytes 196
  72.2 42.5 %all-to-all-start.2 = ((bf16[8,2,16,48,128]{4,3,2,1,0:T(8,128)(2,1)}), bf16[8,2,16,48,128]{4,3,2,1,0:T(8,128)(2,1)}, u32[]{:S(2)}, u32[]{:S(2)}) async-start(bf16[8,2,16,48,128]{4,3,2,1,0:T(8,128)(2,1)} %broadcast_in_dim.48), calls=%async_computation.2 | async-start | bytes 6291456 | tf_op jit(solution)/shard_map/all_to_all | solution.py:174

commit v11 on v10

--- a/solution.py
+++ b/solution.py
@@ -157,17 +157,20 @@
     ).astype(jnp.bfloat16)
 
     offsets = [head % DILATION_RATE for head in range(HEAD_COUNT)]
+    half = HEAD_COUNT // 2
+    grouped = normed.reshape(DILATION_RATE, group_rows, width)
     own_far = jnp.stack(
         [
-            jnp.stack(
-                [
-                    projected_t[
-                        (part * HEAD_COUNT + h) * head_size : (part * HEAD_COUNT + h + 1) * head_size,
-                        o * group_rows : (o + 1) * group_rows,
-                    ]
-                    for h, o in enumerate(offsets)
-                ]
+            jnp.einsum(
+                "ljc,chld->hldj",
+                grouped,
+                qkv_weight[:, part * width : (part + 1) * width].reshape(
+                    width, HEAD_COUNT // DILATION_RATE, DILATION_RATE, head_size
+                ),
+                preferred_element_type=jnp.float32,
             )
+            .astype(jnp.bfloat16)
+            .reshape(HEAD_COUNT, head_size, group_rows)
             for part in (1, 2)
         ]
     )
@@ -202,7 +205,6 @@
         scratch_shapes=[pltpu.VMEM((rows, head_size + 16), jnp.bfloat16)],
     )(projected_t, projected_t, projected_t, near_bias)
 
-    half = HEAD_COUNT // 2
     paired = projected_t.reshape(6, half * head_size, rows)
     far_paired = far.reshape(seq_count, 2, 2, half, head_size, group_rows)
     group_block = pl.BlockSpec(

time: 132 us -> 131 us (level)
  waiting for transfers between devices: 42.2 us -> 31.4 us
  local copies, waits for them, and re-layouts: 8.64 us -> 15.4 us
  matrix products: 18.2 us -> 22.2 us
    all_to_all x1, waiting for transfers between devices: 35.6 us -> 29.6 us  [body(): lax.all_to_all(projected.reshape(device_count, block_rows, width), ('tile...]
    all_to_all x1, waiting for transfers between devices: 5.85 us -> 0.01 us  [body(): lax.all_to_all(jnp.broadcast_to(own_far[None], (seq_count,) + own_far.sha...]
    unnamed x27 -> x16, local copies, waits for them, and re-layouts: 2.07 us -> 6.15 us
    dot_general x1, matrix products: 4.64 us -> 8.48 us  [body(): lax.dot_general(qkv_weight, normed, (((0,), (1,)), ((), ())), preferred_e...]
    slice x0 -> x1, local copies, waits for them, and re-layouts: none -> 3.24 us  [body(): qkv_weight[:, part * width:(part + 1) * width]]
  transfers between devices with their start and end apart: 3 -> 3, of which waited for: 3 -> 2; matrix products, arithmetic and copies ran while one was open for 8% -> 18% of each run, Pallas kernels for 22% -> 23%
where the time goes in v11:
time: 131 us; the launch traced here: 130 us
  Pallas kernels  40.6 us (31%)
  waiting for transfers between devices  31.4 us (24%)
  matrix products  22.2 us (17%)
  starting transfers between devices  16.2 us (12%)
  local copies, waits for them, and re-layouts  15.4 us (12%)
  other arithmetic  3.09 us (2%)
    all_to_all x1, waiting for transfers between devices, body(): lax.all_to_all(projected.reshape(device_count, block_rows, width), ('tile...  29.6 us
    pallas_call x1, Pallas kernels, body(): pl.pallas_call(functools.partial(nearby_kernel, groups=DILATION_RATE, gro...  29.3 us
    pallas_call x1, Pallas kernels, body(): pl.pallas_call(functools.partial(dilated_kernel, factor=factor), grid=(ha...  11.3 us
    dot_general x1, matrix products, body(): lax.dot_general(qkv_weight, normed, (((0,), (1,)), ((), ())), preferred_e...  8.48 us
    all_to_all x1, starting transfers between devices, body(): lax.all_to_all(slot.reshape(device_count, block_rows), ('tile', 'seq'), s...  7.3 us
    unnamed x16, local copies, waits for them, and re-layouts  6.15 us
    dot_general x1, matrix products, body(): jnp.dot(embeddings, in_weight, preferred_element_type=jnp.float32)  5.34 us
    all_to_all x1, starting transfers between devices, body(): lax.all_to_all(jnp.broadcast_to(own_far[None], (seq_count,) + own_far.sha...  4.79 us
  transfers between devices with their start and end apart: 3, of which 2 were waited for; matrix products, arithmetic and copies ran while one was open for 18% of the time, Pallas kernels for 23%

profile of v11, /device:TPU:0, one launch (start us, length us, event | category | flops | bytes accessed | tf_op | source)
XLA Modules:
  0.0 129.8 jit_solution(15740408516605316180)
XLA Ops:
  0.0 0.0 copy-start
  0.0 1.5 %all_to_all.12 = s32[32,1,32]{2,1,0:T(1,128)} reshape(s32[1024]{0:T(1024)} %param.9) | data formatting | bytes 8192 | tf_op jit(solution)/shard_map/all_to_all | solution.py:133
  1.5 7.3 %all-to-all-start = ((s32[32,1,32]{2,1,0:T(1,128)}), s32[32,1,32]{2,1,0:T(1,128)S(1)}, u32[]{:S(2)}, u32[]{:S(2)}) async-start(s32[32,1,32]{2,1,0:T(1,128)} %all_to_all.12), calls=%async_computation | async-start | bytes 32768 | tf_op jit(solution)/shard_map/all_to_all | solution.py:133
  8.8 5.3 %convolution_convert_fusion.1 = bf16[1024,768]{1,0:T(8,128)(2,1)} fusion(bf16[1024,1536]{1,0:T(8,128)(2,1)S(1)} %copy-done, bf16[1536,768]{1,0:T(8,128)(2,1)} %param.11), kind=kOutput, calls=%fused_computation.15 | convolution fusion | flops 2416705536 | bytes 7077888 | tf_op jit(solution)/shard_map/dot_general | solution.py:123
  14.2 1.8 %all-to-all-done = s32[32,1,32]{2,1,0:T(1,128)S(1)} async-done(((s32[32,1,32]{2,1,0:T(1,128)}), s32[32,1,32]{2,1,0:T(1,128)S(1)}, u32[]{:S(2)}, u32[]{:S(2)}) %all-to-all-start) | async-done | bytes 4128 | tf_op jit(solution)/shard_map/all_to_all | solution.py:133
  16.0 4.2 %all-to-all-start.1 = ((bf16[32,32,768]{2,1,0:T(8,128)(2,1)}), bf16[32,32,768]{2,1,0:T(8,128)(2,1)}, u32[]{:S(2)}, u32[]{:S(2)}) async-start(bf16[32,32,768]{2,1,0:T(8,128)(2,1)} %bitcast.48), calls=%async_computation.1 | async-start | bytes 3145728 | tf_op jit(solution)/shard_map/all_to_all | solution.py:126
  20.1 3.2 %fusion.44 = (bf16[768,768]{1,0:T(8,128)(2,1)}, bf16[768,768]{1,0:T(8,128)(2,1)}) fusion(bf16[768,2304]{1,0:T(8,128)(2,1)} %param.13), kind=kLoop, calls=%fused_computation.62 | loop fusion | bytes 4718592 | tf_op jit(solution)/shard_map/slice | solution.py:167
  23.4 2.4 %copy.22 = bf16[768,768]{0,1:T(8,128)(2,1)} copy(bf16[768,768]{1,0:T(8,128)(2,1)} %get-tuple-element.5) | data formatting | bytes 2359296
  25.8 2.4 %copy.23 = bf16[768,768]{0,1:T(8,128)(2,1)} copy(bf16[768,768]{1,0:T(8,128)(2,1)} %get-tuple-element.6) | data formatting | bytes 2359296
  28.2 0.1 sub.34
  28.3 29.6 %all-to-all-done.1 = bf16[32,32,768]{2,1,0:T(8,128)(2,1)} async-done(((bf16[32,32,768]{2,1,0:T(8,128)(2,1)}), bf16[32,32,768]{2,1,0:T(8,128)(2,1)}, u32[]{:S(2)}, u32[]{:S(2)}) %all-to-all-start.1) | async-done | bytes 1572896 | tf_op jit(solution)/shard_map/all_to_all | solution.py:126
  57.9 3.4 %convert_reduce_fusion = (f32[1024]{0:T(1024)S(1)}, bf16[1024,768]{1,0:T(8,128)(2,1)S(1)}) fusion(bf16[1024,768]{1,0:T(8,128)(2,1)} %bitcast.2, s32[1024]{0:T(1024)S(1)} %fusion.36), kind=kOutput, calls=%fused_computation.3 | convolution fusion | flops 1614019584 | bytes 3153920 | tf_op jit(solution)/shard_map/dot_general | solution.py:141
  61.3 0.0 copy-start.1
  61.3 0.0 copy-start.5
  61.3 0.6 fusion.3
  62.0 0.1 copy-done.5
  62.0 0.5 fusion.5
  62.6 0.7 copy-done.4
  63.3 0.6 fusion.23
  64.0 0.6 copy-done.3
  64.6 0.6 fusion.20
  65.3 2.4 %broadcast_in_dim.48 = bf16[8,2,16,48,128]{4,3,2,1,0:T(8,128)(2,1)} broadcast(bf16[2,16,48,128]{3,2,1,0:T(8,128)(2,1)S(1)} %pad_maximum_fusion), dimensions={1,2,3,4} | broadcast | bytes 3538944 | tf_op jit(solution)/shard_map/broadcast_in_dim | solution.py:178
  67.6 4.8 %all-to-all-start.2 = ((bf16[8,2,16,48,128]{4,3,2,1,0:T(8,128)(2,1)}), bf16[8,2,16,48,128]{4,3,2,1,0:T(8,128)(2,1)}, u32[]{:S(2)}, u32[]{:S(2)}) async-start(bf16[8,2,16,48,128]{4,3,2,1,0:T(8,128)(2,1)} %broadcast_in_dim.48), calls=%async_computation.2 | async-start | bytes 6291456 | tf_op jit(solution)/shard_map/all_to_all | solution.py:177
  73.2 0.1 add_compare_fusion
  73.2 0.7 select_convert_fusion.1.bias_ref
  73.9 1.0 select_convert_fusion.fbias_ref
  75.0 8.5 %convolution_convert_fusion = bf16[1024,2304]{0,1:T(8,128)(2,1)} fusion(bf16[1024,768]{1,0:T(8,128)(2,1)} %copy-done.2, bf16[768,2304]{1,0:T(8,128)(2,1)} %param.13), kind=kOutput, calls=%fused_computation | convolution fusion | flops 3626237952 | bytes 9830400 | tf_op jit(solution)/shard_map/dot_general | solution.py:155
  83.4 29.3 %shard_map.82 = bf16[768,1024]{1,0:T(8,128)(2,1)} custom-call(bf16[2304,1024]{1,0:T(8,128)(2,1)} %bitcast.40, bf16[2304,1024]{1,0:T(8,128)(2,1)} %bitcast.41, bf16[2304,1024]{1,0:T(8,128)(2,1)} %bitcast.42, bf16[16,1024]{1,0:T(8,128)(2,1)} %select_convert_fusion.1.bias_ref), custom_call_target="tpu_custom_call" | custom-call | tf_op jit(solution)/shard_map/pallas_call | solution.py:197
  112.8 0.0 all-to-all-done.2
  112.8 11.3 %shard_map.83 = bf16[2,384,1024]{2,1,0:T(8,128)(2,1)} custom-call(bf16[6,384,1024]{2,1,0:T(8,128)(2,1)} %bitcast.43, bf16[6,384,1024]{2,1,0:T(8,128)(2,1)} %bitcast.44, bf16[6,384,1024]{2,1,0:T(8,128)(2,1)} %bitcast.45, bf16[16,1024]{1,0:T(8,128)(2,1)} %select_convert_fusion.1.bias_ref, ...), custom_call_target="tpu_custom_call", output_to_operand_aliasing={{}: (7, {})} | custom-call | tf_op jit(solution)/shard_map/pallas_call | solution.py:214
  124.1 3.7 %fusion.7 = bf16[1024,768]{1,0:T(8,128)(2,1)S(1)} fusion(bf16[1024,768]{1,0:T(8,128)(2,1)} %copy-done.1, bf16[768,1024]{1,0:T(8,128)(2,1)} %bitcast.47, bf16[768,768]{1,0:T(8,128)(2,1)} %param.14, pred[1024]{0:T(1024)(128)(4,1)S(1)} %fusion.34), kind=kOutput, calls=%fused_computation.12 | convolution fusion | flops 1211105280 | bytes 5899264 | tf_op jit(solution)/shard_map/dot_general | solution.py:235
  127.8 2.0 %copy.37 = bf16[128,8,768]{2,1,0:T(8,128)(2,1)} copy(bf16[128,8,768]{2,0,1:T(8,128)(2,1)S(1)} %bitcast.51) | data formatting | bytes 3145728 | tf_op jit(solution)/shard_map/transpose | solution.py:239
  (19 shorter events, 0.2 us)
Async XLA Ops:
  0.0 8.8 %copy-start = (bf16[1024,1536]{1,0:T(8,128)(2,1)S(1)}, bf16[1024,1536]{1,0:T(8,128)(2,1)}, u32[]{:S(2)}) copy-start(bf16[1024,1536]{1,0:T(8,128)(2,1)} %param.8) | copy-start | bytes 9437188
  1.5 14.4 %all-to-all-start = ((s32[32,1,32]{2,1,0:T(1,128)}), s32[32,1,32]{2,1,0:T(1,128)S(1)}, u32[]{:S(2)}, u32[]{:S(2)}) async-start(s32[32,1,32]{2,1,0:T(1,128)} %all_to_all.12), calls=%async_computation | async-start | bytes 32768 | tf_op jit(solution)/shard_map/all_to_all | solution.py:133
  16.0 41.9 %all-to-all-start.1 = ((bf16[32,32,768]{2,1,0:T(8,128)(2,1)}), bf16[32,32,768]{2,1,0:T(8,128)(2,1)}, u32[]{:S(2)}, u32[]{:S(2)}) async-start(bf16[32,32,768]{2,1,0:T(8,128)(2,1)} %bitcast.48), calls=%async_computation.1 | async-start | bytes 3145728 | tf_op jit(solution)/shard_map/all_to_all | solution.py:126
  61.3 1.3 copy-start.1
  61.3 0.7 copy-start.5
  62.0 1.3 copy-start.4
  62.6 1.4 %copy-start.2 = (bf16[1024,768]{1,0:T(8,128)(2,1)}, bf16[1024,768]{1,0:T(8,128)(2,1)S(1)}, u32[]{:S(2)}) copy-start(bf16[1024,768]{1,0:T(8,128)(2,1)S(1)} %fusion.5) | copy-start | bytes 4718596
  63.3 1.3 copy-start.3
  67.6 5.5 %copy-start.6 = (s32[16]{0:T(128)S(1)}, s32[16]{0:T(128)}, u32[]{:S(2)}) copy-start(s32[16]{0:T(128)} %constant.81.clone) | copy-start | bytes 196
  67.6 45.1 %all-to-all-start.2 = ((bf16[8,2,16,48,128]{4,3,2,1,0:T(8,128)(2,1)}), bf16[8,2,16,48,128]{4,3,2,1,0:T(8,128)(2,1)}, u32[]{:S(2)}, u32[]{:S(2)}) async-start(bf16[8,2,16,48,128]{4,3,2,1,0:T(8,128)(2,1)} %broadcast_in_dim.48), calls=%async_computation.2 | async-start | bytes 6291456 | tf_op jit(solution)/shard_map/all_to_all | solution.py:177

commit v12 on v11

--- a/solution.py
+++ b/solution.py
@@ -38,26 +38,21 @@
 def nearby_kernel(
     qt_ref, kt_ref, vt_ref, bias_ref, o_ref, keys_ref, *, groups, group_rows, factor
 ):
-    keys_ref[...] = extend(kt_ref[...], bias_ref[...]).T
-    key_count = keys_ref.shape[0]
+    key_count = keys_ref.shape[1]
     block = QUERY_BLOCK
     ones = ones_row(block)
-    for first_row in range(0, groups * group_rows, block):
-        rows = pl.ds(first_row, block)
-        queries_t = extend(qt_ref[:, rows], ones)
-        if PASS1 >= key_count and PASS2 >= key_count:
-            scores_t = jnp.dot(keys_ref[...], queries_t, preferred_element_type=jnp.float32)
-            top = jnp.max(scores_t, axis=0, keepdims=True)
-            weights_t = jnp.exp2((scores_t - top) * factor)
-            total = jnp.sum(weights_t, axis=0, keepdims=True)
-            summed_t = jnp.dot(
-                vt_ref[...], weights_t.astype(jnp.bfloat16), preferred_element_type=jnp.float32
-            )
-        else:
+    for pair in range(2):
+        keys_ref[pair] = extend(kt_ref[pair], bias_ref[...]).T
+    for pair in range(2):
+        for first_row in range(0, groups * group_rows, block):
+            rows = pl.ds(first_row, block)
+            queries_t = extend(qt_ref[pair, :, rows], ones)
             top = None
             for first in range(0, key_count, PASS1):
                 scores_t = jnp.dot(
-                    keys_ref[pl.ds(first, PASS1), :], queries_t, preferred_element_type=jnp.float32
+                    keys_ref[pair, pl.ds(first, PASS1), :],
+                    queries_t,
+                    preferred_element_type=jnp.float32,
                 )
                 part = jnp.max(scores_t, axis=0, keepdims=True)
                 top = part if top is None else jnp.maximum(top, part)
@@ -65,18 +60,20 @@
             summed_t = None
             for first in range(0, key_count, PASS2):
                 scores_t = jnp.dot(
-                    keys_ref[pl.ds(first, PASS2), :], queries_t, preferred_element_type=jnp.float32
+                    keys_ref[pair, pl.ds(first, PASS2), :],
+                    queries_t,
+                    preferred_element_type=jnp.float32,
                 )
                 weights_t = jnp.exp2((scores_t - top) * factor)
                 part = jnp.sum(weights_t, axis=0, keepdims=True)
                 step = jnp.dot(
-                    vt_ref[:, pl.ds(first, PASS2)],
+                    vt_ref[pair, :, pl.ds(first, PASS2)],
                     weights_t.astype(jnp.bfloat16),
                     preferred_element_type=jnp.float32,
                 )
                 total = part if total is None else total + part
                 summed_t = step if summed_t is None else summed_t + step
-        o_ref[:, rows] = (summed_t / total).astype(o_ref.dtype)
+            o_ref[pair, :, rows] = (summed_t / total).astype(o_ref.dtype)
 
 
 def joined(ref, pair):
@@ -189,23 +186,23 @@
         extra_row[None] & (far_position >= slide_length)[:, None, :], big_negative, 0.0
     ).astype(jnp.bfloat16)
 
-    query_block = pl.BlockSpec((head_size, rows), lambda h: (h, 0))
-    keys_block = pl.BlockSpec((head_size, rows), lambda h: (HEAD_COUNT + h, 0))
-    values_block = pl.BlockSpec((head_size, rows), lambda h: (2 * HEAD_COUNT + h, 0))
-    bias_block = pl.BlockSpec((16, rows), lambda h: (0, 0))
+    bias_block = pl.BlockSpec((16, rows), lambda i: (0, 0))
     factor = scale * 1.4426950408889634
+    paired = projected_t.reshape(6, half * head_size, rows)
+    head_pairs = [
+        pl.BlockSpec((2, head_size, rows), lambda i, part=part: (part, i, 0)) for part in range(3)
+    ]
     nearby = pl.pallas_call(
         functools.partial(
             nearby_kernel, groups=DILATION_RATE, group_rows=group_rows, factor=factor
         ),
-        grid=(HEAD_COUNT,),
-        in_specs=[query_block, keys_block, values_block, bias_block],
-        out_specs=query_block,
-        out_shape=jax.ShapeDtypeStruct((width, rows), jnp.bfloat16),
-        scratch_shapes=[pltpu.VMEM((rows, head_size + 16), jnp.bfloat16)],
-    )(projected_t, projected_t, projected_t, near_bias)
-
-    paired = projected_t.reshape(6, half * head_size, rows)
+        grid=(half,),
+        in_specs=head_pairs + [bias_block],
+        out_specs=head_pairs[0],
+        out_shape=jax.ShapeDtypeStruct((2, half * head_size, rows), jnp.bfloat16),
+        scratch_shapes=[pltpu.VMEM((2, rows, head_size + 16), jnp.bfloat16)],
+    )(paired, paired, paired, near_bias)
+
     far_paired = far.reshape(seq_count, 2, 2, half, head_size, group_rows)
     group_block = pl.BlockSpec(
         (2, head_size, group_rows), lambda i: (0, i, i % DILATION_RATE)
@@ -229,7 +226,7 @@
         input_output_aliases={7: 0},
     )(
         paired, paired, paired, near_bias, far_paired, far_paired, far_bias,
-        nearby.reshape(2, half * head_size, rows),
+        nearby,
     ).reshape(width, rows)
 
     output = lax.dot_general(

time: 131 us -> 136 us (1.038)
  local copies, waits for them, and re-layouts: 15.4 us -> 21.9 us
    convert_element_type x0 -> x1, local copies, waits for them, and re-layouts: none -> 6.63 us  [body(): projected_t = lax.dot_general(qkv_weight, normed, (((0,), (1,)), ((), ())...]
  transfers between devices with their start and end apart: 3 -> 3, of which waited for: 2 -> 2; matrix products, arithmetic and copies ran while one was open for 18% -> 22% of each run, Pallas kernels for 23% -> 21%
where the time goes in v12:
time: 136 us; the launch traced here: 135 us
  Pallas kernels  39.3 us (29%)
  waiting for transfers between devices  31.4 us (23%)
  matrix products  22.2 us (16%)
  local copies, waits for them, and re-layouts  21.9 us (16%)
  starting transfers between devices  16.2 us (12%)
  other arithmetic  3.09 us (2%)
    all_to_all x1, waiting for transfers between devices, body(): lax.all_to_all(projected.reshape(device_count, block_rows, width), ('tile...  29.6 us
    pallas_call x1, Pallas kernels, body(): pl.pallas_call(functools.partial(nearby_kernel, groups=DILATION_RATE, gro...  28 us
    pallas_call x1, Pallas kernels, body(): pl.pallas_call(functools.partial(dilated_kernel, factor=factor), grid=(ha...  11.3 us
    dot_general x1, matrix products, body(): lax.dot_general(qkv_weight, normed, (((0,), (1,)), ((), ())), preferred_e...  8.48 us
    all_to_all x1, starting transfers between devices, body(): lax.all_to_all(slot.reshape(device_count, block_rows), ('tile', 'seq'), s...  7.3 us
    convert_element_type x1, local copies, waits for them, and re-layouts, body(): projected_t = lax.dot_general(qkv_weight, normed, (((0,), (1,)), ((), ())...  6.63 us
    unnamed x16, local copies, waits for them, and re-layouts  6.15 us
    dot_general x1, matrix products, body(): jnp.dot(embeddings, in_weight, preferred_element_type=jnp.float32)  5.34 us
  transfers between devices with their start and end apart: 3, of which 2 were waited for; matrix products, arithmetic and copies ran while one was open for 22% of the time, Pallas kernels for 21%

profile of v12, /device:TPU:0, one launch (start us, length us, event | category | flops | bytes accessed | tf_op | source)
XLA Modules:
  0.0 135.0 jit_solution(3609761784967593986)
XLA Ops:
  0.0 1.5 %all_to_all.12 = s32[32,1,32]{2,1,0:T(1,128)} reshape(s32[1024]{0:T(1024)} %param.9) | data formatting | bytes 8192 | tf_op jit(solution)/shard_map/all_to_all | solution.py:130
  1.5 7.3 %all-to-all-start = ((s32[32,1,32]{2,1,0:T(1,128)}), s32[32,1,32]{2,1,0:T(1,128)S(1)}, u32[]{:S(2)}, u32[]{:S(2)}) async-start(s32[32,1,32]{2,1,0:T(1,128)} %all_to_all.12), calls=%async_computation | async-start | bytes 32768 | tf_op jit(solution)/shard_map/all_to_all | solution.py:130
  8.8 5.3 %convolution_convert_fusion.1 = bf16[1024,768]{1,0:T(8,128)(2,1)} fusion(bf16[1024,1536]{1,0:T(8,128)(2,1)S(1)} %copy-done, bf16[1536,768]{1,0:T(8,128)(2,1)} %param.11), kind=kOutput, calls=%fused_computation.16 | convolution fusion | flops 2416705536 | bytes 7077888 | tf_op jit(solution)/shard_map/dot_general | solution.py:120
  14.2 1.8 %all-to-all-done = s32[32,1,32]{2,1,0:T(1,128)S(1)} async-done(((s32[32,1,32]{2,1,0:T(1,128)}), s32[32,1,32]{2,1,0:T(1,128)S(1)}, u32[]{:S(2)}, u32[]{:S(2)}) %all-to-all-start) | async-done | bytes 4128 | tf_op jit(solution)/shard_map/all_to_all | solution.py:130
  16.0 4.2 %all-to-all-start.1 = ((bf16[32,32,768]{2,1,0:T(8,128)(2,1)}), bf16[32,32,768]{2,1,0:T(8,128)(2,1)}, u32[]{:S(2)}, u32[]{:S(2)}) async-start(bf16[32,32,768]{2,1,0:T(8,128)(2,1)} %bitcast.46), calls=%async_computation.1 | async-start | bytes 3145728 | tf_op jit(solution)/shard_map/all_to_all | solution.py:123
  20.1 3.2 %fusion.45 = (bf16[768,768]{1,0:T(8,128)(2,1)}, bf16[768,768]{1,0:T(8,128)(2,1)}) fusion(bf16[768,2304]{1,0:T(8,128)(2,1)} %param.13), kind=kLoop, calls=%fused_computation.63 | loop fusion | bytes 4718592 | tf_op jit(solution)/shard_map/slice | solution.py:164
  23.3 2.4 %copy.22 = bf16[768,768]{0,1:T(8,128)(2,1)} copy(bf16[768,768]{1,0:T(8,128)(2,1)} %get-tuple-element.6) | data formatting | bytes 2359296
  25.7 2.4 %copy.21 = bf16[768,768]{0,1:T(8,128)(2,1)} copy(bf16[768,768]{1,0:T(8,128)(2,1)} %get-tuple-element.5) | data formatting | bytes 2359296
  28.2 0.1 sub.34
  28.2 29.6 %all-to-all-done.1 = bf16[32,32,768]{2,1,0:T(8,128)(2,1)} async-done(((bf16[32,32,768]{2,1,0:T(8,128)(2,1)}), bf16[32,32,768]{2,1,0:T(8,128)(2,1)}, u32[]{:S(2)}, u32[]{:S(2)}) %all-to-all-start.1) | async-done | bytes 1572896 | tf_op jit(solution)/shard_map/all_to_all | solution.py:123
  57.9 3.4 %convert_reduce_fusion = (f32[1024]{0:T(1024)S(1)}, bf16[1024,768]{1,0:T(8,128)(2,1)S(1)}) fusion(bf16[1024,768]{1,0:T(8,128)(2,1)} %bitcast.2, s32[1024]{0:T(1024)S(1)} %fusion.37), kind=kOutput, calls=%fused_computation.4 | convolution fusion | flops 1614019584 | bytes 3153920 | tf_op jit(solution)/shard_map/dot_general | solution.py:138
  61.3 0.0 copy-start.1
  61.3 0.0 copy-start.5
  61.3 0.6 fusion.4
  62.0 0.1 copy-done.5
  62.0 0.5 fusion.6
  62.6 0.7 copy-done.4
  63.3 0.6 fusion.21
  64.0 0.6 copy-done.3
  64.6 0.6 fusion.24
  65.3 2.3 %broadcast_in_dim.48 = bf16[8,2,16,48,128]{4,3,2,1,0:T(8,128)(2,1)} broadcast(bf16[2,16,48,128]{3,2,1,0:T(8,128)(2,1)S(1)} %pad_maximum_fusion), dimensions={1,2,3,4} | broadcast | bytes 3538944 | tf_op jit(solution)/shard_map/broadcast_in_dim | solution.py:175
  67.5 4.8 %all-to-all-start.2 = ((bf16[8,2,16,48,128]{4,3,2,1,0:T(8,128)(2,1)}), bf16[8,2,16,48,128]{4,3,2,1,0:T(8,128)(2,1)}, u32[]{:S(2)}, u32[]{:S(2)}) async-start(bf16[8,2,16,48,128]{4,3,2,1,0:T(8,128)(2,1)} %broadcast_in_dim.48), calls=%async_computation.2 | async-start | bytes 6291456 | tf_op jit(solution)/shard_map/all_to_all | solution.py:174
  73.0 0.1 add_compare_fusion
  73.1 0.7 select_convert_fusion.1.bias_ref
  73.8 1.0 select_convert_fusion.fbias_ref
  74.8 8.5 %fusion = bf16[2304,1024]{0,1:T(8,128)(2,1)} fusion(bf16[1024,768]{1,0:T(8,128)(2,1)} %copy-done.2, bf16[768,2304]{1,0:T(8,128)(2,1)} %param.13), kind=kOutput, calls=%fused_computation.1 | convolution fusion | flops 3626237952 | bytes 9830400 | tf_op jit(solution)/shard_map/dot_general | solution.py:152
  83.3 6.6 %copy.12 = bf16[2304,1024]{1,0:T(8,128)(2,1)} copy(bf16[2304,1024]{0,1:T(8,128)(2,1)} %fusion) | data formatting | bytes 9437184 | tf_op jit(solution)/shard_map/convert_element_type | solution.py:154
  89.9 28.0 %shard_map.82.prev_ref = bf16[2,384,1024]{2,1,0:T(8,128)(2,1)} custom-call(bf16[6,384,1024]{2,1,0:T(8,128)(2,1)} %bitcast.39, bf16[6,384,1024]{2,1,0:T(8,128)(2,1)} %bitcast.40, bf16[6,384,1024]{2,1,0:T(8,128)(2,1)} %bitcast.41, bf16[16,1024]{1,0:T(8,128)(2,1)} %select_convert_fusion.1.bias_ref), custom_call_target="tpu_custom_call" | custom-call | tf_op jit(solution)/shard_map/pallas_call | solution.py:195
  117.9 0.0 all-to-all-done.2
  117.9 11.3 %shard_map.83 = bf16[2,384,1024]{2,1,0:T(8,128)(2,1)} custom-call(bf16[6,384,1024]{2,1,0:T(8,128)(2,1)} %bitcast.42, bf16[6,384,1024]{2,1,0:T(8,128)(2,1)} %bitcast.43, bf16[6,384,1024]{2,1,0:T(8,128)(2,1)} %bitcast.44, bf16[16,1024]{1,0:T(8,128)(2,1)} %select_convert_fusion.1.bias_ref, ...), custom_call_target="tpu_custom_call", output_to_operand_aliasing={{}: (7, {})} | custom-call | tf_op jit(solution)/shard_map/pallas_call | solution.py:211
  129.2 3.7 %fusion.8 = bf16[1024,768]{1,0:T(8,128)(2,1)S(1)} fusion(bf16[1024,768]{1,0:T(8,128)(2,1)} %copy-done.1, bf16[768,1024]{1,0:T(8,128)(2,1)} %bitcast.45, bf16[768,768]{1,0:T(8,128)(2,1)} %param.14, pred[1024]{0:T(1024)(128)(4,1)S(1)} %fusion.35), kind=kOutput, calls=%fused_computation.13 | convolution fusion | flops 1211105280 | bytes 5899264 | tf_op jit(solution)/shard_map/dot_general | solution.py:232
  132.9 2.0 %copy.36 = bf16[128,8,768]{2,1,0:T(8,128)(2,1)} copy(bf16[128,8,768]{2,0,1:T(8,128)(2,1)S(1)} %bitcast.49) | data formatting | bytes 3145728 | tf_op jit(solution)/shard_map/transpose | solution.py:236
  (20 shorter events, 0.2 us)
Async XLA Ops:
  0.0 8.8 %copy-start = (bf16[1024,1536]{1,0:T(8,128)(2,1)S(1)}, bf16[1024,1536]{1,0:T(8,128)(2,1)}, u32[]{:S(2)}) copy-start(bf16[1024,1536]{1,0:T(8,128)(2,1)} %param.8) | copy-start | bytes 9437188
  1.5 14.4 %all-to-all-start = ((s32[32,1,32]{2,1,0:T(1,128)}), s32[32,1,32]{2,1,0:T(1,128)S(1)}, u32[]{:S(2)}, u32[]{:S(2)}) async-start(s32[32,1,32]{2,1,0:T(1,128)} %all_to_all.12), calls=%async_computation | async-start | bytes 32768 | tf_op jit(solution)/shard_map/all_to_all | solution.py:130
  16.0 41.9 %all-to-all-start.1 = ((bf16[32,32,768]{2,1,0:T(8,128)(2,1)}), bf16[32,32,768]{2,1,0:T(8,128)(2,1)}, u32[]{:S(2)}, u32[]{:S(2)}) async-start(bf16[32,32,768]{2,1,0:T(8,128)(2,1)} %bitcast.46), calls=%async_computation.1 | async-start | bytes 3145728 | tf_op jit(solution)/shard_map/all_to_all | solution.py:123
  61.3 1.3 copy-start.1
  61.3 0.7 copy-start.5
  62.0 1.3 copy-start.4
  62.6 1.4 %copy-start.2 = (bf16[1024,768]{1,0:T(8,128)(2,1)}, bf16[1024,768]{1,0:T(8,128)(2,1)S(1)}, u32[]{:S(2)}) copy-start(bf16[1024,768]{1,0:T(8,128)(2,1)S(1)} %fusion.6) | copy-start | bytes 4718596
  63.3 1.3 copy-start.3
  67.5 5.5 %copy-start.6 = (s32[16]{0:T(128)S(1)}, s32[16]{0:T(128)}, u32[]{:S(2)}) copy-start(s32[16]{0:T(128)} %constant.81.clone) | copy-start | bytes 196
  67.5 50.4 %all-to-all-start.2 = ((bf16[8,2,16,48,128]{4,3,2,1,0:T(8,128)(2,1)}), bf16[8,2,16,48,128]{4,3,2,1,0:T(8,128)(2,1)}, u32[]{:S(2)}, u32[]{:S(2)}) async-start(bf16[8,2,16,48,128]{4,3,2,1,0:T(8,128)(2,1)} %broadcast_in_dim.48), calls=%async_computation.2 | async-start | bytes 6291456 | tf_op jit(solution)/shard_map/all_to_all | solution.py:174

commit v13 on v11

--- a/solution.py
+++ b/solution.py
@@ -35,48 +35,37 @@
     return jnp.where(row == 0, 1.0, 0.0).astype(jnp.bfloat16)
 
 
-def nearby_kernel(
-    qt_ref, kt_ref, vt_ref, bias_ref, o_ref, keys_ref, *, groups, group_rows, factor
-):
+def nearby_kernel(*refs, groups, group_rows, factor):
+    *query_refs, kt_ref, vt_ref, bias_ref, o_ref, keys_ref = refs
     keys_ref[...] = extend(kt_ref[...], bias_ref[...]).T
     key_count = keys_ref.shape[0]
-    block = QUERY_BLOCK
-    ones = ones_row(block)
-    for first_row in range(0, groups * group_rows, block):
-        rows = pl.ds(first_row, block)
-        queries_t = extend(qt_ref[:, rows], ones)
-        if PASS1 >= key_count and PASS2 >= key_count:
-            scores_t = jnp.dot(keys_ref[...], queries_t, preferred_element_type=jnp.float32)
-            top = jnp.max(scores_t, axis=0, keepdims=True)
-            weights_t = jnp.exp2((scores_t - top) * factor)
-            total = jnp.sum(weights_t, axis=0, keepdims=True)
-            summed_t = jnp.dot(
-                vt_ref[...], weights_t.astype(jnp.bfloat16), preferred_element_type=jnp.float32
-            )
-        else:
-            top = None
-            for first in range(0, key_count, PASS1):
-                scores_t = jnp.dot(
-                    keys_ref[pl.ds(first, PASS1), :], queries_t, preferred_element_type=jnp.float32
-                )
-                part = jnp.max(scores_t, axis=0, keepdims=True)
-                top = part if top is None else jnp.maximum(top, part)
-            total = None
-            summed_t = None
-            for first in range(0, key_count, PASS2):
-                scores_t = jnp.dot(
-                    keys_ref[pl.ds(first, PASS2), :], queries_t, preferred_element_type=jnp.float32
-                )
-                weights_t = jnp.exp2((scores_t - top) * factor)
-                part = jnp.sum(weights_t, axis=0, keepdims=True)
-                step = jnp.dot(
-                    vt_ref[:, pl.ds(first, PASS2)],
-                    weights_t.astype(jnp.bfloat16),
-                    preferred_element_type=jnp.float32,
-                )
-                total = part if total is None else total + part
-                summed_t = step if summed_t is None else summed_t + step
-        o_ref[:, rows] = (summed_t / total).astype(o_ref.dtype)
+    width = (groups - 1) * group_rows
+    queries_t = extend(
+        jnp.concatenate([ref[...] for ref in query_refs], axis=1), ones_row(width)
+    )
+    top = None
+    for first in range(0, key_count, PASS1):
+        scores_t = jnp.dot(
+            keys_ref[pl.ds(first, PASS1), :], queries_t, preferred_element_type=jnp.float32
+        )
+        part = jnp.max(scores_t, axis=0, keepdims=True)
+        top = part if top is None else jnp.maximum(top, part)
+    total = None
+    summed_t = None
+    for first in range(0, key_count, PASS2):
+        scores_t = jnp.dot(
+            keys_ref[pl.ds(first, PASS2), :], queries_t, preferred_element_type=jnp.float32
+        )
+        weights_t = jnp.exp2((scores_t - top) * factor)
+        part = jnp.sum(weights_t, axis=0, keepdims=True)
+        step = jnp.dot(
+            vt_ref[:, pl.ds(first, PASS2)],
+            weights_t.astype(jnp.bfloat16),
+            preferred_element_type=jnp.float32,
+        )
+        total = part if total is None else total + part
+        summed_t = step if summed_t is None else summed_t + step
+    o_ref[:, pl.ds(0, width)] = (summed_t / total).astype(o_ref.dtype)
 
 
 def joined(ref, pair):
@@ -199,17 +188,22 @@
             nearby_kernel, groups=DILATION_RATE, group_rows=group_rows, factor=factor
         ),
         grid=(HEAD_COUNT,),
-        in_specs=[query_block, keys_block, values_block, bias_block],
+        in_specs=[
+            pl.BlockSpec(
+                (head_size, group_rows),
+                lambda h, t=t: (h, (h % DILATION_RATE + 1 + t) % DILATION_RATE),
+            )
+            for t in range(DILATION_RATE - 1)
+        ]
+        + [keys_block, values_block, bias_block],
         out_specs=query_block,
         out_shape=jax.ShapeDtypeStruct((width, rows), jnp.bfloat16),
         scratch_shapes=[pltpu.VMEM((rows, head_size + 16), jnp.bfloat16)],
-    )(projected_t, projected_t, projected_t, near_bias)
+    )(*([projected_t] * (DILATION_RATE - 1)), projected_t, projected_t, near_bias)
 
     paired = projected_t.reshape(6, half * head_size, rows)
     far_paired = far.reshape(seq_count, 2, 2, half, head_size, group_rows)
-    group_block = pl.BlockSpec(
-        (2, head_size, group_rows), lambda i: (0, i, i % DILATION_RATE)
-    )
+    group_block = pl.BlockSpec((2, head_size, group_rows), lambda i: (0, i, DILATION_RATE - 1))
     far_block = (seq_count, 1, 2, 1, head_size, group_rows)
     attended_t = pl.pallas_call(
         functools.partial(dilated_kernel, factor=factor),
@@ -231,6 +225,14 @@
         paired, paired, paired, near_bias, far_paired, far_paired, far_bias,
         nearby.reshape(2, half * head_size, rows),
     ).reshape(width, rows)
+    attended_t = jnp.concatenate(
+        [
+            jnp.roll(
+                attended_t[h * head_size : (h + 1) * head_size], (o + 1) * group_rows, axis=1
+            )
+            for h, o in enumerate(offsets)
+        ]
+    )
 
     output = lax.dot_general(
         attended_t, out_weight, (((0,), (0,)), ((), ())), preferred_element_type=jnp.float32

time: 131 us -> 137 us (1.046)
  local copies, waits for them, and re-layouts: 15.4 us -> 23.6 us
  matrix products: 22.2 us -> 20 us
    slice x0 -> x7, local copies, waits for them, and re-layouts: none -> 6.29 us  [body(): jnp.roll(attended_t[h * head_size:(h + 1) * head_size], (o + 1) * group_r...]
    dot_general x1, matrix products: 3.73 us -> 1.54 us  [body(): lax.dot_general(attended_t, out_weight, (((0,), (0,)), ((), ())), preferr...]
    unnamed x16 -> x21, local copies, waits for them, and re-layouts: 6.15 us -> 7.21 us
  transfers between devices with their start and end apart: 3 -> 3, of which waited for: 2 -> 2; matrix products, arithmetic and copies ran while one was open for 18% -> 18% of each run, Pallas kernels for 23% -> 21%
where the time goes in v13:
time: 137 us; the launch traced here: 135 us
  Pallas kernels  40 us (29%)
  waiting for transfers between devices  31.4 us (23%)
  local copies, waits for them, and re-layouts  23.6 us (17%)
  matrix products  20 us (15%)
  starting transfers between devices  16.2 us (12%)
  other arithmetic  3.24 us (2%)
    all_to_all x1, waiting for transfers between devices, body(): lax.all_to_all(projected.reshape(device_count, block_rows, width), ('tile...  29.6 us
    pallas_call x1, Pallas kernels, body(): pl.pallas_call(functools.partial(nearby_kernel, groups=DILATION_RATE, gro...  28.7 us
    pallas_call x1, Pallas kernels, body(): pl.pallas_call(functools.partial(dilated_kernel, factor=factor), grid=(ha...  11.3 us
    dot_general x1, matrix products, body(): lax.dot_general(qkv_weight, normed, (((0,), (1,)), ((), ())), preferred_e...  8.47 us
    all_to_all x1, starting transfers between devices, body(): lax.all_to_all(slot.reshape(device_count, block_rows), ('tile', 'seq'), s...  7.3 us
    unnamed x21, local copies, waits for them, and re-layouts  7.21 us
    slice x7, local copies, waits for them, and re-layouts, body(): jnp.roll(attended_t[h * head_size:(h + 1) * head_size], (o + 1) * group_r...  6.29 us
    dot_general x1, matrix products, body(): jnp.dot(embeddings, in_weight, preferred_element_type=jnp.float32)  5.34 us
  transfers between devices with their start and end apart: 3, of which 2 were waited for; matrix products, arithmetic and copies ran while one was open for 18% of the time, Pallas kernels for 21%

profile of v13, /device:TPU:0, one launch (start us, length us, event | category | flops | bytes accessed | tf_op | source)
XLA Modules:
  0.0 135.5 jit_solution(15039395654414571592)
XLA Ops:
  0.0 1.5 %all_to_all.12 = s32[32,1,32]{2,1,0:T(1,128)} reshape(s32[1024]{0:T(1024)} %param.9) | data formatting | bytes 8192 | tf_op jit(solution)/shard_map/all_to_all | solution.py:122
  1.5 7.3 %all-to-all-start = ((s32[32,1,32]{2,1,0:T(1,128)}), s32[32,1,32]{2,1,0:T(1,128)S(1)}, u32[]{:S(2)}, u32[]{:S(2)}) async-start(s32[32,1,32]{2,1,0:T(1,128)} %all_to_all.12), calls=%async_computation | async-start | bytes 32768 | tf_op jit(solution)/shard_map/all_to_all | solution.py:122
  8.8 5.3 %convolution_convert_fusion.1 = bf16[1024,768]{1,0:T(8,128)(2,1)} fusion(bf16[1024,1536]{1,0:T(8,128)(2,1)S(1)} %copy-done, bf16[1536,768]{1,0:T(8,128)(2,1)} %param.11), kind=kOutput, calls=%fused_computation.15 | convolution fusion | flops 2416705536 | bytes 7077888 | tf_op jit(solution)/shard_map/dot_general | solution.py:112
  14.2 1.8 %all-to-all-done = s32[32,1,32]{2,1,0:T(1,128)S(1)} async-done(((s32[32,1,32]{2,1,0:T(1,128)}), s32[32,1,32]{2,1,0:T(1,128)S(1)}, u32[]{:S(2)}, u32[]{:S(2)}) %all-to-all-start) | async-done | bytes 4128 | tf_op jit(solution)/shard_map/all_to_all | solution.py:122
  16.0 4.2 %all-to-all-start.1 = ((bf16[32,32,768]{2,1,0:T(8,128)(2,1)}), bf16[32,32,768]{2,1,0:T(8,128)(2,1)}, u32[]{:S(2)}, u32[]{:S(2)}) async-start(bf16[32,32,768]{2,1,0:T(8,128)(2,1)} %bitcast.62), calls=%async_computation.1 | async-start | bytes 3145728 | tf_op jit(solution)/shard_map/all_to_all | solution.py:115
  20.1 3.2 %fusion.44 = (bf16[768,768]{1,0:T(8,128)(2,1)}, bf16[768,768]{1,0:T(8,128)(2,1)}) fusion(bf16[768,2304]{1,0:T(8,128)(2,1)} %param.13), kind=kLoop, calls=%fused_computation.78 | loop fusion | bytes 4718592 | tf_op jit(solution)/shard_map/slice | solution.py:156
  23.4 2.4 %copy.22 = bf16[768,768]{0,1:T(8,128)(2,1)} copy(bf16[768,768]{1,0:T(8,128)(2,1)} %get-tuple-element.5) | data formatting | bytes 2359296
  25.7 2.4 %copy.23 = bf16[768,768]{0,1:T(8,128)(2,1)} copy(bf16[768,768]{1,0:T(8,128)(2,1)} %get-tuple-element.6) | data formatting | bytes 2359296
  28.2 29.6 %all-to-all-done.1 = bf16[32,32,768]{2,1,0:T(8,128)(2,1)} async-done(((bf16[32,32,768]{2,1,0:T(8,128)(2,1)}), bf16[32,32,768]{2,1,0:T(8,128)(2,1)}, u32[]{:S(2)}, u32[]{:S(2)}) %all-to-all-start.1) | async-done | bytes 1572896 | tf_op jit(solution)/shard_map/all_to_all | solution.py:115
  57.9 3.4 %convert_reduce_fusion = (f32[1024]{0:T(1024)S(1)}, bf16[1024,768]{1,0:T(8,128)(2,1)S(1)}) fusion(bf16[1024,768]{1,0:T(8,128)(2,1)} %bitcast.2, s32[1024]{0:T(1024)S(1)} %fusion.36), kind=kOutput, calls=%fused_computation.3 | convolution fusion | flops 1614019584 | bytes 3153920 | tf_op jit(solution)/shard_map/dot_general | solution.py:130
  61.3 0.6 fusion.3
  62.6 0.7 copy-done.5
  63.3 0.6 fusion.23
  64.6 0.6 fusion.20
  65.3 2.3 %broadcast_in_dim.48 = bf16[8,2,16,48,128]{4,3,2,1,0:T(8,128)(2,1)} broadcast(bf16[2,16,48,128]{3,2,1,0:T(8,128)(2,1)S(1)} %pad_maximum_fusion), dimensions={1,2,3,4} | broadcast | bytes 3538944 | tf_op jit(solution)/shard_map/broadcast_in_dim | solution.py:167
  67.6 4.8 %all-to-all-start.2 = ((bf16[8,2,16,48,128]{4,3,2,1,0:T(8,128)(2,1)}), bf16[8,2,16,48,128]{4,3,2,1,0:T(8,128)(2,1)}, u32[]{:S(2)}, u32[]{:S(2)}) async-start(bf16[8,2,16,48,128]{4,3,2,1,0:T(8,128)(2,1)} %broadcast_in_dim.48), calls=%async_computation.2 | async-start | bytes 6291456 | tf_op jit(solution)/shard_map/all_to_all | solution.py:166
  73.2 0.7 select_convert_fusion.1.refs_9_.bias_ref
  73.9 1.0 select_convert_fusion.fbias_ref
  74.9 8.5 %convolution_convert_fusion = bf16[1024,2304]{0,1:T(8,128)(2,1)} fusion(bf16[1024,768]{1,0:T(8,128)(2,1)} %copy-done.3, bf16[768,2304]{1,0:T(8,128)(2,1)} %param.13), kind=kOutput, calls=%fused_computation | convolution fusion | flops 3626237952 | bytes 9830400 | tf_op jit(solution)/shard_map/dot_general | solution.py:144
  83.4 28.7 %shard_map.82 = bf16[768,1024]{1,0:T(8,128)(2,1)} custom-call(bf16[2304,1024]{1,0:T(8,128)(2,1)} %bitcast.40, bf16[2304,1024]{1,0:T(8,128)(2,1)} %bitcast.41, bf16[2304,1024]{1,0:T(8,128)(2,1)} %bitcast.42, bf16[2304,1024]{1,0:T(8,128)(2,1)} %bitcast.43, bf16[2304,1024]{1,0:T(8,128)(2,1)} %bitcast.44, bf16[2304,1024]{1,0:T(8,128)(2,1)} %bitcast.45, ...), custom_call_target="tpu_custom_call" | custom-call | tf_op jit(solution)/shard_map/pallas_call | solution.py:186
  112.1 11.3 %shard_map.83 = bf16[2,384,1024]{2,1,0:T(8,128)(2,1)} custom-call(bf16[6,384,1024]{2,1,0:T(8,128)(2,1)} %bitcast.49, bf16[6,384,1024]{2,1,0:T(8,128)(2,1)} %bitcast.50, bf16[6,384,1024]{2,1,0:T(8,128)(2,1)} %bitcast.51, bf16[16,1024]{1,0:T(8,128)(2,1)} %select_convert_fusion.1.refs_9_.bias_ref, ...), custom_call_target="tpu_custom_call", output_to_operand_aliasing={{}: (7, {})} | custom-call | tf_op jit(solution)/shard_map/pallas_call | solution.py:208
  123.4 0.8 fusion.46
  124.2 0.8 fusion.48
  124.9 0.8 fusion.50
  125.8 0.9 fusion.51
  126.7 0.9 fusion.49
  127.6 1.0 fusion.47
  128.6 1.0 fusion.45
  129.8 1.1 slice_dynamic-update-slice_fusion.1
  131.0 0.9 slice_dynamic-update-slice_fusion
  131.9 1.5 %fusion.7 = bf16[1024,768]{1,0:T(8,128)(2,1)S(1)} fusion(bf16[1024,768]{1,0:T(8,128)(2,1)S(1)} %copy-done.2, bf16[768,1024]{1,0:T(8,128)(2,1)S(1)} %slice_dynamic-update-slice_fusion, bf16[768,768]{1,0:T(8,128)(2,1)S(1)} %copy-done.8, pred[1024]{0:T(1024)(128)(4,1)S(1)} %fusion.34), kind=kOutput, calls=%fused_computation.12 | convolution fusion | flops 1211105280 | bytes 5899264 | tf_op jit(solution)/shard_map/dot_general | solution.py:237
  133.5 2.0 %copy.37 = bf16[128,8,768]{2,1,0:T(8,128)(2,1)} copy(bf16[128,8,768]{2,0,1:T(8,128)(2,1)S(1)} %bitcast.65) | data formatting | bytes 3145728 | tf_op jit(solution)/shard_map/transpose | solution.py:241
  (46 shorter events, 1.7 us)
Async XLA Ops:
  0.0 8.8 %copy-start = (bf16[1024,1536]{1,0:T(8,128)(2,1)S(1)}, bf16[1024,1536]{1,0:T(8,128)(2,1)}, u32[]{:S(2)}) copy-start(bf16[1024,1536]{1,0:T(8,128)(2,1)} %param.8) | copy-start | bytes 9437188
  1.5 14.4 %all-to-all-start = ((s32[32,1,32]{2,1,0:T(1,128)}), s32[32,1,32]{2,1,0:T(1,128)S(1)}, u32[]{:S(2)}, u32[]{:S(2)}) async-start(s32[32,1,32]{2,1,0:T(1,128)} %all_to_all.12), calls=%async_computation | async-start | bytes 32768 | tf_op jit(solution)/shard_map/all_to_all | solution.py:122
  16.0 41.9 %all-to-all-start.1 = ((bf16[32,32,768]{2,1,0:T(8,128)(2,1)}), bf16[32,32,768]{2,1,0:T(8,128)(2,1)}, u32[]{:S(2)}, u32[]{:S(2)}) async-start(bf16[32,32,768]{2,1,0:T(8,128)(2,1)} %bitcast.62), calls=%async_computation.1 | async-start | bytes 3145728 | tf_op jit(solution)/shard_map/all_to_all | solution.py:115
  61.3 1.3 copy-start.1
  61.3 0.7 copy-start.6
  62.0 1.3 copy-start.5
  62.6 1.4 %copy-start.3 = (bf16[1024,768]{1,0:T(8,128)(2,1)}, bf16[1024,768]{1,0:T(8,128)(2,1)S(1)}, u32[]{:S(2)}) copy-start(bf16[1024,768]{1,0:T(8,128)(2,1)S(1)} %fusion.5) | copy-start | bytes 4718596
  63.3 1.3 copy-start.4
  67.6 5.5 %copy-start.7 = (s32[16]{0:T(128)S(1)}, s32[16]{0:T(128)}, u32[]{:S(2)}) copy-start(s32[16]{0:T(128)} %constant.81.clone) | copy-start | bytes 196
  67.6 44.5 %all-to-all-start.2 = ((bf16[8,2,16,48,128]{4,3,2,1,0:T(8,128)(2,1)}), bf16[8,2,16,48,128]{4,3,2,1,0:T(8,128)(2,1)}, u32[]{:S(2)}, u32[]{:S(2)}) async-start(bf16[8,2,16,48,128]{4,3,2,1,0:T(8,128)(2,1)} %broadcast_in_dim.48), calls=%async_computation.2 | async-start | bytes 6291456 | tf_op jit(solution)/shard_map/all_to_all | solution.py:166
  129.7 2.2 %copy-start.2 = (bf16[1024,768]{1,0:T(8,128)(2,1)S(1)}, bf16[1024,768]{1,0:T(8,128)(2,1)}, u32[]{:S(2)}) copy-start(bf16[1024,768]{1,0:T(8,128)(2,1)} %copy-done.1) | copy-start | bytes 4718596
  129.7 2.2 %copy-start.8 = (bf16[768,768]{1,0:T(8,128)(2,1)S(1)}, bf16[768,768]{1,0:T(8,128)(2,1)}, u32[]{:S(2)}) copy-start(bf16[768,768]{1,0:T(8,128)(2,1)} %param.14) | copy-start | bytes 3538948

commit v14 on v11

--- a/solution.py
+++ b/solution.py
@@ -123,17 +123,21 @@
     projected = jnp.dot(embeddings, in_weight, preferred_element_type=jnp.float32).astype(
         jnp.bfloat16
     )
-    arrived = lax.all_to_all(
-        projected.reshape(device_count, block_rows, width),
+    destination = jnp.arange(rows, dtype=jnp.int32) // block_rows
+    own_slot = slot - destination * rows
+    digits = jnp.stack([own_slot // 32, own_slot % 32], axis=1).astype(jnp.bfloat16)
+    sent = jnp.concatenate([projected, jnp.pad(digits, ((0, 0), (0, 126)))], axis=1)
+    received = lax.all_to_all(
+        sent.reshape(device_count, block_rows, width + 128),
         ("tile", "seq"),
         split_axis=0,
         concat_axis=0,
         tiled=True,
-    ).reshape(rows, width)
-    arrived_slot = lax.all_to_all(
-        slot.reshape(device_count, block_rows), ("tile", "seq"), split_axis=0, concat_axis=0, tiled=True
-    ).reshape(rows)
-    local_slot = arrived_slot - my_index * rows
+    ).reshape(rows, width + 128)
+    arrived = received[:, :width]
+    local_slot = (
+        received[:, width].astype(jnp.int32) * 32 + received[:, width + 1].astype(jnp.int32)
+    )
     stored_slot = (local_slot % DILATION_RATE) * group_rows + local_slot // DILATION_RATE
     placement = (
         stored_slot[None, :] == jnp.arange(rows, dtype=jnp.int32)[:, None]

time: 131 us -> 136 us (1.038)
  starting transfers between devices: 16.2 us -> 12.2 us
  waiting for transfers between devices: 31.4 us -> 35.2 us
  other arithmetic: 3.09 us -> 6.64 us
  local copies, waits for them, and re-layouts: 15.4 us -> 18.5 us
    all_to_all x2 -> x1, starting transfers between devices: 11.5 us -> 7.41 us  [body(): lax.all_to_all(sent.reshape(device_count, block_rows, width + 128), ('til...]
    all_to_all x2 -> x1, waiting for transfers between devices: 31.4 us -> 35.2 us  [body(): lax.all_to_all(sent.reshape(device_count, block_rows, width + 128), ('til...]
    concatenate x0 -> x1, local copies, waits for them, and re-layouts: none -> 3.8 us  [body(): jnp.concatenate([projected, jnp.pad(digits, ((0, 0), (0, 126)))], axis=1)]
    all_to_all x1 -> x0, local copies, waits for them, and re-layouts: 1.52 us -> none  [body(): lax.all_to_all(slot.reshape(device_count, block_rows), ('tile', 'seq'), s...]
    concatenate x0 -> x1, other arithmetic: none -> 1.38 us  [body(): jnp.concatenate([projected, jnp.pad(digits, ((0, 0), (0, 126)))], axis=1)]
  transfers between devices with their start and end apart: 3 -> 2, of which waited for: 2 -> 1; matrix products, arithmetic and copies ran while one was open for 18% -> 14% of each run, Pallas kernels for 23% -> 22%
where the time goes in v14:
time: 136 us; the launch traced here: 135 us
  Pallas kernels  40.6 us (30%)
  waiting for transfers between devices  35.2 us (26%)
  matrix products  21.2 us (16%)
  local copies, waits for them, and re-layouts  18.5 us (14%)
  starting transfers between devices  12.2 us (9%)
  other arithmetic  6.64 us (5%)
    all_to_all x1, waiting for transfers between devices, body(): lax.all_to_all(sent.reshape(device_count, block_rows, width + 128), ('til...  35.2 us
    pallas_call x1, Pallas kernels, body(): pl.pallas_call(functools.partial(nearby_kernel, groups=DILATION_RATE, gro...  29.3 us
    pallas_call x1, Pallas kernels, body(): pl.pallas_call(functools.partial(dilated_kernel, factor=factor), grid=(ha...  11.3 us
    dot_general x1, matrix products, body(): lax.dot_general(qkv_weight, normed, (((0,), (1,)), ((), ())), preferred_e...  8.48 us
    all_to_all x1, starting transfers between devices, body(): lax.all_to_all(sent.reshape(device_count, block_rows, width + 128), ('til...  7.41 us
    unnamed x16, local copies, waits for them, and re-layouts  7.09 us
    all_to_all x1, starting transfers between devices, body(): lax.all_to_all(jnp.broadcast_to(own_far[None], (seq_count,) + own_far.sha...  4.78 us
    dot_general x1, matrix products, body(): jnp.dot(embeddings, in_weight, preferred_element_type=jnp.float32)  4.32 us
  transfers between devices with their start and end apart: 2, of which 1 were waited for; matrix products, arithmetic and copies ran while one was open for 14% of the time, Pallas kernels for 22%

profile of v14, /device:TPU:0, one launch (start us, length us, event | category | flops | bytes accessed | tf_op | source)
XLA Modules:
  0.0 135.2 jit_solution(14907046418869171281)
XLA Ops:
  0.0 0.0 copy-start
  0.0 0.9 fusion.42
  0.9 1.0 copy-done
  1.9 4.3 %convolution_convert_fusion.1 = bf16[1024,768]{0,1:T(8,128)(2,1)S(1)} fusion(bf16[1024,1536]{1,0:T(8,128)(2,1)S(1)} %copy-done, bf16[1536,768]{1,0:T(8,128)(2,1)} %param.11), kind=kOutput, calls=%fused_computation.16 | convolution fusion | flops 2416705536 | bytes 7077888 | tf_op jit(solution)/shard_map/dot_general | solution.py:123
  6.2 1.4 %pad_maximum_fusion = bf16[1024,896]{0,1:T(8,128)(2,1)} fusion(bf16[1024,128]{0,1:T(8,128)(2,1)S(1)} %fusion.29, bf16[1024,768]{0,1:T(8,128)(2,1)S(1)} %convolution_convert_fusion.1), kind=kLoop, calls=%fused_computation.14 | loop fusion | flops 3670016 | bytes 3670016 | tf_op jit(solution)/shard_map/concatenate | solution.py:129
  7.6 3.8 %copy.21 = bf16[1024,896]{1,0:T(8,128)(2,1)} copy(bf16[1024,896]{0,1:T(8,128)(2,1)} %pad_maximum_fusion) | data formatting | bytes 3670016 | tf_op jit(solution)/shard_map/concatenate | solution.py:129
  11.4 7.4 %all-to-all-start = ((bf16[32,32,896]{2,1,0:T(8,128)(2,1)}), bf16[32,32,896]{2,1,0:T(8,128)(2,1)}, u32[]{:S(2)}, u32[]{:S(2)}) async-start(bf16[32,32,896]{2,1,0:T(8,128)(2,1)} %bitcast.45), calls=%async_computation | async-start | bytes 3670016 | tf_op jit(solution)/shard_map/all_to_all | solution.py:130
  18.8 3.2 %fusion.56 = (bf16[768,768]{1,0:T(8,128)(2,1)}, bf16[768,768]{1,0:T(8,128)(2,1)}) fusion(bf16[768,2304]{1,0:T(8,128)(2,1)} %param.13), kind=kLoop, calls=%fused_computation.85 | loop fusion | bytes 4718592 | tf_op jit(solution)/shard_map/slice | solution.py:171
  22.1 2.4 %copy.32 = bf16[768,768]{0,1:T(8,128)(2,1)} copy(bf16[768,768]{1,0:T(8,128)(2,1)} %get-tuple-element.5) | data formatting | bytes 2359296
  24.5 2.4 %copy.33 = bf16[768,768]{0,1:T(8,128)(2,1)} copy(bf16[768,768]{1,0:T(8,128)(2,1)} %get-tuple-element.6) | data formatting | bytes 2359296
  26.8 35.2 %all-to-all-done = bf16[32,32,896]{2,1,0:T(8,128)(2,1)} async-done(((bf16[32,32,896]{2,1,0:T(8,128)(2,1)}), bf16[32,32,896]{2,1,0:T(8,128)(2,1)}, u32[]{:S(2)}, u32[]{:S(2)}) %all-to-all-start) | async-done | bytes 1835040 | tf_op jit(solution)/shard_map/all_to_all | solution.py:130
  62.0 1.3 add_reduce_fusion
  63.4 0.0 copy-start.5
  63.4 3.4 %convert_reduce_fusion = (f32[1024]{0:T(1024)S(1)}, bf16[1024,768]{1,0:T(8,128)(2,1)S(1)}) fusion(bf16[1024,896]{1,0:T(8,128)(2,1)} %bitcast.2, s32[1024]{0:T(1024)S(1)} %fusion.45), kind=kOutput, calls=%fused_computation.3 | convolution fusion | flops 1614019584 | bytes 3153920 | tf_op jit(solution)/shard_map/dot_general | solution.py:145
  66.8 0.0 copy-start.1
  66.8 0.6 fusion.3
  67.5 0.5 fusion.5
  68.1 0.7 copy-done.4
  68.8 0.6 fusion.24
  69.4 0.6 copy-done.3
  70.0 0.6 fusion.21
  70.7 2.4 %broadcast_in_dim.48 = bf16[8,2,16,48,128]{4,3,2,1,0:T(8,128)(2,1)} broadcast(bf16[2,16,48,128]{3,2,1,0:T(8,128)(2,1)S(1)} %pad_maximum_fusion.1), dimensions={1,2,3,4} | broadcast | bytes 3538944 | tf_op jit(solution)/shard_map/broadcast_in_dim | solution.py:182
  73.1 4.8 %all-to-all-start.1 = ((bf16[8,2,16,48,128]{4,3,2,1,0:T(8,128)(2,1)}), bf16[8,2,16,48,128]{4,3,2,1,0:T(8,128)(2,1)}, u32[]{:S(2)}, u32[]{:S(2)}) async-start(bf16[8,2,16,48,128]{4,3,2,1,0:T(8,128)(2,1)} %broadcast_in_dim.48), calls=%async_computation.1 | async-start | bytes 6291456 | tf_op jit(solution)/shard_map/all_to_all | solution.py:181
  78.6 0.1 add_compare_fusion
  78.7 0.7 select_convert_fusion.1.bias_ref
  79.4 1.0 select_convert_fusion.fbias_ref
  80.4 8.5 %convolution_convert_fusion = bf16[1024,2304]{0,1:T(8,128)(2,1)} fusion(bf16[1024,768]{1,0:T(8,128)(2,1)} %copy-done.2, bf16[768,2304]{1,0:T(8,128)(2,1)} %param.13), kind=kOutput, calls=%fused_computation | convolution fusion | flops 3626237952 | bytes 9830400 | tf_op jit(solution)/shard_map/dot_general | solution.py:159
  88.9 29.3 %shard_map.82 = bf16[768,1024]{1,0:T(8,128)(2,1)} custom-call(bf16[2304,1024]{1,0:T(8,128)(2,1)} %bitcast.39, bf16[2304,1024]{1,0:T(8,128)(2,1)} %bitcast.40, bf16[2304,1024]{1,0:T(8,128)(2,1)} %bitcast.41, bf16[16,1024]{1,0:T(8,128)(2,1)} %select_convert_fusion.1.bias_ref), custom_call_target="tpu_custom_call" | custom-call | tf_op jit(solution)/shard_map/pallas_call | solution.py:201
  118.2 0.0 all-to-all-done.1
  118.2 11.3 %shard_map.83 = bf16[2,384,1024]{2,1,0:T(8,128)(2,1)} custom-call(bf16[6,384,1024]{2,1,0:T(8,128)(2,1)} %bitcast.42, bf16[6,384,1024]{2,1,0:T(8,128)(2,1)} %bitcast.43, bf16[6,384,1024]{2,1,0:T(8,128)(2,1)} %bitcast.44, bf16[16,1024]{1,0:T(8,128)(2,1)} %select_convert_fusion.1.bias_ref, ...), custom_call_target="tpu_custom_call", output_to_operand_aliasing={{}: (7, {})} | custom-call | tf_op jit(solution)/shard_map/pallas_call | solution.py:218
  129.5 3.7 %fusion.7 = bf16[1024,768]{1,0:T(8,128)(2,1)S(1)} fusion(bf16[1024,768]{1,0:T(8,128)(2,1)} %copy-done.1, bf16[768,1024]{1,0:T(8,128)(2,1)} %bitcast.47, bf16[768,768]{1,0:T(8,128)(2,1)} %param.14, pred[1024]{0:T(1024)(128)(4,1)S(1)} %fusion.38), kind=kOutput, calls=%fused_computation.12 | convolution fusion | flops 1211105280 | bytes 5899264 | tf_op jit(solution)/shard_map/dot_general | solution.py:239
  133.2 2.0 %copy.47 = bf16[128,8,768]{2,1,0:T(8,128)(2,1)} copy(bf16[128,8,768]{2,0,1:T(8,128)(2,1)S(1)} %bitcast.50) | data formatting | bytes 3145728 | tf_op jit(solution)/shard_map/transpose | solution.py:243
  (21 shorter events, 0.2 us)
Async XLA Ops:
  0.0 1.9 %copy-start = (bf16[1024,1536]{1,0:T(8,128)(2,1)S(1)}, bf16[1024,1536]{1,0:T(8,128)(2,1)}, u32[]{:S(2)}) copy-start(bf16[1024,1536]{1,0:T(8,128)(2,1)} %param.8) | copy-start | bytes 9437188
  11.4 50.6 %all-to-all-start = ((bf16[32,32,896]{2,1,0:T(8,128)(2,1)}), bf16[32,32,896]{2,1,0:T(8,128)(2,1)}, u32[]{:S(2)}, u32[]{:S(2)}) async-start(bf16[32,32,896]{2,1,0:T(8,128)(2,1)} %bitcast.45), calls=%async_computation | async-start | bytes 3670016 | tf_op jit(solution)/shard_map/all_to_all | solution.py:130
  63.4 4.1 %copy-start.5 = (f32[768]{0:T(1024)S(1)}, f32[768]{0:T(1024)}, u32[]{:S(2)}) copy-start(f32[768]{0:T(1024)} %param.12) | copy-start | bytes 9220
  66.8 1.2 copy-start.1
  67.5 1.3 copy-start.4
  68.1 1.4 copy-start.2
  68.8 1.3 copy-start.3
  73.1 5.5 %copy-start.6 = (s32[16]{0:T(128)S(1)}, s32[16]{0:T(128)}, u32[]{:S(2)}) copy-start(s32[16]{0:T(128)} %constant.111.clone) | copy-start | bytes 196
  73.1 45.1 %all-to-all-start.1 = ((bf16[8,2,16,48,128]{4,3,2,1,0:T(8,128)(2,1)}), bf16[8,2,16,48,128]{4,3,2,1,0:T(8,128)(2,1)}, u32[]{:S(2)}, u32[]{:S(2)}) async-start(bf16[8,2,16,48,128]{4,3,2,1,0:T(8,128)(2,1)} %broadcast_in_dim.48), calls=%async_computation.1 | async-start | bytes 6291456 | tf_op jit(solution)/shard_map/all_to_all | solution.py:181

commit v15 on v12

--- a/solution.py
+++ b/solution.py
@@ -36,17 +36,19 @@
 
 
 def nearby_kernel(
-    qt_ref, kt_ref, vt_ref, bias_ref, o_ref, keys_ref, *, groups, group_rows, factor
+    qa_ref, qb_ref, ka_ref, kb_ref, va_ref, vb_ref, bias_ref, o_ref, keys_ref,
+    *, groups, group_rows, factor
 ):
     key_count = keys_ref.shape[1]
     block = QUERY_BLOCK
     ones = ones_row(block)
-    for pair in range(2):
-        keys_ref[pair] = extend(kt_ref[pair], bias_ref[...]).T
-    for pair in range(2):
+    heads = ((qa_ref, ka_ref, va_ref), (qb_ref, kb_ref, vb_ref))
+    for pair, (_, kt_ref, _) in enumerate(heads):
+        keys_ref[pair] = extend(kt_ref[...], bias_ref[...]).T
+    for pair, (qt_ref, _, vt_ref) in enumerate(heads):
         for first_row in range(0, groups * group_rows, block):
             rows = pl.ds(first_row, block)
-            queries_t = extend(qt_ref[pair, :, rows], ones)
+            queries_t = extend(qt_ref[:, rows], ones)
             top = None
             for first in range(0, key_count, PASS1):
                 scores_t = jnp.dot(
@@ -67,7 +69,7 @@
                 weights_t = jnp.exp2((scores_t - top) * factor)
                 part = jnp.sum(weights_t, axis=0, keepdims=True)
                 step = jnp.dot(
-                    vt_ref[pair, :, pl.ds(first, PASS2)],
+                    vt_ref[:, pl.ds(first, PASS2)],
                     weights_t.astype(jnp.bfloat16),
                     preferred_element_type=jnp.float32,
                 )
@@ -186,23 +188,28 @@
         extra_row[None] & (far_position >= slide_length)[:, None, :], big_negative, 0.0
     ).astype(jnp.bfloat16)
 
-    bias_block = pl.BlockSpec((16, rows), lambda i: (0, 0))
+    query_block = pl.BlockSpec((head_size, rows), lambda h: (h, 0))
+    keys_block = pl.BlockSpec((head_size, rows), lambda h: (HEAD_COUNT + h, 0))
+    values_block = pl.BlockSpec((head_size, rows), lambda h: (2 * HEAD_COUNT + h, 0))
+    bias_block = pl.BlockSpec((16, rows), lambda h: (0, 0))
     factor = scale * 1.4426950408889634
-    paired = projected_t.reshape(6, half * head_size, rows)
-    head_pairs = [
-        pl.BlockSpec((2, head_size, rows), lambda i, part=part: (part, i, 0)) for part in range(3)
-    ]
+    half = HEAD_COUNT // 2
     nearby = pl.pallas_call(
         functools.partial(
             nearby_kernel, groups=DILATION_RATE, group_rows=group_rows, factor=factor
         ),
         grid=(half,),
-        in_specs=head_pairs + [bias_block],
-        out_specs=head_pairs[0],
+        in_specs=[
+            pl.BlockSpec((head_size, rows), lambda i, first=first: (first + i, 0))
+            for first in range(0, 3 * HEAD_COUNT, half)
+        ]
+        + [pl.BlockSpec((16, rows), lambda i: (0, 0))],
+        out_specs=pl.BlockSpec((2, head_size, rows), lambda i: (0, i, 0)),
         out_shape=jax.ShapeDtypeStruct((2, half * head_size, rows), jnp.bfloat16),
         scratch_shapes=[pltpu.VMEM((2, rows, head_size + 16), jnp.bfloat16)],
-    )(paired, paired, paired, near_bias)
-
+    )(*([projected_t] * 6), near_bias)
+
+    paired = projected_t.reshape(6, half * head_size, rows)
     far_paired = far.reshape(seq_count, 2, 2, half, head_size, group_rows)
     group_block = pl.BlockSpec(
         (2, head_size, group_rows), lambda i: (0, i, i % DILATION_RATE)

time: 136 us -> 130 us (0.956)
  local copies, waits for them, and re-layouts: 21.9 us -> 15.4 us
    convert_element_type x1 -> x0, local copies, waits for them, and re-layouts: 6.63 us -> none  [body(): projected_t = lax.dot_general(qkv_weight, normed, (((0,), (1,)), ((), ())...]
  transfers between devices with their start and end apart: 3 -> 3, of which waited for: 2 -> 2; matrix products, arithmetic and copies ran while one was open for 22% -> 18% of each run, Pallas kernels for 21% -> 22%
where the time goes in v15:
time: 130 us; the launch traced here: 129 us
  Pallas kernels  39.7 us (31%)
  waiting for transfers between devices  31.4 us (24%)
  matrix products  22.2 us (17%)
  starting transfers between devices  16.2 us (12%)
  local copies, waits for them, and re-layouts  15.4 us (12%)
  other arithmetic  3.09 us (2%)
    all_to_all x1, waiting for transfers between devices, body(): lax.all_to_all(projected.reshape(device_count, block_rows, width), ('tile...  29.6 us
    pallas_call x1, Pallas kernels, body(): pl.pallas_call(functools.partial(nearby_kernel, groups=DILATION_RATE, gro...  28.4 us
    pallas_call x1, Pallas kernels, body(): pl.pallas_call(functools.partial(dilated_kernel, factor=factor), grid=(ha...  11.3 us
    dot_general x1, matrix products, body(): lax.dot_general(qkv_weight, normed, (((0,), (1,)), ((), ())), preferred_e...  8.48 us
    all_to_all x1, starting transfers between devices, body(): lax.all_to_all(slot.reshape(device_count, block_rows), ('tile', 'seq'), s...  7.3 us
    unnamed x16, local copies, waits for them, and re-layouts  6.15 us
    dot_general x1, matrix products, body(): jnp.dot(embeddings, in_weight, preferred_element_type=jnp.float32)  5.34 us
    all_to_all x1, starting transfers between devices, body(): lax.all_to_all(jnp.broadcast_to(own_far[None], (seq_count,) + own_far.sha...  4.79 us
  transfers between devices with their start and end apart: 3, of which 2 were waited for; matrix products, arithmetic and copies ran while one was open for 18% of the time, Pallas kernels for 22%

profile of v15, /device:TPU:0, one launch (start us, length us, event | category | flops | bytes accessed | tf_op | source)
XLA Modules:
  0.0 128.9 jit_solution(17349116371836919669)
XLA Ops:
  0.0 1.5 %all_to_all.12 = s32[32,1,32]{2,1,0:T(1,128)} reshape(s32[1024]{0:T(1024)} %param.9) | data formatting | bytes 8192 | tf_op jit(solution)/shard_map/all_to_all | solution.py:132
  1.5 7.3 %all-to-all-start = ((s32[32,1,32]{2,1,0:T(1,128)}), s32[32,1,32]{2,1,0:T(1,128)S(1)}, u32[]{:S(2)}, u32[]{:S(2)}) async-start(s32[32,1,32]{2,1,0:T(1,128)} %all_to_all.12), calls=%async_computation | async-start | bytes 32768 | tf_op jit(solution)/shard_map/all_to_all | solution.py:132
  8.8 5.3 %convolution_convert_fusion.1 = bf16[1024,768]{1,0:T(8,128)(2,1)} fusion(bf16[1024,1536]{1,0:T(8,128)(2,1)S(1)} %copy-done, bf16[1536,768]{1,0:T(8,128)(2,1)} %param.11), kind=kOutput, calls=%fused_computation.15 | convolution fusion | flops 2416705536 | bytes 7077888 | tf_op jit(solution)/shard_map/dot_general | solution.py:122
  14.2 1.8 %all-to-all-done = s32[32,1,32]{2,1,0:T(1,128)S(1)} async-done(((s32[32,1,32]{2,1,0:T(1,128)}), s32[32,1,32]{2,1,0:T(1,128)S(1)}, u32[]{:S(2)}, u32[]{:S(2)}) %all-to-all-start) | async-done | bytes 4128 | tf_op jit(solution)/shard_map/all_to_all | solution.py:132
  16.0 4.2 %all-to-all-start.1 = ((bf16[32,32,768]{2,1,0:T(8,128)(2,1)}), bf16[32,32,768]{2,1,0:T(8,128)(2,1)}, u32[]{:S(2)}, u32[]{:S(2)}) async-start(bf16[32,32,768]{2,1,0:T(8,128)(2,1)} %bitcast.49), calls=%async_computation.1 | async-start | bytes 3145728 | tf_op jit(solution)/shard_map/all_to_all | solution.py:125
  20.1 3.2 %fusion.44 = (bf16[768,768]{1,0:T(8,128)(2,1)}, bf16[768,768]{1,0:T(8,128)(2,1)}) fusion(bf16[768,2304]{1,0:T(8,128)(2,1)} %param.13), kind=kLoop, calls=%fused_computation.62 | loop fusion | bytes 4718592 | tf_op jit(solution)/shard_map/slice | solution.py:166
  23.4 2.4 %copy.22 = bf16[768,768]{0,1:T(8,128)(2,1)} copy(bf16[768,768]{1,0:T(8,128)(2,1)} %get-tuple-element.5) | data formatting | bytes 2359296
  25.8 2.4 %copy.23 = bf16[768,768]{0,1:T(8,128)(2,1)} copy(bf16[768,768]{1,0:T(8,128)(2,1)} %get-tuple-element.6) | data formatting | bytes 2359296
  28.2 0.1 sub.34
  28.3 29.6 %all-to-all-done.1 = bf16[32,32,768]{2,1,0:T(8,128)(2,1)} async-done(((bf16[32,32,768]{2,1,0:T(8,128)(2,1)}), bf16[32,32,768]{2,1,0:T(8,128)(2,1)}, u32[]{:S(2)}, u32[]{:S(2)}) %all-to-all-start.1) | async-done | bytes 1572896 | tf_op jit(solution)/shard_map/all_to_all | solution.py:125
  57.9 3.4 %convert_reduce_fusion = (f32[1024]{0:T(1024)S(1)}, bf16[1024,768]{1,0:T(8,128)(2,1)S(1)}) fusion(bf16[1024,768]{1,0:T(8,128)(2,1)} %bitcast.2, s32[1024]{0:T(1024)S(1)} %fusion.36), kind=kOutput, calls=%fused_computation.3 | convolution fusion | flops 1614019584 | bytes 3153920 | tf_op jit(solution)/shard_map/dot_general | solution.py:140
  61.3 0.0 copy-start.1
  61.3 0.0 copy-start.5
  61.3 0.6 fusion.3
  62.0 0.1 copy-done.5
  62.0 0.5 fusion.5
  62.6 0.7 copy-done.4
  63.3 0.6 fusion.23
  63.9 0.0 copy-done.2
  64.0 0.6 copy-done.3
  64.6 0.6 fusion.20
  65.3 2.4 %broadcast_in_dim.48 = bf16[8,2,16,48,128]{4,3,2,1,0:T(8,128)(2,1)} broadcast(bf16[2,16,48,128]{3,2,1,0:T(8,128)(2,1)S(1)} %pad_maximum_fusion), dimensions={1,2,3,4} | broadcast | bytes 3538944 | tf_op jit(solution)/shard_map/broadcast_in_dim | solution.py:177
  67.6 4.8 %all-to-all-start.2 = ((bf16[8,2,16,48,128]{4,3,2,1,0:T(8,128)(2,1)}), bf16[8,2,16,48,128]{4,3,2,1,0:T(8,128)(2,1)}, u32[]{:S(2)}, u32[]{:S(2)}) async-start(bf16[8,2,16,48,128]{4,3,2,1,0:T(8,128)(2,1)} %broadcast_in_dim.48), calls=%async_computation.2 | async-start | bytes 6291456 | tf_op jit(solution)/shard_map/all_to_all | solution.py:176
  73.2 0.1 add_compare_fusion
  73.2 0.7 select_convert_fusion.1.bias_ref
  73.9 1.0 select_convert_fusion.fbias_ref
  75.0 8.5 %convolution_convert_fusion = bf16[1024,2304]{0,1:T(8,128)(2,1)} fusion(bf16[1024,768]{1,0:T(8,128)(2,1)} %copy-done.2, bf16[768,2304]{1,0:T(8,128)(2,1)} %param.13), kind=kOutput, calls=%fused_computation | convolution fusion | flops 3626237952 | bytes 9830400 | tf_op jit(solution)/shard_map/dot_general | solution.py:154
  83.4 28.4 %shard_map.82.prev_ref = bf16[2,384,1024]{2,1,0:T(8,128)(2,1)} custom-call(bf16[2304,1024]{1,0:T(8,128)(2,1)} %bitcast.39, bf16[2304,1024]{1,0:T(8,128)(2,1)} %bitcast.40, bf16[2304,1024]{1,0:T(8,128)(2,1)} %bitcast.41, bf16[2304,1024]{1,0:T(8,128)(2,1)} %bitcast.42, bf16[2304,1024]{1,0:T(8,128)(2,1)} %bitcast.43, bf16[2304,1024]{1,0:T(8,128)(2,1)} %bitcast.44, ...), custom_call_target="tpu_custom_call" | custom-call | tf_op jit(solution)/shard_map/pallas_call | solution.py:197
  111.8 0.0 all-to-all-done.2
  111.8 11.3 %shard_map.83 = bf16[2,384,1024]{2,1,0:T(8,128)(2,1)} custom-call(bf16[6,384,1024]{2,1,0:T(8,128)(2,1)} %bitcast.45, bf16[6,384,1024]{2,1,0:T(8,128)(2,1)} %bitcast.46, bf16[6,384,1024]{2,1,0:T(8,128)(2,1)} %bitcast.47, bf16[16,1024]{1,0:T(8,128)(2,1)} %select_convert_fusion.1.bias_ref, ...), custom_call_target="tpu_custom_call", output_to_operand_aliasing={{}: (7, {})} | custom-call | tf_op jit(solution)/shard_map/pallas_call | solution.py:218
  123.2 3.7 %fusion.7 = bf16[1024,768]{1,0:T(8,128)(2,1)S(1)} fusion(bf16[1024,768]{1,0:T(8,128)(2,1)} %copy-done.1, bf16[768,1024]{1,0:T(8,128)(2,1)} %bitcast.48, bf16[768,768]{1,0:T(8,128)(2,1)} %param.14, pred[1024]{0:T(1024)(128)(4,1)S(1)} %fusion.34), kind=kOutput, calls=%fused_computation.12 | convolution fusion | flops 1211105280 | bytes 5899264 | tf_op jit(solution)/shard_map/dot_general | solution.py:239
  126.9 2.0 %copy.37 = bf16[128,8,768]{2,1,0:T(8,128)(2,1)} copy(bf16[128,8,768]{2,0,1:T(8,128)(2,1)S(1)} %bitcast.52) | data formatting | bytes 3145728 | tf_op jit(solution)/shard_map/transpose | solution.py:243
  (19 shorter events, 0.2 us)
Async XLA Ops:
  0.0 8.8 %copy-start = (bf16[1024,1536]{1,0:T(8,128)(2,1)S(1)}, bf16[1024,1536]{1,0:T(8,128)(2,1)}, u32[]{:S(2)}) copy-start(bf16[1024,1536]{1,0:T(8,128)(2,1)} %param.8) | copy-start | bytes 9437188
  1.5 14.4 %all-to-all-start = ((s32[32,1,32]{2,1,0:T(1,128)}), s32[32,1,32]{2,1,0:T(1,128)S(1)}, u32[]{:S(2)}, u32[]{:S(2)}) async-start(s32[32,1,32]{2,1,0:T(1,128)} %all_to_all.12), calls=%async_computation | async-start | bytes 32768 | tf_op jit(solution)/shard_map/all_to_all | solution.py:132
  16.0 41.9 %all-to-all-start.1 = ((bf16[32,32,768]{2,1,0:T(8,128)(2,1)}), bf16[32,32,768]{2,1,0:T(8,128)(2,1)}, u32[]{:S(2)}, u32[]{:S(2)}) async-start(bf16[32,32,768]{2,1,0:T(8,128)(2,1)} %bitcast.49), calls=%async_computation.1 | async-start | bytes 3145728 | tf_op jit(solution)/shard_map/all_to_all | solution.py:125
  61.3 1.3 copy-start.1
  61.3 0.7 copy-start.5
  62.0 1.3 copy-start.4
  62.6 1.4 %copy-start.2 = (bf16[1024,768]{1,0:T(8,128)(2,1)}, bf16[1024,768]{1,0:T(8,128)(2,1)S(1)}, u32[]{:S(2)}) copy-start(bf16[1024,768]{1,0:T(8,128)(2,1)S(1)} %fusion.5) | copy-start | bytes 4718596
  63.3 1.3 copy-start.3
  67.6 5.5 %copy-start.6 = (s32[16]{0:T(128)S(1)}, s32[16]{0:T(128)}, u32[]{:S(2)}) copy-start(s32[16]{0:T(128)} %constant.81.clone) | copy-start | bytes 196
  67.6 44.2 %all-to-all-start.2 = ((bf16[8,2,16,48,128]{4,3,2,1,0:T(8,128)(2,1)}), bf16[8,2,16,48,128]{4,3,2,1,0:T(8,128)(2,1)}, u32[]{:S(2)}, u32[]{:S(2)}) async-start(bf16[8,2,16,48,128]{4,3,2,1,0:T(8,128)(2,1)} %broadcast_in_dim.48), calls=%async_computation.2 | async-start | bytes 6291456 | tf_op jit(solution)/shard_map/all_to_all | solution.py:176

commit v16 on v15

--- a/solution.py
+++ b/solution.py
@@ -9,7 +9,7 @@
 
 HEAD_COUNT = 16
 QUERY_BLOCK = 1024
-PASS1 = 1024
+PASS1 = 512
 PASS2 = 512
 DILATION_RATE = 8
 

time: 130 us -> 128 us (0.985)
  Pallas kernels: 39.7 us -> 37.1 us
    pallas_call x1, Pallas kernels: 28.4 us -> 25.8 us  [body(): pl.pallas_call(functools.partial(nearby_kernel, groups=DILATION_RATE, gro...]
  transfers between devices with their start and end apart: 3 -> 3, of which waited for: 2 -> 3; matrix products, arithmetic and copies ran while one was open for 18% -> 19% of each run, Pallas kernels for 22% -> 20%
where the time goes in v16:
time: 128 us; the launch traced here: 127 us
  Pallas kernels  37.1 us (29%)
  waiting for transfers between devices  32.3 us (25%)
  matrix products  22.2 us (17%)
  starting transfers between devices  16.2 us (13%)
  local copies, waits for them, and re-layouts  15.4 us (12%)
  other arithmetic  3.09 us (2%)
    all_to_all x1, waiting for transfers between devices, body(): lax.all_to_all(projected.reshape(device_count, block_rows, width), ('tile...  29.6 us
    pallas_call x1, Pallas kernels, body(): pl.pallas_call(functools.partial(nearby_kernel, groups=DILATION_RATE, gro...  25.8 us
    pallas_call x1, Pallas kernels, body(): pl.pallas_call(functools.partial(dilated_kernel, factor=factor), grid=(ha...  11.3 us
    dot_general x1, matrix products, body(): lax.dot_general(qkv_weight, normed, (((0,), (1,)), ((), ())), preferred_e...  8.48 us
    all_to_all x1, starting transfers between devices, body(): lax.all_to_all(slot.reshape(device_count, block_rows), ('tile', 'seq'), s...  7.3 us
    unnamed x16, local copies, waits for them, and re-layouts  6.15 us
    dot_general x1, matrix products, body(): jnp.dot(embeddings, in_weight, preferred_element_type=jnp.float32)  5.34 us
    all_to_all x1, starting transfers between devices, body(): lax.all_to_all(jnp.broadcast_to(own_far[None], (seq_count,) + own_far.sha...  4.79 us
  transfers between devices with their start and end apart: 3, of which 3 were waited for; matrix products, arithmetic and copies ran while one was open for 19% of the time, Pallas kernels for 20%

profile of v16, /device:TPU:0, one launch (start us, length us, event | category | flops | bytes accessed | tf_op | source)
XLA Modules:
  0.0 127.2 jit_solution(12201902297347844891)
XLA Ops:
  0.0 1.5 %all_to_all.12 = s32[32,1,32]{2,1,0:T(1,128)} reshape(s32[1024]{0:T(1024)} %param.9) | data formatting | bytes 8192 | tf_op jit(solution)/shard_map/all_to_all | solution.py:132
  1.5 7.3 %all-to-all-start = ((s32[32,1,32]{2,1,0:T(1,128)}), s32[32,1,32]{2,1,0:T(1,128)S(1)}, u32[]{:S(2)}, u32[]{:S(2)}) async-start(s32[32,1,32]{2,1,0:T(1,128)} %all_to_all.12), calls=%async_computation | async-start | bytes 32768 | tf_op jit(solution)/shard_map/all_to_all | solution.py:132
  8.8 5.3 %convolution_convert_fusion.1 = bf16[1024,768]{1,0:T(8,128)(2,1)} fusion(bf16[1024,1536]{1,0:T(8,128)(2,1)S(1)} %copy-done, bf16[1536,768]{1,0:T(8,128)(2,1)} %param.11), kind=kOutput, calls=%fused_computation.15 | convolution fusion | flops 2416705536 | bytes 7077888 | tf_op jit(solution)/shard_map/dot_general | solution.py:122
  14.2 1.8 %all-to-all-done = s32[32,1,32]{2,1,0:T(1,128)S(1)} async-done(((s32[32,1,32]{2,1,0:T(1,128)}), s32[32,1,32]{2,1,0:T(1,128)S(1)}, u32[]{:S(2)}, u32[]{:S(2)}) %all-to-all-start) | async-done | bytes 4128 | tf_op jit(solution)/shard_map/all_to_all | solution.py:132
  16.0 4.2 %all-to-all-start.1 = ((bf16[32,32,768]{2,1,0:T(8,128)(2,1)}), bf16[32,32,768]{2,1,0:T(8,128)(2,1)}, u32[]{:S(2)}, u32[]{:S(2)}) async-start(bf16[32,32,768]{2,1,0:T(8,128)(2,1)} %bitcast.49), calls=%async_computation.1 | async-start | bytes 3145728 | tf_op jit(solution)/shard_map/all_to_all | solution.py:125
  20.1 3.2 %fusion.44 = (bf16[768,768]{1,0:T(8,128)(2,1)}, bf16[768,768]{1,0:T(8,128)(2,1)}) fusion(bf16[768,2304]{1,0:T(8,128)(2,1)} %param.13), kind=kLoop, calls=%fused_computation.62 | loop fusion | bytes 4718592 | tf_op jit(solution)/shard_map/slice | solution.py:166
  23.4 2.4 %copy.22 = bf16[768,768]{0,1:T(8,128)(2,1)} copy(bf16[768,768]{1,0:T(8,128)(2,1)} %get-tuple-element.5) | data formatting | bytes 2359296
  25.8 2.4 %copy.23 = bf16[768,768]{0,1:T(8,128)(2,1)} copy(bf16[768,768]{1,0:T(8,128)(2,1)} %get-tuple-element.6) | data formatting | bytes 2359296
  28.2 0.1 sub.34
  28.3 29.6 %all-to-all-done.1 = bf16[32,32,768]{2,1,0:T(8,128)(2,1)} async-done(((bf16[32,32,768]{2,1,0:T(8,128)(2,1)}), bf16[32,32,768]{2,1,0:T(8,128)(2,1)}, u32[]{:S(2)}, u32[]{:S(2)}) %all-to-all-start.1) | async-done | bytes 1572896 | tf_op jit(solution)/shard_map/all_to_all | solution.py:125
  57.9 3.4 %convert_reduce_fusion = (f32[1024]{0:T(1024)S(1)}, bf16[1024,768]{1,0:T(8,128)(2,1)S(1)}) fusion(bf16[1024,768]{1,0:T(8,128)(2,1)} %bitcast.2, s32[1024]{0:T(1024)S(1)} %fusion.36), kind=kOutput, calls=%fused_computation.3 | convolution fusion | flops 1614019584 | bytes 3153920 | tf_op jit(solution)/shard_map/dot_general | solution.py:140
  61.3 0.0 copy-start.1
  61.3 0.0 copy-start.5
  61.3 0.6 fusion.3
  62.0 0.1 copy-done.5
  62.0 0.5 fusion.5
  62.6 0.0 copy-done.1
  62.6 0.7 copy-done.4
  63.3 0.6 fusion.23
  64.0 0.6 copy-done.3
  64.6 0.6 fusion.20
  65.3 2.4 %broadcast_in_dim.48 = bf16[8,2,16,48,128]{4,3,2,1,0:T(8,128)(2,1)} broadcast(bf16[2,16,48,128]{3,2,1,0:T(8,128)(2,1)S(1)} %pad_maximum_fusion), dimensions={1,2,3,4} | broadcast | bytes 3538944 | tf_op jit(solution)/shard_map/broadcast_in_dim | solution.py:177
  67.6 4.8 %all-to-all-start.2 = ((bf16[8,2,16,48,128]{4,3,2,1,0:T(8,128)(2,1)}), bf16[8,2,16,48,128]{4,3,2,1,0:T(8,128)(2,1)}, u32[]{:S(2)}, u32[]{:S(2)}) async-start(bf16[8,2,16,48,128]{4,3,2,1,0:T(8,128)(2,1)} %broadcast_in_dim.48), calls=%async_computation.2 | async-start | bytes 6291456 | tf_op jit(solution)/shard_map/all_to_all | solution.py:176
  73.2 0.1 add_compare_fusion
  73.2 0.7 select_convert_fusion.1.bias_ref
  73.9 1.0 select_convert_fusion.fbias_ref
  75.0 8.5 %convolution_convert_fusion = bf16[1024,2304]{0,1:T(8,128)(2,1)} fusion(bf16[1024,768]{1,0:T(8,128)(2,1)} %copy-done.2, bf16[768,2304]{1,0:T(8,128)(2,1)} %param.13), kind=kOutput, calls=%fused_computation | convolution fusion | flops 3626237952 | bytes 9830400 | tf_op jit(solution)/shard_map/dot_general | solution.py:154
  83.4 25.8 %shard_map.82.prev_ref = bf16[2,384,1024]{2,1,0:T(8,128)(2,1)} custom-call(bf16[2304,1024]{1,0:T(8,128)(2,1)} %bitcast.39, bf16[2304,1024]{1,0:T(8,128)(2,1)} %bitcast.40, bf16[2304,1024]{1,0:T(8,128)(2,1)} %bitcast.41, bf16[2304,1024]{1,0:T(8,128)(2,1)} %bitcast.42, bf16[2304,1024]{1,0:T(8,128)(2,1)} %bitcast.43, bf16[2304,1024]{1,0:T(8,128)(2,1)} %bitcast.44, ...), custom_call_target="tpu_custom_call" | custom-call | tf_op jit(solution)/shard_map/pallas_call | solution.py:197
  109.2 0.9 all-to-all-done.2
  110.2 11.3 %shard_map.83 = bf16[2,384,1024]{2,1,0:T(8,128)(2,1)} custom-call(bf16[6,384,1024]{2,1,0:T(8,128)(2,1)} %bitcast.45, bf16[6,384,1024]{2,1,0:T(8,128)(2,1)} %bitcast.46, bf16[6,384,1024]{2,1,0:T(8,128)(2,1)} %bitcast.47, bf16[16,1024]{1,0:T(8,128)(2,1)} %select_convert_fusion.1.bias_ref, ...), custom_call_target="tpu_custom_call", output_to_operand_aliasing={{}: (7, {})} | custom-call | tf_op jit(solution)/shard_map/pallas_call | solution.py:218
  121.5 3.7 %fusion.7 = bf16[1024,768]{1,0:T(8,128)(2,1)S(1)} fusion(bf16[1024,768]{1,0:T(8,128)(2,1)} %copy-done.1, bf16[768,1024]{1,0:T(8,128)(2,1)} %bitcast.48, bf16[768,768]{1,0:T(8,128)(2,1)} %param.14, pred[1024]{0:T(1024)(128)(4,1)S(1)} %fusion.34), kind=kOutput, calls=%fused_computation.12 | convolution fusion | flops 1211105280 | bytes 5899264 | tf_op jit(solution)/shard_map/dot_general | solution.py:239
  125.2 2.0 %copy.37 = bf16[128,8,768]{2,1,0:T(8,128)(2,1)} copy(bf16[128,8,768]{2,0,1:T(8,128)(2,1)S(1)} %bitcast.52) | data formatting | bytes 3145728 | tf_op jit(solution)/shard_map/transpose | solution.py:243
  (19 shorter events, 0.2 us)
Async XLA Ops:
  0.0 8.8 %copy-start = (bf16[1024,1536]{1,0:T(8,128)(2,1)S(1)}, bf16[1024,1536]{1,0:T(8,128)(2,1)}, u32[]{:S(2)}) copy-start(bf16[1024,1536]{1,0:T(8,128)(2,1)} %param.8) | copy-start | bytes 9437188
  1.5 14.4 %all-to-all-start = ((s32[32,1,32]{2,1,0:T(1,128)}), s32[32,1,32]{2,1,0:T(1,128)S(1)}, u32[]{:S(2)}, u32[]{:S(2)}) async-start(s32[32,1,32]{2,1,0:T(1,128)} %all_to_all.12), calls=%async_computation | async-start | bytes 32768 | tf_op jit(solution)/shard_map/all_to_all | solution.py:132
  16.0 41.9 %all-to-all-start.1 = ((bf16[32,32,768]{2,1,0:T(8,128)(2,1)}), bf16[32,32,768]{2,1,0:T(8,128)(2,1)}, u32[]{:S(2)}, u32[]{:S(2)}) async-start(bf16[32,32,768]{2,1,0:T(8,128)(2,1)} %bitcast.49), calls=%async_computation.1 | async-start | bytes 3145728 | tf_op jit(solution)/shard_map/all_to_all | solution.py:125
  61.3 1.3 copy-start.1
  61.3 0.7 copy-start.5
  62.0 1.3 copy-start.4
  62.6 1.4 %copy-start.2 = (bf16[1024,768]{1,0:T(8,128)(2,1)}, bf16[1024,768]{1,0:T(8,128)(2,1)S(1)}, u32[]{:S(2)}) copy-start(bf16[1024,768]{1,0:T(8,128)(2,1)S(1)} %fusion.5) | copy-start | bytes 4718596
  63.3 1.3 copy-start.3
  67.6 5.5 %copy-start.6 = (s32[16]{0:T(128)S(1)}, s32[16]{0:T(128)}, u32[]{:S(2)}) copy-start(s32[16]{0:T(128)} %constant.81.clone) | copy-start | bytes 196
  67.6 42.5 %all-to-all-start.2 = ((bf16[8,2,16,48,128]{4,3,2,1,0:T(8,128)(2,1)}), bf16[8,2,16,48,128]{4,3,2,1,0:T(8,128)(2,1)}, u32[]{:S(2)}, u32[]{:S(2)}) async-start(bf16[8,2,16,48,128]{4,3,2,1,0:T(8,128)(2,1)} %broadcast_in_dim.48), calls=%async_computation.2 | async-start | bytes 6291456 | tf_op jit(solution)/shard_map/all_to_all | solution.py:176

commit v17 on v16

--- a/solution.py
+++ b/solution.py
@@ -35,16 +35,33 @@
     return jnp.where(row == 0, 1.0, 0.0).astype(jnp.bfloat16)
 
 
+def mask_rows(limit, width, position_of):
+    row = lax.broadcasted_iota(jnp.int32, (16, width), 0)
+    lane = lax.broadcasted_iota(jnp.int32, (16, width), 1)
+    invalid = (row == 0) & (position_of(lane) >= limit)
+    return jnp.where(invalid, big_negative, 0.0).astype(jnp.bfloat16)
+
+
+def near_mask(limits_ref, rows):
+    group_rows = rows // DILATION_RATE
+    return mask_rows(
+        limits_ref[0],
+        rows,
+        lambda lane: limits_ref[1] + (lane % group_rows) * DILATION_RATE + lane // group_rows,
+    )
+
+
 def nearby_kernel(
-    qa_ref, qb_ref, ka_ref, kb_ref, va_ref, vb_ref, bias_ref, o_ref, keys_ref,
+    qa_ref, qb_ref, ka_ref, kb_ref, va_ref, vb_ref, limits_ref, o_ref, keys_ref,
     *, groups, group_rows, factor
 ):
     key_count = keys_ref.shape[1]
     block = QUERY_BLOCK
     ones = ones_row(block)
     heads = ((qa_ref, ka_ref, va_ref), (qb_ref, kb_ref, vb_ref))
+    bias = near_mask(limits_ref, keys_ref.shape[1])
     for pair, (_, kt_ref, _) in enumerate(heads):
-        keys_ref[pair] = extend(kt_ref[...], bias_ref[...]).T
+        keys_ref[pair] = extend(kt_ref[...], bias).T
     for pair, (qt_ref, _, vt_ref) in enumerate(heads):
         for first_row in range(0, groups * group_rows, block):
             rows = pl.ds(first_row, block)
@@ -83,13 +100,20 @@
 
 
 def dilated_kernel(
-    qt_ref, kt_ref, vt_ref, bias_ref, fk_ref, fv_ref, fbias_ref, prev_ref, o_ref, *, factor
+    qt_ref, kt_ref, vt_ref, limits_ref, fk_ref, fv_ref, prev_ref, o_ref, *, factor
 ):
     del prev_ref
+    offset = pl.program_id(0) % DILATION_RATE
+    near_bias = near_mask(limits_ref, kt_ref.shape[2])
+    far_bias = mask_rows(
+        limits_ref[0],
+        fk_ref.shape[0] * fk_ref.shape[5],
+        lambda lane: lane * DILATION_RATE + offset,
+    )
     for pair in range(2):
         queries_t = extend(qt_ref[pair], ones_row(qt_ref.shape[2]))
-        near_keys = extend(kt_ref[pair], bias_ref[...]).T
-        far_keys = extend(joined(fk_ref, pair), fbias_ref[0]).T
+        near_keys = extend(kt_ref[pair], near_bias).T
+        far_keys = extend(joined(fk_ref, pair), far_bias).T
         near = jnp.dot(near_keys, queries_t, preferred_element_type=jnp.float32)
         far = jnp.dot(far_keys, queries_t, preferred_element_type=jnp.float32)
         top = jnp.maximum(
@@ -145,10 +169,7 @@
     stored = jnp.arange(rows, dtype=jnp.int32)
     local_position = (stored % group_rows) * DILATION_RATE + stored // group_rows
     position_ok = lax.axis_index("seq") * rows + local_position < slide_length
-    extra_row = lax.broadcasted_iota(jnp.int32, (16, 1), 0) == 0
-    near_bias = jnp.where(
-        extra_row & ~position_ok[None, :], big_negative, 0.0
-    ).astype(jnp.bfloat16)
+    limits = jnp.stack([slide_length, lax.axis_index("seq") * rows]).astype(jnp.int32)
 
     normed = normalize(features, norm_gain)
     projected_t = lax.dot_general(
@@ -180,18 +201,7 @@
         concat_axis=0,
         tiled=True,
     )
-    far_position = (
-        jnp.arange(far_count, dtype=jnp.int32)[None, :] * DILATION_RATE
-        + jnp.asarray(offsets, jnp.int32)[:, None]
-    )
-    far_bias = jnp.where(
-        extra_row[None] & (far_position >= slide_length)[:, None, :], big_negative, 0.0
-    ).astype(jnp.bfloat16)
-
-    query_block = pl.BlockSpec((head_size, rows), lambda h: (h, 0))
-    keys_block = pl.BlockSpec((head_size, rows), lambda h: (HEAD_COUNT + h, 0))
-    values_block = pl.BlockSpec((head_size, rows), lambda h: (2 * HEAD_COUNT + h, 0))
-    bias_block = pl.BlockSpec((16, rows), lambda h: (0, 0))
+    bias_block = pl.BlockSpec(memory_space=pltpu.SMEM)
     factor = scale * 1.4426950408889634
     half = HEAD_COUNT // 2
     nearby = pl.pallas_call(
@@ -203,11 +213,11 @@
             pl.BlockSpec((head_size, rows), lambda i, first=first: (first + i, 0))
             for first in range(0, 3 * HEAD_COUNT, half)
         ]
-        + [pl.BlockSpec((16, rows), lambda i: (0, 0))],
+        + [bias_block],
         out_specs=pl.BlockSpec((2, head_size, rows), lambda i: (0, i, 0)),
         out_shape=jax.ShapeDtypeStruct((2, half * head_size, rows), jnp.bfloat16),
         scratch_shapes=[pltpu.VMEM((2, rows, head_size + 16), jnp.bfloat16)],
-    )(*([projected_t] * 6), near_bias)
+    )(*([projected_t] * 6), limits)
 
     paired = projected_t.reshape(6, half * head_size, rows)
     far_paired = far.reshape(seq_count, 2, 2, half, head_size, group_rows)
@@ -225,14 +235,13 @@
             bias_block,
             pl.BlockSpec(far_block, lambda i: (0, 0, 0, i, 0, 0)),
             pl.BlockSpec(far_block, lambda i: (0, 1, 0, i, 0, 0)),
-            pl.BlockSpec((1, 16, far_count), lambda i: (i, 0, 0)),
             pl.BlockSpec(memory_space=pl.ANY),
         ],
         out_specs=group_block,
         out_shape=jax.ShapeDtypeStruct((2, half * head_size, rows), jnp.bfloat16),
-        input_output_aliases={7: 0},
+        input_output_aliases={6: 0},
     )(
-        paired, paired, paired, near_bias, far_paired, far_paired, far_bias,
+        paired, paired, paired, limits, far_paired, far_paired,
         nearby,
     ).reshape(width, rows)
 

time: 128 us -> 128 us (level)
  waiting for transfers between devices: 32.3 us -> 33.7 us
    convert_element_type x2 -> x0, other arithmetic: 1.71 us -> none  [the longest x1 1.02 us: body(): far_bias = jnp.where(extra_row[None] & (far_position >= slide_length)[:,...]
    all_to_all x1, waiting for transfers between devices: 0.91 us -> 2.34 us  [body(): lax.all_to_all(jnp.broadcast_to(own_far[None], (seq_count,) + own_far.sha...]
    unnamed x16 -> x14, local copies, waits for them, and re-layouts: 6.15 us -> 6.14 us
  transfers between devices with their start and end apart: 3 -> 3, of which waited for: 3 -> 3; matrix products, arithmetic and copies ran while one was open for 19% -> 18% of each run, Pallas kernels for 20% -> 20%
where the time goes in v17:
time: 128 us; the launch traced here: 127 us
  Pallas kernels  37 us (29%)
  waiting for transfers between devices  33.7 us (26%)
  matrix products  22.2 us (17%)
  starting transfers between devices  16.1 us (13%)
  local copies, waits for them, and re-layouts  15.4 us (12%)
  other arithmetic  1.83 us (1%)
    all_to_all x1, waiting for transfers between devices, body(): lax.all_to_all(projected.reshape(device_count, block_rows, width), ('tile...  29.6 us
    pallas_call x1, Pallas kernels, body(): pl.pallas_call(functools.partial(nearby_kernel, groups=DILATION_RATE, gro...  25.7 us
    pallas_call x1, Pallas kernels, body(): pl.pallas_call(functools.partial(dilated_kernel, factor=factor), grid=(ha...  11.4 us
    dot_general x1, matrix products, body(): lax.dot_general(qkv_weight, normed, (((0,), (1,)), ((), ())), preferred_e...  8.48 us
    all_to_all x1, starting transfers between devices, body(): lax.all_to_all(slot.reshape(device_count, block_rows), ('tile', 'seq'), s...  7.3 us
    unnamed x14, local copies, waits for them, and re-layouts  6.14 us
    dot_general x1, matrix products, body(): jnp.dot(embeddings, in_weight, preferred_element_type=jnp.float32)  5.34 us
    all_to_all x1, starting transfers between devices, body(): lax.all_to_all(jnp.broadcast_to(own_far[None], (seq_count,) + own_far.sha...  4.65 us
  transfers between devices with their start and end apart: 3, of which 3 were waited for; matrix products, arithmetic and copies ran while one was open for 18% of the time, Pallas kernels for 20%

profile of v17, /device:TPU:0, one launch (start us, length us, event | category | flops | bytes accessed | tf_op | source)
XLA Modules:
  0.0 127.1 jit_solution(684965976891737270)
XLA Ops:
  0.0 0.0 copy-start
  0.0 1.5 %all_to_all.12 = s32[32,1,32]{2,1,0:T(1,128)} reshape(s32[1024]{0:T(1024)} %param.8) | data formatting | bytes 8192 | tf_op jit(solution)/shard_map/all_to_all | solution.py:156
  1.5 7.3 %all-to-all-start = ((s32[32,1,32]{2,1,0:T(1,128)}), s32[32,1,32]{2,1,0:T(1,128)S(1)}, u32[]{:S(2)}, u32[]{:S(2)}) async-start(s32[32,1,32]{2,1,0:T(1,128)} %all_to_all.12), calls=%async_computation | async-start | bytes 32768 | tf_op jit(solution)/shard_map/all_to_all | solution.py:156
  8.8 0.0 copy-done
  8.8 5.3 %convolution_convert_fusion.1 = bf16[1024,768]{1,0:T(8,128)(2,1)} fusion(bf16[1024,1536]{1,0:T(8,128)(2,1)S(1)} %copy-done, bf16[1536,768]{1,0:T(8,128)(2,1)} %param.10), kind=kOutput, calls=%fused_computation.15 | convolution fusion | flops 2416705536 | bytes 7077888 | tf_op jit(solution)/shard_map/dot_general | solution.py:146
  14.2 1.8 %all-to-all-done = s32[32,1,32]{2,1,0:T(1,128)S(1)} async-done(((s32[32,1,32]{2,1,0:T(1,128)}), s32[32,1,32]{2,1,0:T(1,128)S(1)}, u32[]{:S(2)}, u32[]{:S(2)}) %all-to-all-start) | async-done | bytes 4128 | tf_op jit(solution)/shard_map/all_to_all | solution.py:156
  16.0 4.2 %all-to-all-start.1 = ((bf16[32,32,768]{2,1,0:T(8,128)(2,1)}), bf16[32,32,768]{2,1,0:T(8,128)(2,1)}, u32[]{:S(2)}, u32[]{:S(2)}) async-start(bf16[32,32,768]{2,1,0:T(8,128)(2,1)} %bitcast.48), calls=%async_computation.1 | async-start | bytes 3145728 | tf_op jit(solution)/shard_map/all_to_all | solution.py:149
  20.1 3.2 %fusion.43 = (bf16[768,768]{1,0:T(8,128)(2,1)}, bf16[768,768]{1,0:T(8,128)(2,1)}) fusion(bf16[768,2304]{1,0:T(8,128)(2,1)} %param.12), kind=kLoop, calls=%fused_computation.57 | loop fusion | bytes 4718592 | tf_op jit(solution)/shard_map/slice | solution.py:187
  23.4 2.4 %copy.21 = bf16[768,768]{0,1:T(8,128)(2,1)} copy(bf16[768,768]{1,0:T(8,128)(2,1)} %get-tuple-element.5) | data formatting | bytes 2359296
  25.8 2.4 %copy.22 = bf16[768,768]{0,1:T(8,128)(2,1)} copy(bf16[768,768]{1,0:T(8,128)(2,1)} %get-tuple-element.6) | data formatting | bytes 2359296
  28.2 0.1 sub.34
  28.3 29.6 %all-to-all-done.1 = bf16[32,32,768]{2,1,0:T(8,128)(2,1)} async-done(((bf16[32,32,768]{2,1,0:T(8,128)(2,1)}), bf16[32,32,768]{2,1,0:T(8,128)(2,1)}, u32[]{:S(2)}, u32[]{:S(2)}) %all-to-all-start.1) | async-done | bytes 1572896 | tf_op jit(solution)/shard_map/all_to_all | solution.py:149
  57.9 3.4 %convert_reduce_fusion = (f32[1024]{0:T(1024)S(1)}, bf16[1024,768]{1,0:T(8,128)(2,1)S(1)}) fusion(bf16[1024,768]{1,0:T(8,128)(2,1)} %bitcast.2, s32[1024]{0:T(1024)S(1)} %fusion.36), kind=kOutput, calls=%fused_computation.3 | convolution fusion | flops 1614019584 | bytes 3153920 | tf_op jit(solution)/shard_map/dot_general | solution.py:164
  61.3 0.0 copy-start.1
  61.3 0.0 copy-start.5
  61.3 0.6 fusion.3
  62.0 0.1 copy-done.5
  62.0 0.5 fusion.5
  62.6 0.0 copy-done.1
  62.6 0.7 copy-done.4
  63.3 0.6 fusion.23
  64.0 0.6 copy-done.3
  64.6 0.6 fusion.20
  65.3 2.4 %broadcast_in_dim.11 = bf16[8,2,16,48,128]{4,3,2,1,0:T(8,128)(2,1)} broadcast(bf16[2,16,48,128]{3,2,1,0:T(8,128)(2,1)S(1)} %pad_maximum_fusion), dimensions={1,2,3,4} | broadcast | bytes 3538944 | tf_op jit(solution)/shard_map/broadcast_in_dim | solution.py:198
  67.6 4.6 %all-to-all-start.2 = ((bf16[8,2,16,48,128]{4,3,2,1,0:T(8,128)(2,1)}), bf16[8,2,16,48,128]{4,3,2,1,0:T(8,128)(2,1)}, u32[]{:S(2)}, u32[]{:S(2)}) async-start(bf16[8,2,16,48,128]{4,3,2,1,0:T(8,128)(2,1)} %broadcast_in_dim.11), calls=%async_computation.2 | async-start | bytes 6291456 | tf_op jit(solution)/shard_map/all_to_all | solution.py:197
  72.9 0.6 pad_add_fusion.limits_ref
  73.5 8.5 %convolution_convert_fusion = bf16[1024,2304]{0,1:T(8,128)(2,1)} fusion(bf16[1024,768]{1,0:T(8,128)(2,1)} %copy-done.2, bf16[768,2304]{1,0:T(8,128)(2,1)} %param.12), kind=kOutput, calls=%fused_computation | convolution fusion | flops 3626237952 | bytes 9830400 | tf_op jit(solution)/shard_map/dot_general | solution.py:175
  82.0 25.7 %shard_map.73.prev_ref = bf16[2,384,1024]{2,1,0:T(8,128)(2,1)} custom-call(bf16[2304,1024]{1,0:T(8,128)(2,1)} %bitcast.38, bf16[2304,1024]{1,0:T(8,128)(2,1)} %bitcast.39, bf16[2304,1024]{1,0:T(8,128)(2,1)} %bitcast.40, bf16[2304,1024]{1,0:T(8,128)(2,1)} %bitcast.41, bf16[2304,1024]{1,0:T(8,128)(2,1)} %bitcast.42, bf16[2304,1024]{1,0:T(8,128)(2,1)} %bitcast.43, ...), custom_call_target="tpu_custom_call" | custom-call | tf_op jit(solution)/shard_map/pallas_call | solution.py:207
  107.6 2.3 %all-to-all-done.2 = bf16[8,2,16,48,128]{4,3,2,1,0:T(8,128)(2,1)} async-done(((bf16[8,2,16,48,128]{4,3,2,1,0:T(8,128)(2,1)}), bf16[8,2,16,48,128]{4,3,2,1,0:T(8,128)(2,1)}, u32[]{:S(2)}, u32[]{:S(2)}) %all-to-all-start.2) | async-done | bytes 3145760 | tf_op jit(solution)/shard_map/all_to_all | solution.py:197
  110.0 11.4 %shard_map.74 = bf16[2,384,1024]{2,1,0:T(8,128)(2,1)} custom-call(bf16[6,384,1024]{2,1,0:T(8,128)(2,1)} %bitcast.44, bf16[6,384,1024]{2,1,0:T(8,128)(2,1)} %bitcast.45, bf16[6,384,1024]{2,1,0:T(8,128)(2,1)} %bitcast.46, s32[2]{0:T(128)} %pad_add_fusion.limits_ref, ...), custom_call_target="tpu_custom_call", output_to_operand_aliasing={{}: (6, {})} | custom-call | tf_op jit(solution)/shard_map/pallas_call | solution.py:228
  121.4 3.7 %fusion.7 = bf16[1024,768]{1,0:T(8,128)(2,1)S(1)} fusion(bf16[1024,768]{1,0:T(8,128)(2,1)} %copy-done.1, bf16[768,1024]{1,0:T(8,128)(2,1)} %bitcast.47, bf16[768,768]{1,0:T(8,128)(2,1)} %param.13, pred[1024]{0:T(1024)(128)(4,1)S(1)} %fusion.34), kind=kOutput, calls=%fused_computation.12 | convolution fusion | flops 1211105280 | bytes 5899264 | tf_op jit(solution)/shard_map/dot_general | solution.py:248
  125.1 2.0 %copy.36 = bf16[128,8,768]{2,1,0:T(8,128)(2,1)} copy(bf16[128,8,768]{2,0,1:T(8,128)(2,1)S(1)} %bitcast.51) | data formatting | bytes 3145728 | tf_op jit(solution)/shard_map/transpose | solution.py:252
  (12 shorter events, 0.2 us)
Async XLA Ops:
  0.0 8.8 %copy-start = (bf16[1024,1536]{1,0:T(8,128)(2,1)S(1)}, bf16[1024,1536]{1,0:T(8,128)(2,1)}, u32[]{:S(2)}) copy-start(bf16[1024,1536]{1,0:T(8,128)(2,1)} %param.7) | copy-start | bytes 9437188
  1.5 14.5 %all-to-all-start = ((s32[32,1,32]{2,1,0:T(1,128)}), s32[32,1,32]{2,1,0:T(1,128)S(1)}, u32[]{:S(2)}, u32[]{:S(2)}) async-start(s32[32,1,32]{2,1,0:T(1,128)} %all_to_all.12), calls=%async_computation | async-start | bytes 32768 | tf_op jit(solution)/shard_map/all_to_all | solution.py:156
  16.0 41.9 %all-to-all-start.1 = ((bf16[32,32,768]{2,1,0:T(8,128)(2,1)}), bf16[32,32,768]{2,1,0:T(8,128)(2,1)}, u32[]{:S(2)}, u32[]{:S(2)}) async-start(bf16[32,32,768]{2,1,0:T(8,128)(2,1)} %bitcast.48), calls=%async_computation.1 | async-start | bytes 3145728 | tf_op jit(solution)/shard_map/all_to_all | solution.py:149
  61.3 1.3 copy-start.1
  61.3 0.7 copy-start.5
  62.0 1.3 copy-start.4
  62.6 1.4 %copy-start.2 = (bf16[1024,768]{1,0:T(8,128)(2,1)}, bf16[1024,768]{1,0:T(8,128)(2,1)S(1)}, u32[]{:S(2)}) copy-start(bf16[1024,768]{1,0:T(8,128)(2,1)S(1)} %fusion.5) | copy-start | bytes 4718596
  63.3 1.3 copy-start.3
  67.6 42.4 %all-to-all-start.2 = ((bf16[8,2,16,48,128]{4,3,2,1,0:T(8,128)(2,1)}), bf16[8,2,16,48,128]{4,3,2,1,0:T(8,128)(2,1)}, u32[]{:S(2)}, u32[]{:S(2)}) async-start(bf16[8,2,16,48,128]{4,3,2,1,0:T(8,128)(2,1)} %broadcast_in_dim.11), calls=%async_computation.2 | async-start | bytes 6291456 | tf_op jit(solution)/shard_map/all_to_all | solution.py:197

commit v18 on v16

--- a/solution.py
+++ b/solution.py
@@ -78,14 +78,15 @@
             o_ref[pair, :, rows] = (summed_t / total).astype(o_ref.dtype)
 
 
-def joined(ref, pair):
-    return jnp.concatenate([ref[chunk, 0, pair, 0] for chunk in range(ref.shape[0])], axis=1)
+def joined(refs, pair):
+    return jnp.concatenate([ref[0, pair, 0] for ref in refs], axis=1)
 
 
 def dilated_kernel(
-    qt_ref, kt_ref, vt_ref, bias_ref, fk_ref, fv_ref, fbias_ref, prev_ref, o_ref, *, factor
+    qt_ref, kt_ref, vt_ref, bias_ref, *refs, factor, chunks
 ):
-    del prev_ref
+    fk_ref, fv_ref = refs[:chunks], refs[chunks : 2 * chunks]
+    fbias_ref, _, o_ref = refs[2 * chunks :]
     for pair in range(2):
         queries_t = extend(qt_ref[pair], ones_row(qt_ref.shape[2]))
         near_keys = extend(kt_ref[pair], bias_ref[...]).T
@@ -173,15 +174,14 @@
             for part in (1, 2)
         ]
     )
-    far = lax.all_to_all(
-        jnp.broadcast_to(own_far[None], (seq_count,) + own_far.shape),
-        "seq",
-        split_axis=0,
-        concat_axis=0,
-        tiled=True,
-    )
+    far_chunks = [own_far] + [
+        lax.ppermute(own_far, "seq", [(j, (j + k) % seq_count) for j in range(seq_count)])
+        for k in range(1, seq_count)
+    ]
+    source = (lax.axis_index("seq") - jnp.arange(seq_count, dtype=jnp.int32)) % seq_count
     far_position = (
-        jnp.arange(far_count, dtype=jnp.int32)[None, :] * DILATION_RATE
+        (source[:, None] * group_rows + jnp.arange(group_rows, dtype=jnp.int32)[None, :]).reshape(1, far_count)
+        * DILATION_RATE
         + jnp.asarray(offsets, jnp.int32)[:, None]
     )
     far_bias = jnp.where(
@@ -210,29 +210,31 @@
     )(*([projected_t] * 6), near_bias)
 
     paired = projected_t.reshape(6, half * head_size, rows)
-    far_paired = far.reshape(seq_count, 2, 2, half, head_size, group_rows)
+    far_paired = [chunk.reshape(2, 2, half, head_size, group_rows) for chunk in far_chunks]
     group_block = pl.BlockSpec(
         (2, head_size, group_rows), lambda i: (0, i, i % DILATION_RATE)
     )
-    far_block = (seq_count, 1, 2, 1, head_size, group_rows)
+    far_block = (1, 2, 1, head_size, group_rows)
     attended_t = pl.pallas_call(
-        functools.partial(dilated_kernel, factor=factor),
+        functools.partial(dilated_kernel, factor=factor, chunks=seq_count),
         grid=(half,),
         in_specs=[
             pl.BlockSpec((2, head_size, group_rows), lambda i: (0, i, i % DILATION_RATE)),
             pl.BlockSpec((2, head_size, rows), lambda i: (1, i, 0)),
             pl.BlockSpec((2, head_size, rows), lambda i: (2, i, 0)),
             bias_block,
-            pl.BlockSpec(far_block, lambda i: (0, 0, 0, i, 0, 0)),
-            pl.BlockSpec(far_block, lambda i: (0, 1, 0, i, 0, 0)),
+        ]
+        + [pl.BlockSpec(far_block, lambda i: (0, 0, i, 0, 0))] * seq_count
+        + [pl.BlockSpec(far_block, lambda i: (1, 0, i, 0, 0))] * seq_count
+        + [
             pl.BlockSpec((1, 16, far_count), lambda i: (i, 0, 0)),
             pl.BlockSpec(memory_space=pl.ANY),
         ],
         out_specs=group_block,
         out_shape=jax.ShapeDtypeStruct((2, half * head_size, rows), jnp.bfloat16),
-        input_output_aliases={7: 0},
+        input_output_aliases={5 + 2 * seq_count: 0},
     )(
-        paired, paired, paired, near_bias, far_paired, far_paired, far_bias,
+        paired, paired, paired, near_bias, *far_paired, *far_paired, far_bias,
         nearby,
     ).reshape(width, rows)
 

time: 128 us -> 138 us (1.078); the launches traced: 127 us -> 136 us
  waiting for transfers between devices: 32.3 us -> 44.2 us
  matrix products: 22.2 us -> 19.3 us
  local copies, waits for them, and re-layouts: 15.4 us -> 13 us
  other arithmetic: 3.09 us -> 4.7 us
    ppermute x0 -> x7, waiting for transfers between devices: none -> 14.3 us  [body(): lax.ppermute(own_far, 'seq', [(j, (j + k) % seq_count) for j in range(seq...]
    all_to_all x1 -> x0, starting transfers between devices: 4.79 us -> none  [body(): lax.all_to_all(jnp.broadcast_to(own_far[None], (seq_count,) + own_far.sha...]
    ppermute x0 -> x7, starting transfers between devices: none -> 4.2 us  [body(): lax.ppermute(own_far, 'seq', [(j, (j + k) % seq_count) for j in range(seq...]
    dot_general x1, matrix products: 8.48 us -> 5.55 us  [body(): lax.dot_general(qkv_weight, normed, (((0,), (1,)), ((), ())), preferred_e...]
    broadcast_in_dim x1 -> x0, local copies, waits for them, and re-layouts: 2.37 us -> none  [body(): jnp.broadcast_to(own_far[None], (seq_count,) + own_far.shape)]
    another operation x1 -> x2, other arithmetic: 0.04 us -> 1.59 us  [body(): jnp.stack([jnp.einsum('ljc,chld->hldj', grouped, qkv_weight[:, part * wid...]
    all_to_all x1, waiting for transfers between devices: 29.6 us -> 28.2 us  [body(): lax.all_to_all(projected.reshape(device_count, block_rows, width), ('tile...]
    unnamed x16 -> x28, local copies, waits for them, and re-layouts: 6.15 us -> 6.19 us
  transfers between devices with their start and end apart: 3 -> 9, of which waited for: 3 -> 4; matrix products, arithmetic and copies ran while one was open for 19% -> 16% of each run, Pallas kernels for 20% -> 19%
where the time goes in v18:
time: 138 us; the launch traced here: 136 us
  waiting for transfers between devices  44.2 us (32%)
  Pallas kernels  37.9 us (27%)
  matrix products  19.3 us (14%)
  starting transfers between devices  15.7 us (11%)
  local copies, waits for them, and re-layouts  13 us (9%)
  other arithmetic  4.7 us (3%)
    all_to_all x1, waiting for transfers between devices, body(): lax.all_to_all(projected.reshape(device_count, block_rows, width), ('tile...  28.2 us
    pallas_call x1, Pallas kernels, body(): pl.pallas_call(functools.partial(nearby_kernel, groups=DILATION_RATE, gro...  25.9 us
    ppermute x7, waiting for transfers between devices, body(): lax.ppermute(own_far, 'seq', [(j, (j + k) % seq_count) for j in range(seq...  14.3 us
    pallas_call x1, Pallas kernels, body(): pl.pallas_call(functools.partial(dilated_kernel, factor=factor, chunks=se...  12 us
    all_to_all x1, starting transfers between devices, body(): lax.all_to_all(slot.reshape(device_count, block_rows), ('tile', 'seq'), s...  7.3 us
    unnamed x28, local copies, waits for them, and re-layouts  6.19 us
    dot_general x1, matrix products, body(): lax.dot_general(qkv_weight, normed, (((0,), (1,)), ((), ())), preferred_e...  5.55 us
    dot_general x1, matrix products, body(): jnp.dot(embeddings, in_weight, preferred_element_type=jnp.float32)  5.34 us
  transfers between devices with their start and end apart: 9, of which 4 were waited for; matrix products, arithmetic and copies ran while one was open for 16% of the time, Pallas kernels for 19%

profile of v18, /device:TPU:0, one launch (start us, length us, event | category | flops | bytes accessed | tf_op | source)
XLA Modules:
  0.0 135.6 jit_solution(7836234104843870017)
XLA Ops:
  0.0 1.5 %all_to_all.9 = s32[32,1,32]{2,1,0:T(1,128)} reshape(s32[1024]{0:T(1024)} %param.9) | data formatting | bytes 8192 | tf_op jit(solution)/shard_map/all_to_all | solution.py:133
  1.5 7.3 %all-to-all-start = ((s32[32,1,32]{2,1,0:T(1,128)}), s32[32,1,32]{2,1,0:T(1,128)S(1)}, u32[]{:S(2)}, u32[]{:S(2)}) async-start(s32[32,1,32]{2,1,0:T(1,128)} %all_to_all.9), calls=%async_computation | async-start | bytes 32768 | tf_op jit(solution)/shard_map/all_to_all | solution.py:133
  8.8 5.3 %convolution_convert_fusion.1 = bf16[1024,768]{1,0:T(8,128)(2,1)} fusion(bf16[1024,1536]{1,0:T(8,128)(2,1)S(1)} %copy-done, bf16[1536,768]{1,0:T(8,128)(2,1)} %param.11), kind=kOutput, calls=%fused_computation.15 | convolution fusion | flops 2416705536 | bytes 7077888 | tf_op jit(solution)/shard_map/dot_general | solution.py:123
  14.2 1.8 %all-to-all-done = s32[32,1,32]{2,1,0:T(1,128)S(1)} async-done(((s32[32,1,32]{2,1,0:T(1,128)}), s32[32,1,32]{2,1,0:T(1,128)S(1)}, u32[]{:S(2)}, u32[]{:S(2)}) %all-to-all-start) | async-done | bytes 4128 | tf_op jit(solution)/shard_map/all_to_all | solution.py:133
  16.0 4.2 %all-to-all-start.1 = ((bf16[32,32,768]{2,1,0:T(8,128)(2,1)}), bf16[32,32,768]{2,1,0:T(8,128)(2,1)}, u32[]{:S(2)}, u32[]{:S(2)}) async-start(bf16[32,32,768]{2,1,0:T(8,128)(2,1)} %bitcast.61), calls=%async_computation.1 | async-start | bytes 3145728 | tf_op jit(solution)/shard_map/all_to_all | solution.py:126
  20.8 3.2 %fusion.30 = (bf16[768,768]{1,0:T(8,128)(2,1)}, bf16[768,768]{1,0:T(8,128)(2,1)}) fusion(bf16[768,2304]{1,0:T(8,128)(2,1)} %param.13), kind=kLoop, calls=%fused_computation.62 | loop fusion | bytes 4718592 | tf_op jit(solution)/shard_map/slice | solution.py:167
  24.0 2.4 %copy.27 = bf16[768,768]{0,1:T(8,128)(2,1)} copy(bf16[768,768]{1,0:T(8,128)(2,1)} %get-tuple-element.5) | data formatting | bytes 2359296
  26.4 2.4 %copy.28 = bf16[768,768]{0,1:T(8,128)(2,1)} copy(bf16[768,768]{1,0:T(8,128)(2,1)} %get-tuple-element.6) | data formatting | bytes 2359296
  28.9 0.7 select_convert_fusion.1.bias_ref
  29.7 28.2 %all-to-all-done.1 = bf16[32,32,768]{2,1,0:T(8,128)(2,1)} async-done(((bf16[32,32,768]{2,1,0:T(8,128)(2,1)}), bf16[32,32,768]{2,1,0:T(8,128)(2,1)}, u32[]{:S(2)}, u32[]{:S(2)}) %all-to-all-start.1) | async-done | bytes 1572896 | tf_op jit(solution)/shard_map/all_to_all | solution.py:126
  57.9 3.4 %convert_reduce_fusion = (f32[1024]{0:T(1024)S(1)}, bf16[1024,768]{1,0:T(8,128)(2,1)S(1)}) fusion(bf16[1024,768]{1,0:T(8,128)(2,1)} %bitcast.2, s32[1024]{0:T(1024)S(1)} %fusion.20), kind=kOutput, calls=%fused_computation.3 | convolution fusion | flops 1614019584 | bytes 3153920 | tf_op jit(solution)/shard_map/dot_general | solution.py:141
  61.3 0.6 fusion.3
  62.0 0.5 fusion.5
  62.6 0.7 copy-done.5
  63.3 0.6 convolution_convert_fusion.3
  63.9 0.6 copy-done.6
  64.6 0.6 convolution_convert_fusion.2
  65.2 0.8 pad_maximum_fusion.1
  66.0 1.4 %collective-permute-start.6 = (bf16[2,16,48,128]{3,2,1,0:T(8,128)(2,1)}, bf16[2,16,48,128]{3,2,1,0:T(8,128)(2,1)S(1)}, u32[]{:S(2)}, u32[]{:S(2)}) collective-permute-start(bf16[2,16,48,128]{3,2,1,0:T(8,128)(2,1)} %pad_maximum_fusion.1), channel_id=1, source_target_pairs={{0,7},{1,0},{2,1},{3,2},{4,3},{5,4},{6,5},{7,6},{8,15},{9,8},{10,9... | collective-permute-start | bytes 1179656 | tf_op jit(solution)/shard_map/ppermute | solution.py:178
  67.4 0.8 collective-permute-start.5
  68.3 1.0 select_convert_fusion.refs_16_
  69.3 0.3 collective-permute-start.4
  69.6 1.5 %collective-permute-start.3 = (bf16[2,16,48,128]{3,2,1,0:T(8,128)(2,1)}, bf16[2,16,48,128]{3,2,1,0:T(8,128)(2,1)}, u32[]{:S(2)}, u32[]{:S(2)}) collective-permute-start(bf16[2,16,48,128]{3,2,1,0:T(8,128)(2,1)} %pad_maximum_fusion.1), channel_id=1, source_target_pairs={{0,4},{1,5},{2,6},{3,7},{4,0},{5,1},{6,2},{7,3},{8,12},{9,13},{10,... | collective-permute-start | bytes 1179656 | tf_op jit(solution)/shard_map/ppermute | solution.py:178
  71.2 0.2 collective-permute-start.2
  71.3 5.7 %collective-permute-done.6 = bf16[2,16,48,128]{3,2,1,0:T(8,128)(2,1)S(1)} collective-permute-done((bf16[2,16,48,128]{3,2,1,0:T(8,128)(2,1)}, bf16[2,16,48,128]{3,2,1,0:T(8,128)(2,1)S(1)}, u32[]{:S(2)}, u32[]{:S(2)}) %collective-permute-start.6) | collective-permute-done | bytes 393248 | tf_op jit(solution)/shard_map/ppermute | solution.py:178
  77.0 8.6 %collective-permute-done.5 = bf16[2,16,48,128]{3,2,1,0:T(8,128)(2,1)S(1)} collective-permute-done((bf16[2,16,48,128]{3,2,1,0:T(8,128)(2,1)}, bf16[2,16,48,128]{3,2,1,0:T(8,128)(2,1)S(1)}, u32[]{:S(2)}, u32[]{:S(2)}) %collective-permute-start.5) | collective-permute-done | bytes 393248 | tf_op jit(solution)/shard_map/ppermute | solution.py:178
  85.6 5.5 %convolution_convert_fusion = bf16[1024,2304]{0,1:T(8,128)(2,1)} fusion(bf16[1024,768]{1,0:T(8,128)(2,1)S(1)} %fusion.5, bf16[768,2304]{1,0:T(8,128)(2,1)S(1)} %copy-done.2), kind=kOutput, calls=%fused_computation | convolution fusion | flops 3626237952 | bytes 9830400 | tf_op jit(solution)/shard_map/dot_general | solution.py:155
  91.2 25.9 %shard_map.82.refs_17_ = bf16[2,384,1024]{2,1,0:T(8,128)(2,1)} custom-call(bf16[2304,1024]{1,0:T(8,128)(2,1)} %bitcast.51, bf16[2304,1024]{1,0:T(8,128)(2,1)} %bitcast.52, bf16[2304,1024]{1,0:T(8,128)(2,1)} %bitcast.53, bf16[2304,1024]{1,0:T(8,128)(2,1)} %bitcast.54, bf16[2304,1024]{1,0:T(8,128)(2,1)} %bitcast.55, bf16[2304,1024]{1,0:T(8,128)(2,1)} %bitcast.56, ...), custom_call_target="tpu_custom_call" | custom-call | tf_op jit(solution)/shard_map/pallas_call | solution.py:197
  117.0 0.8 pad_maximum_fusion.refs_0_.refs_8_
  117.9 12.0 %shard_map.83 = bf16[2,384,1024]{2,1,0:T(8,128)(2,1)} custom-call(bf16[6,384,1024]{2,1,0:T(8,128)(2,1)} %bitcast.57, bf16[6,384,1024]{2,1,0:T(8,128)(2,1)} %bitcast.58, bf16[6,384,1024]{2,1,0:T(8,128)(2,1)} %bitcast.59, bf16[16,1024]{1,0:T(8,128)(2,1)} %select_convert_fusion.1.bias_ref, ...), custom_call_target="tpu_custom_call", output_to_operand_aliasing={{}: (21, {})} | custom-call | tf_op jit(solution)/shard_map/pallas_call | solution.py:218
  129.9 3.7 %fusion.7 = bf16[1024,768]{1,0:T(8,128)(2,1)S(1)} fusion(bf16[1024,768]{1,0:T(8,128)(2,1)} %copy-done.1, bf16[768,1024]{1,0:T(8,128)(2,1)} %bitcast.60, bf16[768,768]{1,0:T(8,128)(2,1)} %param.14, pred[1024]{0:T(1024)(128)(4,1)S(1)} %fusion.18), kind=kOutput, calls=%fused_computation.12 | convolution fusion | flops 1211105280 | bytes 5899264 | tf_op jit(solution)/shard_map/dot_general | solution.py:241
  133.6 2.0 %copy.30 = bf16[128,8,768]{2,1,0:T(8,128)(2,1)} copy(bf16[128,8,768]{2,0,1:T(8,128)(2,1)S(1)} %bitcast.64) | data formatting | bytes 3145728 | tf_op jit(solution)/shard_map/transpose | solution.py:245
  (42 shorter events, 0.5 us)
Async XLA Ops:
  0.0 8.8 %copy-start = (bf16[1024,1536]{1,0:T(8,128)(2,1)S(1)}, bf16[1024,1536]{1,0:T(8,128)(2,1)}, u32[]{:S(2)}) copy-start(bf16[1024,1536]{1,0:T(8,128)(2,1)} %param.8) | copy-start | bytes 9437188
  1.5 14.5 %all-to-all-start = ((s32[32,1,32]{2,1,0:T(1,128)}), s32[32,1,32]{2,1,0:T(1,128)S(1)}, u32[]{:S(2)}, u32[]{:S(2)}) async-start(s32[32,1,32]{2,1,0:T(1,128)} %all_to_all.9), calls=%async_computation | async-start | bytes 32768 | tf_op jit(solution)/shard_map/all_to_all | solution.py:133
  16.0 41.9 %all-to-all-start.1 = ((bf16[32,32,768]{2,1,0:T(8,128)(2,1)}), bf16[32,32,768]{2,1,0:T(8,128)(2,1)}, u32[]{:S(2)}, u32[]{:S(2)}) async-start(bf16[32,32,768]{2,1,0:T(8,128)(2,1)} %bitcast.61), calls=%async_computation.1 | async-start | bytes 3145728 | tf_op jit(solution)/shard_map/all_to_all | solution.py:126
  61.3 1.3 copy-start.1
  61.3 0.7 copy-start.11
  62.0 1.3 copy-start.5
  63.3 1.3 copy-start.6
  63.9 1.3 copy-start.7
  64.6 3.6 %copy-start.12 = (s32[16]{0:T(128)S(1)}, s32[16]{0:T(128)}, u32[]{:S(2)}) copy-start(s32[16]{0:T(128)} %constant.90.clone) | copy-start | bytes 196
  64.6 21.0 %copy-start.2 = (bf16[768,2304]{1,0:T(8,128)(2,1)S(1)}, bf16[768,2304]{1,0:T(8,128)(2,1)}, u32[]{:S(2)}) copy-start(bf16[768,2304]{1,0:T(8,128)(2,1)} %param.13) | copy-start | bytes 10616836
  65.2 20.4 %copy-start.9 = (bf16[8,128,2,48]{1,3,0,2:T(8,128)(2,1)}, bf16[8,128,2,48]{1,3,0,2:T(8,128)(2,1)S(1)}, u32[]{:S(2)}) copy-start(bf16[8,128,2,48]{1,3,0,2:T(8,128)(2,1)S(1)} %convolution_convert_fusion.2) | copy-start | bytes 589828
  66.0 11.0 %collective-permute-start.6 = (bf16[2,16,48,128]{3,2,1,0:T(8,128)(2,1)}, bf16[2,16,48,128]{3,2,1,0:T(8,128)(2,1)S(1)}, u32[]{:S(2)}, u32[]{:S(2)}) collective-permute-start(bf16[2,16,48,128]{3,2,1,0:T(8,128)(2,1)} %pad_maximum_fusion.1), channel_id=1, source_target_pairs={{0,7},{1,0},{2,1},{3,2},{4,3},{5,4},{6,5},{7,6},{8,15},{9,8},{10,9... | collective-permute-start | bytes 1179656 | tf_op jit(solution)/shard_map/ppermute | solution.py:178
  67.4 18.2 %collective-permute-start.5 = (bf16[2,16,48,128]{3,2,1,0:T(8,128)(2,1)}, bf16[2,16,48,128]{3,2,1,0:T(8,128)(2,1)S(1)}, u32[]{:S(2)}, u32[]{:S(2)}) collective-permute-start(bf16[2,16,48,128]{3,2,1,0:T(8,128)(2,1)} %pad_maximum_fusion.1), channel_id=1, source_target_pairs={{0,6},{1,7},{2,0},{3,1},{4,2},{5,3},{6,4},{7,5},{8,14},{9,15},{10,... | collective-permute-start | bytes 1179656 | tf_op jit(solution)/shard_map/ppermute | solution.py:178
  69.3 48.5 %collective-permute-start.4 = (bf16[2,16,48,128]{3,2,1,0:T(8,128)(2,1)}, bf16[2,16,48,128]{3,2,1,0:T(8,128)(2,1)}, u32[]{:S(2)}, u32[]{:S(2)}) collective-permute-start(bf16[2,16,48,128]{3,2,1,0:T(8,128)(2,1)} %pad_maximum_fusion.1), channel_id=1, source_target_pairs={{0,5},{1,6},{2,7},{3,0},{4,1},{5,2},{6,3},{7,4},{8,13},{9,14},{10,... | collective-permute-start | bytes 1179656 | tf_op jit(solution)/shard_map/ppermute | solution.py:178
  69.6 48.2 %collective-permute-start.3 = (bf16[2,16,48,128]{3,2,1,0:T(8,128)(2,1)}, bf16[2,16,48,128]{3,2,1,0:T(8,128)(2,1)}, u32[]{:S(2)}, u32[]{:S(2)}) collective-permute-start(bf16[2,16,48,128]{3,2,1,0:T(8,128)(2,1)} %pad_maximum_fusion.1), channel_id=1, source_target_pairs={{0,4},{1,5},{2,6},{3,7},{4,0},{5,1},{6,2},{7,3},{8,12},{9,13},{10,... | collective-permute-start | bytes 1179656 | tf_op jit(solution)/shard_map/ppermute | solution.py:178
  71.2 46.7 %collective-permute-start.2 = (bf16[2,16,48,128]{3,2,1,0:T(8,128)(2,1)}, bf16[2,16,48,128]{3,2,1,0:T(8,128)(2,1)}, u32[]{:S(2)}, u32[]{:S(2)}) collective-permute-start(bf16[2,16,48,128]{3,2,1,0:T(8,128)(2,1)} %pad_maximum_fusion.1), channel_id=1, source_target_pairs={{0,3},{1,4},{2,5},{3,6},{4,7},{5,0},{6,1},{7,2},{8,11},{9,12},{10,... | collective-permute-start | bytes 1179656 | tf_op jit(solution)/shard_map/ppermute | solution.py:178
  77.0 14.2 %copy-start.3 = (bf16[2,16,48,128]{3,2,1,0:T(8,128)(2,1)}, bf16[2,16,48,128]{3,2,1,0:T(8,128)(2,1)S(1)}, u32[]{:S(2)}) copy-start(bf16[2,16,48,128]{3,2,1,0:T(8,128)(2,1)S(1)} %collective-permute-done.6) | copy-start | bytes 1179652
  77.0 40.8 %collective-permute-start.1 = (bf16[2,16,48,128]{3,2,1,0:T(8,128)(2,1)}, bf16[2,16,48,128]{3,2,1,0:T(8,128)(2,1)}, u32[]{:S(2)}, u32[]{:S(2)}) collective-permute-start(bf16[2,16,48,128]{3,2,1,0:T(8,128)(2,1)} %pad_maximum_fusion.1), channel_id=1, source_target_pairs={{0,2},{1,3},{2,4},{3,5},{4,6},{5,7},{6,0},{7,1},{8,10},{9,11},{10,... | collective-permute-start | bytes 1179656 | tf_op jit(solution)/shard_map/ppermute | solution.py:178
  85.6 5.6 %copy-start.4 = (bf16[2,16,48,128]{3,2,1,0:T(8,128)(2,1)}, bf16[2,16,48,128]{3,2,1,0:T(8,128)(2,1)S(1)}, u32[]{:S(2)}) copy-start(bf16[2,16,48,128]{3,2,1,0:T(8,128)(2,1)S(1)} %collective-permute-done.5) | copy-start | bytes 1179652
  85.6 32.3 %collective-permute-start = (bf16[2,16,48,128]{3,2,1,0:T(8,128)(2,1)}, bf16[2,16,48,128]{3,2,1,0:T(8,128)(2,1)}, u32[]{:S(2)}, u32[]{:S(2)}) collective-permute-start(bf16[2,16,48,128]{3,2,1,0:T(8,128)(2,1)} %pad_maximum_fusion.1), channel_id=1, source_target_pairs={{0,1},{1,2},{2,3},{3,4},{4,5},{5,6},{6,7},{7,0},{8,9},{9,10},{10,1... | collective-permute-start | bytes 1179656 | tf_op jit(solution)/shard_map/ppermute | solution.py:178
  91.2 25.9 %copy-start.8 = (bf16[8,128,2,48]{1,3,0,2:T(8,128)(2,1)S(1)}, bf16[8,128,2,48]{1,3,0,2:T(8,128)(2,1)}, u32[]{:S(2)}) copy-start(bf16[8,128,2,48]{1,3,0,2:T(8,128)(2,1)} %copy-done.7) | copy-start | bytes 589828
  91.2 25.9 %copy-start.10 = (bf16[8,128,2,48]{1,3,0,2:T(8,128)(2,1)S(1)}, bf16[8,128,2,48]{1,3,0,2:T(8,128)(2,1)}, u32[]{:S(2)}) copy-start(bf16[8,128,2,48]{1,3,0,2:T(8,128)(2,1)} %copy-done.9) | copy-start | bytes 589828

commit v19 on v17

--- a/solution.py
+++ b/solution.py
@@ -9,7 +9,7 @@
 
 HEAD_COUNT = 16
 QUERY_BLOCK = 1024
-PASS1 = 512
+PASS1 = 1024
 PASS2 = 512
 DILATION_RATE = 8
 

time: 128 us -> 128 us (level)
  Pallas kernels: 37 us -> 39.8 us
  waiting for transfers between devices: 33.7 us -> 31.4 us
    pallas_call x1, Pallas kernels: 25.7 us -> 28.4 us  [body(): pl.pallas_call(functools.partial(nearby_kernel, groups=DILATION_RATE, gro...]
    all_to_all x1, waiting for transfers between devices: 2.34 us -> 0.01 us  [body(): lax.all_to_all(jnp.broadcast_to(own_far[None], (seq_count,) + own_far.sha...]
  transfers between devices with their start and end apart: 3 -> 3, of which waited for: 3 -> 2; matrix products, arithmetic and copies ran while one was open for 18% -> 18% of each run, Pallas kernels for 20% -> 22%
where the time goes in v19:
time: 128 us
  Pallas kernels  39.8 us (31%)
  waiting for transfers between devices  31.4 us (25%)
  matrix products  22.2 us (17%)
  starting transfers between devices  16.1 us (13%)
  local copies, waits for them, and re-layouts  15.4 us (12%)
  other arithmetic  1.83 us (1%)
    all_to_all x1, waiting for transfers between devices, body(): lax.all_to_all(projected.reshape(device_count, block_rows, width), ('tile...  29.6 us
    pallas_call x1, Pallas kernels, body(): pl.pallas_call(functools.partial(nearby_kernel, groups=DILATION_RATE, gro...  28.4 us
    pallas_call x1, Pallas kernels, body(): pl.pallas_call(functools.partial(dilated_kernel, factor=factor), grid=(ha...  11.4 us
    dot_general x1, matrix products, body(): lax.dot_general(qkv_weight, normed, (((0,), (1,)), ((), ())), preferred_e...  8.48 us
    all_to_all x1, starting transfers between devices, body(): lax.all_to_all(slot.reshape(device_count, block_rows), ('tile', 'seq'), s...  7.3 us
    unnamed x14, local copies, waits for them, and re-layouts  6.14 us
    dot_general x1, matrix products, body(): jnp.dot(embeddings, in_weight, preferred_element_type=jnp.float32)  5.34 us
    all_to_all x1, starting transfers between devices, body(): lax.all_to_all(jnp.broadcast_to(own_far[None], (seq_count,) + own_far.sha...  4.65 us
  transfers between devices with their start and end apart: 3, of which 2 were waited for; matrix products, arithmetic and copies ran while one was open for 18% of the time, Pallas kernels for 22%

profile of v19, /device:TPU:0, one launch (start us, length us, event | category | flops | bytes accessed | tf_op | source)
XLA Modules:
  0.0 127.5 jit_solution(12871800561002963617)
XLA Ops:
  0.0 0.0 copy-start
  0.0 1.5 %all_to_all.12 = s32[32,1,32]{2,1,0:T(1,128)} reshape(s32[1024]{0:T(1024)} %param.8) | data formatting | bytes 8192 | tf_op jit(solution)/shard_map/all_to_all | solution.py:156
  1.5 7.3 %all-to-all-start = ((s32[32,1,32]{2,1,0:T(1,128)}), s32[32,1,32]{2,1,0:T(1,128)S(1)}, u32[]{:S(2)}, u32[]{:S(2)}) async-start(s32[32,1,32]{2,1,0:T(1,128)} %all_to_all.12), calls=%async_computation | async-start | bytes 32768 | tf_op jit(solution)/shard_map/all_to_all | solution.py:156
  8.8 0.0 copy-done
  8.8 5.3 %convolution_convert_fusion.1 = bf16[1024,768]{1,0:T(8,128)(2,1)} fusion(bf16[1024,1536]{1,0:T(8,128)(2,1)S(1)} %copy-done, bf16[1536,768]{1,0:T(8,128)(2,1)} %param.10), kind=kOutput, calls=%fused_computation.15 | convolution fusion | flops 2416705536 | bytes 7077888 | tf_op jit(solution)/shard_map/dot_general | solution.py:146
  14.2 1.8 %all-to-all-done = s32[32,1,32]{2,1,0:T(1,128)S(1)} async-done(((s32[32,1,32]{2,1,0:T(1,128)}), s32[32,1,32]{2,1,0:T(1,128)S(1)}, u32[]{:S(2)}, u32[]{:S(2)}) %all-to-all-start) | async-done | bytes 4128 | tf_op jit(solution)/shard_map/all_to_all | solution.py:156
  16.0 4.2 %all-to-all-start.1 = ((bf16[32,32,768]{2,1,0:T(8,128)(2,1)}), bf16[32,32,768]{2,1,0:T(8,128)(2,1)}, u32[]{:S(2)}, u32[]{:S(2)}) async-start(bf16[32,32,768]{2,1,0:T(8,128)(2,1)} %bitcast.48), calls=%async_computation.1 | async-start | bytes 3145728 | tf_op jit(solution)/shard_map/all_to_all | solution.py:149
  20.1 3.2 %fusion.43 = (bf16[768,768]{1,0:T(8,128)(2,1)}, bf16[768,768]{1,0:T(8,128)(2,1)}) fusion(bf16[768,2304]{1,0:T(8,128)(2,1)} %param.12), kind=kLoop, calls=%fused_computation.57 | loop fusion | bytes 4718592 | tf_op jit(solution)/shard_map/slice | solution.py:187
  23.4 2.4 %copy.21 = bf16[768,768]{0,1:T(8,128)(2,1)} copy(bf16[768,768]{1,0:T(8,128)(2,1)} %get-tuple-element.5) | data formatting | bytes 2359296
  25.8 2.4 %copy.22 = bf16[768,768]{0,1:T(8,128)(2,1)} copy(bf16[768,768]{1,0:T(8,128)(2,1)} %get-tuple-element.6) | data formatting | bytes 2359296
  28.2 0.1 sub.34
  28.3 29.6 %all-to-all-done.1 = bf16[32,32,768]{2,1,0:T(8,128)(2,1)} async-done(((bf16[32,32,768]{2,1,0:T(8,128)(2,1)}), bf16[32,32,768]{2,1,0:T(8,128)(2,1)}, u32[]{:S(2)}, u32[]{:S(2)}) %all-to-all-start.1) | async-done | bytes 1572896 | tf_op jit(solution)/shard_map/all_to_all | solution.py:149
  57.9 3.4 %convert_reduce_fusion = (f32[1024]{0:T(1024)S(1)}, bf16[1024,768]{1,0:T(8,128)(2,1)S(1)}) fusion(bf16[1024,768]{1,0:T(8,128)(2,1)} %bitcast.2, s32[1024]{0:T(1024)S(1)} %fusion.36), kind=kOutput, calls=%fused_computation.3 | convolution fusion | flops 1614019584 | bytes 3153920 | tf_op jit(solution)/shard_map/dot_general | solution.py:164
  61.3 0.0 copy-start.1
  61.3 0.0 copy-start.5
  61.3 0.6 fusion.3
  62.0 0.1 copy-done.5
  62.0 0.5 fusion.5
  62.6 0.0 copy-done.1
  62.6 0.7 copy-done.4
  63.3 0.6 fusion.23
  64.0 0.6 copy-done.3
  64.6 0.6 fusion.20
  65.3 2.4 %broadcast_in_dim.11 = bf16[8,2,16,48,128]{4,3,2,1,0:T(8,128)(2,1)} broadcast(bf16[2,16,48,128]{3,2,1,0:T(8,128)(2,1)S(1)} %pad_maximum_fusion), dimensions={1,2,3,4} | broadcast | bytes 3538944 | tf_op jit(solution)/shard_map/broadcast_in_dim | solution.py:198
  67.6 4.6 %all-to-all-start.2 = ((bf16[8,2,16,48,128]{4,3,2,1,0:T(8,128)(2,1)}), bf16[8,2,16,48,128]{4,3,2,1,0:T(8,128)(2,1)}, u32[]{:S(2)}, u32[]{:S(2)}) async-start(bf16[8,2,16,48,128]{4,3,2,1,0:T(8,128)(2,1)} %broadcast_in_dim.11), calls=%async_computation.2 | async-start | bytes 6291456 | tf_op jit(solution)/shard_map/all_to_all | solution.py:197
  72.9 0.6 pad_add_fusion.limits_ref
  73.5 8.5 %convolution_convert_fusion = bf16[1024,2304]{0,1:T(8,128)(2,1)} fusion(bf16[1024,768]{1,0:T(8,128)(2,1)} %copy-done.2, bf16[768,2304]{1,0:T(8,128)(2,1)} %param.12), kind=kOutput, calls=%fused_computation | convolution fusion | flops 3626237952 | bytes 9830400 | tf_op jit(solution)/shard_map/dot_general | solution.py:175
  82.0 28.4 %shard_map.73.prev_ref = bf16[2,384,1024]{2,1,0:T(8,128)(2,1)} custom-call(bf16[2304,1024]{1,0:T(8,128)(2,1)} %bitcast.38, bf16[2304,1024]{1,0:T(8,128)(2,1)} %bitcast.39, bf16[2304,1024]{1,0:T(8,128)(2,1)} %bitcast.40, bf16[2304,1024]{1,0:T(8,128)(2,1)} %bitcast.41, bf16[2304,1024]{1,0:T(8,128)(2,1)} %bitcast.42, bf16[2304,1024]{1,0:T(8,128)(2,1)} %bitcast.43, ...), custom_call_target="tpu_custom_call" | custom-call | tf_op jit(solution)/shard_map/pallas_call | solution.py:207
  110.4 0.0 all-to-all-done.2
  110.4 11.4 %shard_map.74 = bf16[2,384,1024]{2,1,0:T(8,128)(2,1)} custom-call(bf16[6,384,1024]{2,1,0:T(8,128)(2,1)} %bitcast.44, bf16[6,384,1024]{2,1,0:T(8,128)(2,1)} %bitcast.45, bf16[6,384,1024]{2,1,0:T(8,128)(2,1)} %bitcast.46, s32[2]{0:T(128)} %pad_add_fusion.limits_ref, ...), custom_call_target="tpu_custom_call", output_to_operand_aliasing={{}: (6, {})} | custom-call | tf_op jit(solution)/shard_map/pallas_call | solution.py:228
  121.8 3.7 %fusion.7 = bf16[1024,768]{1,0:T(8,128)(2,1)S(1)} fusion(bf16[1024,768]{1,0:T(8,128)(2,1)} %copy-done.1, bf16[768,1024]{1,0:T(8,128)(2,1)} %bitcast.47, bf16[768,768]{1,0:T(8,128)(2,1)} %param.13, pred[1024]{0:T(1024)(128)(4,1)S(1)} %fusion.34), kind=kOutput, calls=%fused_computation.12 | convolution fusion | flops 1211105280 | bytes 5899264 | tf_op jit(solution)/shard_map/dot_general | solution.py:248
  125.5 2.0 %copy.36 = bf16[128,8,768]{2,1,0:T(8,128)(2,1)} copy(bf16[128,8,768]{2,0,1:T(8,128)(2,1)S(1)} %bitcast.51) | data formatting | bytes 3145728 | tf_op jit(solution)/shard_map/transpose | solution.py:252
  (12 shorter events, 0.2 us)
Async XLA Ops:
  0.0 8.8 %copy-start = (bf16[1024,1536]{1,0:T(8,128)(2,1)S(1)}, bf16[1024,1536]{1,0:T(8,128)(2,1)}, u32[]{:S(2)}) copy-start(bf16[1024,1536]{1,0:T(8,128)(2,1)} %param.7) | copy-start | bytes 9437188
  1.5 14.5 %all-to-all-start = ((s32[32,1,32]{2,1,0:T(1,128)}), s32[32,1,32]{2,1,0:T(1,128)S(1)}, u32[]{:S(2)}, u32[]{:S(2)}) async-start(s32[32,1,32]{2,1,0:T(1,128)} %all_to_all.12), calls=%async_computation | async-start | bytes 32768 | tf_op jit(solution)/shard_map/all_to_all | solution.py:156
  16.0 41.9 %all-to-all-start.1 = ((bf16[32,32,768]{2,1,0:T(8,128)(2,1)}), bf16[32,32,768]{2,1,0:T(8,128)(2,1)}, u32[]{:S(2)}, u32[]{:S(2)}) async-start(bf16[32,32,768]{2,1,0:T(8,128)(2,1)} %bitcast.48), calls=%async_computation.1 | async-start | bytes 3145728 | tf_op jit(solution)/shard_map/all_to_all | solution.py:149
  61.3 1.3 copy-start.1
  61.3 0.7 copy-start.5
  62.0 1.3 copy-start.4
  62.6 1.4 %copy-start.2 = (bf16[1024,768]{1,0:T(8,128)(2,1)}, bf16[1024,768]{1,0:T(8,128)(2,1)S(1)}, u32[]{:S(2)}) copy-start(bf16[1024,768]{1,0:T(8,128)(2,1)S(1)} %fusion.5) | copy-start | bytes 4718596
  63.3 1.3 copy-start.3
  67.6 42.8 %all-to-all-start.2 = ((bf16[8,2,16,48,128]{4,3,2,1,0:T(8,128)(2,1)}), bf16[8,2,16,48,128]{4,3,2,1,0:T(8,128)(2,1)}, u32[]{:S(2)}, u32[]{:S(2)}) async-start(bf16[8,2,16,48,128]{4,3,2,1,0:T(8,128)(2,1)} %broadcast_in_dim.11), calls=%async_computation.2 | async-start | bytes 6291456 | tf_op jit(solution)/shard_map/all_to_all | solution.py:197

commit v20 on v16

--- a/solution.py
+++ b/solution.py
@@ -182,7 +182,7 @@
     )
     far_position = (
         jnp.arange(far_count, dtype=jnp.int32)[None, :] * DILATION_RATE
-        + jnp.asarray(offsets, jnp.int32)[:, None]
+        + jnp.asarray(offsets[:half], jnp.int32)[:, None]
     )
     far_bias = jnp.where(
         extra_row[None] & (far_position >= slide_length)[:, None, :], big_negative, 0.0

time: 128 us -> 128 us (level)
    unnamed x16 -> x14, local copies, waits for them, and re-layouts: 6.15 us -> 6.14 us
where the time goes in v20:
time: 128 us; the launch traced here: 127 us
  Pallas kernels  37.1 us (29%)
  waiting for transfers between devices  32.6 us (25%)
  matrix products  22.2 us (17%)
  starting transfers between devices  16.1 us (13%)
  local copies, waits for them, and re-layouts  15.4 us (12%)
  other arithmetic  2.85 us (2%)
    all_to_all x1, waiting for transfers between devices, body(): lax.all_to_all(projected.reshape(device_count, block_rows, width), ('tile...  29.6 us
    pallas_call x1, Pallas kernels, body(): pl.pallas_call(functools.partial(nearby_kernel, groups=DILATION_RATE, gro...  25.8 us
    pallas_call x1, Pallas kernels, body(): pl.pallas_call(functools.partial(dilated_kernel, factor=factor), grid=(ha...  11.3 us
    dot_general x1, matrix products, body(): lax.dot_general(qkv_weight, normed, (((0,), (1,)), ((), ())), preferred_e...  8.48 us
    all_to_all x1, starting transfers between devices, body(): lax.all_to_all(slot.reshape(device_count, block_rows), ('tile', 'seq'), s...  7.3 us
    unnamed x14, local copies, waits for them, and re-layouts  6.14 us
    dot_general x1, matrix products, body(): jnp.dot(embeddings, in_weight, preferred_element_type=jnp.float32)  5.34 us
    all_to_all x1, starting transfers between devices, body(): lax.all_to_all(jnp.broadcast_to(own_far[None], (seq_count,) + own_far.sha...  4.65 us
  transfers between devices with their start and end apart: 3, of which 3 were waited for; matrix products, arithmetic and copies ran while one was open for 19% of the time, Pallas kernels for 20%

profile of v20, /device:TPU:0, one launch (start us, length us, event | category | flops | bytes accessed | tf_op | source)
XLA Modules:
  0.0 127.0 jit_solution(4382768241443769597)
XLA Ops:
  0.0 0.0 copy-start
  0.0 1.5 %all_to_all.12 = s32[32,1,32]{2,1,0:T(1,128)} reshape(s32[1024]{0:T(1024)} %param.9) | data formatting | bytes 8192 | tf_op jit(solution)/shard_map/all_to_all | solution.py:132
  1.5 7.3 %all-to-all-start = ((s32[32,1,32]{2,1,0:T(1,128)}), s32[32,1,32]{2,1,0:T(1,128)S(1)}, u32[]{:S(2)}, u32[]{:S(2)}) async-start(s32[32,1,32]{2,1,0:T(1,128)} %all_to_all.12), calls=%async_computation | async-start | bytes 32768 | tf_op jit(solution)/shard_map/all_to_all | solution.py:132
  8.8 0.0 copy-done
  8.8 5.3 %convolution_convert_fusion.1 = bf16[1024,768]{1,0:T(8,128)(2,1)} fusion(bf16[1024,1536]{1,0:T(8,128)(2,1)S(1)} %copy-done, bf16[1536,768]{1,0:T(8,128)(2,1)} %param.11), kind=kOutput, calls=%fused_computation.15 | convolution fusion | flops 2416705536 | bytes 7077888 | tf_op jit(solution)/shard_map/dot_general | solution.py:122
  14.2 1.8 %all-to-all-done = s32[32,1,32]{2,1,0:T(1,128)S(1)} async-done(((s32[32,1,32]{2,1,0:T(1,128)}), s32[32,1,32]{2,1,0:T(1,128)S(1)}, u32[]{:S(2)}, u32[]{:S(2)}) %all-to-all-start) | async-done | bytes 4128 | tf_op jit(solution)/shard_map/all_to_all | solution.py:132
  16.0 4.2 %all-to-all-start.1 = ((bf16[32,32,768]{2,1,0:T(8,128)(2,1)}), bf16[32,32,768]{2,1,0:T(8,128)(2,1)}, u32[]{:S(2)}, u32[]{:S(2)}) async-start(bf16[32,32,768]{2,1,0:T(8,128)(2,1)} %bitcast.49), calls=%async_computation.1 | async-start | bytes 3145728 | tf_op jit(solution)/shard_map/all_to_all | solution.py:125
  20.1 3.2 %fusion.45 = (bf16[768,768]{1,0:T(8,128)(2,1)}, bf16[768,768]{1,0:T(8,128)(2,1)}) fusion(bf16[768,2304]{1,0:T(8,128)(2,1)} %param.13), kind=kLoop, calls=%fused_computation.63 | loop fusion | bytes 4718592 | tf_op jit(solution)/shard_map/slice | solution.py:166
  23.4 2.4 %copy.22 = bf16[768,768]{0,1:T(8,128)(2,1)} copy(bf16[768,768]{1,0:T(8,128)(2,1)} %get-tuple-element.5) | data formatting | bytes 2359296
  25.8 2.4 %copy.23 = bf16[768,768]{0,1:T(8,128)(2,1)} copy(bf16[768,768]{1,0:T(8,128)(2,1)} %get-tuple-element.6) | data formatting | bytes 2359296
  28.2 0.1 sub.34
  28.3 29.6 %all-to-all-done.1 = bf16[32,32,768]{2,1,0:T(8,128)(2,1)} async-done(((bf16[32,32,768]{2,1,0:T(8,128)(2,1)}), bf16[32,32,768]{2,1,0:T(8,128)(2,1)}, u32[]{:S(2)}, u32[]{:S(2)}) %all-to-all-start.1) | async-done | bytes 1572896 | tf_op jit(solution)/shard_map/all_to_all | solution.py:125
  57.9 3.4 %convert_reduce_fusion = (f32[1024]{0:T(1024)S(1)}, bf16[1024,768]{1,0:T(8,128)(2,1)S(1)}) fusion(bf16[1024,768]{1,0:T(8,128)(2,1)} %bitcast.2, s32[1024]{0:T(1024)S(1)} %fusion.37), kind=kOutput, calls=%fused_computation.3 | convolution fusion | flops 1614019584 | bytes 3153920 | tf_op jit(solution)/shard_map/dot_general | solution.py:140
  61.3 0.0 copy-start.1
  61.3 0.0 copy-start.5
  61.3 0.6 fusion.3
  62.0 0.1 copy-done.5
  62.0 0.5 fusion.5
  62.6 0.7 copy-done.4
  63.3 0.6 fusion.23
  64.0 0.6 copy-done.3
  64.6 0.6 fusion.20
  65.3 2.4 %broadcast_in_dim.48 = bf16[8,2,16,48,128]{4,3,2,1,0:T(8,128)(2,1)} broadcast(bf16[2,16,48,128]{3,2,1,0:T(8,128)(2,1)S(1)} %pad_maximum_fusion), dimensions={1,2,3,4} | broadcast | bytes 3538944 | tf_op jit(solution)/shard_map/broadcast_in_dim | solution.py:177
  67.6 4.6 %all-to-all-start.2 = ((bf16[8,2,16,48,128]{4,3,2,1,0:T(8,128)(2,1)}), bf16[8,2,16,48,128]{4,3,2,1,0:T(8,128)(2,1)}, u32[]{:S(2)}, u32[]{:S(2)}) async-start(bf16[8,2,16,48,128]{4,3,2,1,0:T(8,128)(2,1)} %broadcast_in_dim.48), calls=%async_computation.2 | async-start | bytes 6291456 | tf_op jit(solution)/shard_map/all_to_all | solution.py:176
  73.0 0.7 select_convert_fusion.1.bias_ref
  73.7 0.9 select_convert_fusion.fbias_ref
  74.5 8.5 %convolution_convert_fusion = bf16[1024,2304]{0,1:T(8,128)(2,1)} fusion(bf16[1024,768]{1,0:T(8,128)(2,1)} %copy-done.2, bf16[768,2304]{1,0:T(8,128)(2,1)} %param.13), kind=kOutput, calls=%fused_computation | convolution fusion | flops 3626237952 | bytes 9830400 | tf_op jit(solution)/shard_map/dot_general | solution.py:154
  83.0 25.8 %shard_map.82.prev_ref = bf16[2,384,1024]{2,1,0:T(8,128)(2,1)} custom-call(bf16[2304,1024]{1,0:T(8,128)(2,1)} %bitcast.39, bf16[2304,1024]{1,0:T(8,128)(2,1)} %bitcast.40, bf16[2304,1024]{1,0:T(8,128)(2,1)} %bitcast.41, bf16[2304,1024]{1,0:T(8,128)(2,1)} %bitcast.42, bf16[2304,1024]{1,0:T(8,128)(2,1)} %bitcast.43, bf16[2304,1024]{1,0:T(8,128)(2,1)} %bitcast.44, ...), custom_call_target="tpu_custom_call" | custom-call | tf_op jit(solution)/shard_map/pallas_call | solution.py:197
  108.8 1.2 all-to-all-done.2
  110.0 11.3 %shard_map.83 = bf16[2,384,1024]{2,1,0:T(8,128)(2,1)} custom-call(bf16[6,384,1024]{2,1,0:T(8,128)(2,1)} %bitcast.45, bf16[6,384,1024]{2,1,0:T(8,128)(2,1)} %bitcast.46, bf16[6,384,1024]{2,1,0:T(8,128)(2,1)} %bitcast.47, bf16[16,1024]{1,0:T(8,128)(2,1)} %select_convert_fusion.1.bias_ref, ...), custom_call_target="tpu_custom_call", output_to_operand_aliasing={{}: (7, {})} | custom-call | tf_op jit(solution)/shard_map/pallas_call | solution.py:218
  121.3 3.7 %fusion.7 = bf16[1024,768]{1,0:T(8,128)(2,1)S(1)} fusion(bf16[1024,768]{1,0:T(8,128)(2,1)} %copy-done.1, bf16[768,1024]{1,0:T(8,128)(2,1)} %bitcast.48, bf16[768,768]{1,0:T(8,128)(2,1)} %param.14, pred[1024]{0:T(1024)(128)(4,1)S(1)} %fusion.35), kind=kOutput, calls=%fused_computation.12 | convolution fusion | flops 1211105280 | bytes 5899264 | tf_op jit(solution)/shard_map/dot_general | solution.py:239
  125.0 2.0 %copy.37 = bf16[128,8,768]{2,1,0:T(8,128)(2,1)} copy(bf16[128,8,768]{2,0,1:T(8,128)(2,1)S(1)} %bitcast.52) | data formatting | bytes 3145728 | tf_op jit(solution)/shard_map/transpose | solution.py:243
  (17 shorter events, 0.2 us)
Async XLA Ops:
  0.0 8.8 %copy-start = (bf16[1024,1536]{1,0:T(8,128)(2,1)S(1)}, bf16[1024,1536]{1,0:T(8,128)(2,1)}, u32[]{:S(2)}) copy-start(bf16[1024,1536]{1,0:T(8,128)(2,1)} %param.8) | copy-start | bytes 9437188
  1.5 14.5 %all-to-all-start = ((s32[32,1,32]{2,1,0:T(1,128)}), s32[32,1,32]{2,1,0:T(1,128)S(1)}, u32[]{:S(2)}, u32[]{:S(2)}) async-start(s32[32,1,32]{2,1,0:T(1,128)} %all_to_all.12), calls=%async_computation | async-start | bytes 32768 | tf_op jit(solution)/shard_map/all_to_all | solution.py:132
  16.0 41.9 %all-to-all-start.1 = ((bf16[32,32,768]{2,1,0:T(8,128)(2,1)}), bf16[32,32,768]{2,1,0:T(8,128)(2,1)}, u32[]{:S(2)}, u32[]{:S(2)}) async-start(bf16[32,32,768]{2,1,0:T(8,128)(2,1)} %bitcast.49), calls=%async_computation.1 | async-start | bytes 3145728 | tf_op jit(solution)/shard_map/all_to_all | solution.py:125
  61.3 1.3 copy-start.1
  61.3 0.7 copy-start.5
  62.0 1.3 %copy-start.4 = (bf16[768,768]{0,1:T(8,128)(2,1)S(1)}, bf16[768,768]{0,1:T(8,128)(2,1)}, u32[]{:S(2)}) copy-start(bf16[768,768]{0,1:T(8,128)(2,1)} %copy.22) | copy-start | bytes 3538948
  62.6 1.4 %copy-start.2 = (bf16[1024,768]{1,0:T(8,128)(2,1)}, bf16[1024,768]{1,0:T(8,128)(2,1)S(1)}, u32[]{:S(2)}) copy-start(bf16[1024,768]{1,0:T(8,128)(2,1)S(1)} %fusion.5) | copy-start | bytes 4718596
  63.3 1.3 %copy-start.3 = (bf16[768,768]{0,1:T(8,128)(2,1)S(1)}, bf16[768,768]{0,1:T(8,128)(2,1)}, u32[]{:S(2)}) copy-start(bf16[768,768]{0,1:T(8,128)(2,1)} %copy.23) | copy-start | bytes 3538948
  67.6 42.4 %all-to-all-start.2 = ((bf16[8,2,16,48,128]{4,3,2,1,0:T(8,128)(2,1)}), bf16[8,2,16,48,128]{4,3,2,1,0:T(8,128)(2,1)}, u32[]{:S(2)}, u32[]{:S(2)}) async-start(bf16[8,2,16,48,128]{4,3,2,1,0:T(8,128)(2,1)} %broadcast_in_dim.48), calls=%async_computation.2 | async-start | bytes 6291456 | tf_op jit(solution)/shard_map/all_to_all | solution.py:176
